TPU v7x, 128 devices: a whole 4x4x4 slice. The times are simulated.
128 devices in a mesh: req: 4 (over z), blk: 32 (over y, x, core).
Axes of the slice: x: 4, y: 4, z: 4, core: 2. Of those that a mesh axis runs over, the one named last changes fastest.
Arguments:
- queries: bfloat16 [4, 2048, 2048], P('req', 'blk'), may hold values from -6 to 6
- span_keys: bfloat16 [4, 2048, 512], P('req', 'blk'), may hold values from -6 to 6
- span_values: bfloat16 [4, 2048, 512], P('req', 'blk'), may hold values from -6 to 6
- cache_keys: bfloat16 [4, 4096, 512], P('req', 'blk'), may hold values from -6 to 6
- cache_values: bfloat16 [4, 4096, 512], P('req', 'blk'), may hold values from -6 to 6
- lengths: int32 [4], P('req'), may hold values from 1 to 4096, 10240 in all
- inputs: bfloat16 [4, 2048, 2048], P('req', 'blk'), may hold values from -0.59765625 to 0.59765625
- w_out: bfloat16 [2048, 2048], replicated, may hold values from -0.125 to 0.125
- norm_gain: float32 [2048], replicated, may hold values from 0.1 to 1.9
- route_ids: int32 [4, 2048, 6], P('req', 'blk'), may hold values from 0 to 63, all different within a row; in each aligned block of 64 rows (0 to 63, 64 to 127, ..., all dimensions but the last counted through in order) at most 12 rows name the same one
- route_weights: float32 [4, 2048, 6], P('req', 'blk'), may hold values from 0.2 to 1
- w_gate_up: bfloat16 [128, 1408, 2048], P(('req', 'blk')), may hold values from -0.125 to 0.125
- w_down: bfloat16 [128, 704, 2048], P(('req', 'blk')), may hold values from -0.15625 to 0.15625
Outputs:
- outputs: bfloat16 [4, 2048, 2048], P('req', 'blk')
Inputs may be any that keep to these rules, and one draw needn't show every extreme that they name: `lengths`: the longest cache is exactly 4096. `route_ids`: A token names 6 different experts; within the rows of one device (aligned blocks of 64 tokens) no expert is named more than 12 times, a bound that some block reaches.
All inputs are finite; a program needn't handle non-finite values. No bound on the sum of `lengths` on one device may be relied on, other than what follows from the above.
Results may differ from a plain program's by a relative error of at most 0.019.
Values may be sent and summed in bfloat16 or wider, within the bound.
No kernel may reach another device: no remote copies, remote signals or barrier semaphores. Data moves between devices by JAX's collectives and lax.ppermute only.
A program may use at most 256 MiB of HBM per device.

v0:
```python
import math

import jax
import jax.numpy as jnp
from jax import lax
from jax.sharding import PartitionSpec as P

D = 2048
HEADS = 16
KV_HEADS = 4
HEAD_DIM = 128
EXPERTS = 64
TOP = 6


def softmax_piece(query_rows, key_rows, value_rows, visible, state):
    weighted, row_peak, row_total = state
    key_count = key_rows.shape[0]
    scores = jnp.einsum(
        "qgrd,kgd->qgrk",
        query_rows,
        key_rows.reshape(key_count, KV_HEADS, HEAD_DIM),
        preferred_element_type=jnp.float32,
    ) / math.sqrt(HEAD_DIM)
    wide_mask = visible[:, None, None, :]
    masked = jnp.where(wide_mask, scores, -1e30)
    new_peak = jnp.maximum(row_peak, jnp.max(masked, axis=-1))
    probs_now = jnp.where(wide_mask, jnp.exp(masked - new_peak[..., None]), 0.0)
    row_total = jnp.sum(probs_now, axis=-1)
    weighted = jnp.einsum(
        "qgrk,kgd->qgrd",
        probs_now.astype(jnp.bfloat16),
        value_rows.reshape(key_count, KV_HEADS, HEAD_DIM),
        preferred_element_type=jnp.float32,
    )
    return (weighted, new_peak, row_total)


def fresh_state(row_count, group_size):
    return (
        jnp.zeros((row_count, KV_HEADS, group_size, HEAD_DIM), jnp.float32),
        jnp.full((row_count, KV_HEADS, group_size), -1e30, jnp.float32),
        jnp.zeros((row_count, KV_HEADS, group_size), jnp.float32),
    )


def run_experts(arrived, gate_up, down_rows):
    half_width = down_rows.shape[1]
    hidden = jnp.einsum("shnd,hfd->shnf", arrived, gate_up, preferred_element_type=jnp.float32)
    activated = (jax.nn.silu(hidden[..., :half_width]) * hidden[..., half_width:]).astype(
        jnp.bfloat16
    )
    return jnp.einsum(
        "shnf,hfd->shnd", activated, down_rows, preferred_element_type=jnp.float32
    ).astype(jnp.bfloat16)


def local(
    queries,
    span_keys,
    span_values,
    cache_keys,
    cache_values,
    lengths,
    inputs,
    w_out,
    norm_gain,
    route_ids,
    route_weights,
    w_gate_up,
    w_down,
):
    tok_rows = queries.shape[1]
    group_size = HEADS // KV_HEADS
    blk_count = lax.axis_size("blk")
    blk_index = lax.axis_index("blk")
    length = lengths[0]
    row_index = blk_index * tok_rows + jnp.arange(tok_rows, dtype=jnp.int32)
    everyone = lax.all_gather(queries, "blk", axis=1, tiled=True)[0]
    all_rows = everyone.shape[0]
    block_size = min(512, all_rows)
    cache_len = cache_keys.shape[1]
    cache_seen = blk_index * cache_len + jnp.arange(cache_len, dtype=jnp.int32) < length
    key_rows = jnp.concatenate([cache_keys[0], span_keys[0]], 0)
    value_rows = jnp.concatenate([cache_values[0], span_values[0]], 0)

    def one_block(first_row):
        query_rows = lax.dynamic_slice_in_dim(everyone, first_row, block_size, 0).reshape(
            block_size, KV_HEADS, group_size, HEAD_DIM
        )
        block_index = first_row + jnp.arange(block_size, dtype=jnp.int32)
        visible = jnp.concatenate(
            [
                jnp.broadcast_to(cache_seen[None, :], (block_size, cache_len)),
                row_index[None, :] <= block_index[:, None],
            ],
            1,
        )
        weighted, row_peak, row_total = softmax_piece(
            query_rows, key_rows, value_rows, visible, fresh_state(block_size, group_size)
        )
        return (
            weighted.reshape(block_size, HEADS * HEAD_DIM),
            row_peak.reshape(block_size, HEADS),
            row_total.reshape(block_size, HEADS),
        )

    starts = jnp.arange(all_rows // block_size, dtype=jnp.int32) * block_size
    weighted, row_peak, row_total = lax.map(one_block, starts)
    weighted = weighted.reshape(blk_count, tok_rows, HEADS * HEAD_DIM)
    row_peak = row_peak.reshape(blk_count, tok_rows, HEADS)
    row_total = row_total.reshape(blk_count, tok_rows, HEADS)
    weighted, row_peak, row_total = (
        lax.all_to_all(weighted, "blk", split_axis=0, concat_axis=0, tiled=True),
        lax.all_to_all(row_peak, "blk", split_axis=0, concat_axis=0, tiled=True),
        lax.all_to_all(row_total, "blk", split_axis=0, concat_axis=0, tiled=True),
    )
    merged_peak = jnp.max(row_peak, axis=0)
    weight = jnp.exp(row_peak - merged_peak)
    denominator = jnp.sum(weight * row_total, axis=0)
    numerator = jnp.sum(
        weight[..., None] * weighted.reshape(blk_count, tok_rows, HEADS, HEAD_DIM), axis=0
    )
    attended = (
        (numerator / denominator[..., None])
        .reshape(tok_rows, HEADS * HEAD_DIM)
        .astype(jnp.bfloat16)
    )
    residual = inputs[0].astype(jnp.float32) + jnp.dot(
        attended, w_out, preferred_element_type=jnp.float32
    )
    normalized = (
        residual
        * lax.rsqrt(jnp.mean(residual * residual, axis=-1, keepdims=True) + 1e-06)
        * norm_gain
    ).astype(jnp.bfloat16)
    devices = lax.axis_size("req") * blk_count
    per_device = 2 * EXPERTS // devices
    capacity = max(2, tok_rows * TOP * 2 // EXPERTS)
    flat_ids = route_ids[0].reshape(-1)
    onehot = (flat_ids[:, None] == jnp.arange(EXPERTS, dtype=jnp.int32)[None, :]).astype(jnp.int32)
    slot_index = jnp.sum((jnp.cumsum(onehot, axis=0) - onehot) * onehot, axis=1)
    slot_target = flat_ids * capacity + slot_index
    slot_match = slot_target[:, None] == jnp.arange(EXPERTS * capacity, dtype=jnp.int32)[None, :]
    dispatch = jnp.sum(slot_match.reshape(tok_rows, TOP, -1).astype(jnp.float32), axis=1).astype(
        jnp.bfloat16
    )
    combine_weights = jnp.sum(
        jnp.where(slot_match, route_weights[0].reshape(-1)[:, None], 0.0).reshape(
            tok_rows, TOP, -1
        ),
        axis=1,
    )
    outgoing = lax.dot_general(
        dispatch, normalized, (((0,), (0,)), ((), ())), preferred_element_type=jnp.float32
    ).astype(jnp.bfloat16)
    doubled = jnp.broadcast_to(
        outgoing.reshape(EXPERTS, 1, capacity, D), (EXPERTS, 2, capacity, D)
    ).reshape(devices, per_device, capacity, D)
    returned = lax.all_to_all(
        run_experts(
            lax.all_to_all(doubled, ("req", "blk"), split_axis=0, concat_axis=0, tiled=True),
            w_gate_up,
            w_down,
        ),
        ("req", "blk"),
        split_axis=0,
        concat_axis=0,
        tiled=True,
    )
    halves = returned.reshape(EXPERTS, 2, capacity, D).astype(jnp.float32)
    summed = (halves[:, 0] + halves[:, 1]).reshape(EXPERTS * capacity, D)
    expert_sum = jnp.dot(
        combine_weights, summed, precision=lax.Precision.HIGHEST, preferred_element_type=jnp.float32
    )
    return (residual + expert_sum).astype(jnp.bfloat16)[None]


def solution(mesh):
    in_specs = (
        P("req", "blk", None),
        P("req", "blk", None),
        P("req", "blk", None),
        P("req", "blk", None),
        P("req", "blk", None),
        P("req"),
        P("req", "blk", None),
        P(),
        P(),
        P("req", "blk", None),
        P("req", "blk", None),
        P(("req", "blk"), None, None),
        P(("req", "blk"), None, None),
    )
    out_specs = P("req", "blk", None)
    return jax.shard_map(local, mesh=mesh, in_specs=in_specs, out_specs=out_specs, check_vma=False)
```

profile of v0, /device:TPU:1, one launch (start us, length us, event | category | flops | bytes accessed | tf_op | source)
XLA Modules:
  0.0 757.6 jit_solution(5051596786279227721)
XLA Ops:
  7.3 1.8 pad_maximum_fusion
  9.2 1.7 reshape.171
  10.9 55.0 %all-gather.2.cloned.1.call-done = bf16[1,2048,2048]{2,1,0:T(8,128)(2,1)} async-done(((bf16[1,64,2048]{2,1,0:T(8,128)(2,1)}), bf16[1,2048,2048]{2,1,0:T(8,128)(2,1)}) %all-gather.2.cloned.1.call-update) | async-done | bytes 8388624 | tf_op jit(solution)/shard_map/all_gather | solution.py:79
  65.9 133.3 %while.16 = (s32[]{:T(128)}, f32[4,512,2048]{2,1,0:T(8,128)}, f32[4,512,16]{1,0,2:T(4,128)}, f32[4,512,16]{1,0,2:T(4,128)}, s32[4]{0:T(128)S(1)}, /*index=5*/bf1...) while((s32[]{:T(128)}, f32[4,512,2048]{2,1,0:T(8,128)}, ...), condition=%wide.wide.region_3.4_spmd.clone, body=%wide.wide.region_0.3_spmd.clone.sunk | while | flops 825877312 | bytes 52434320 | solution.py:109
  69.9 3.6 constant_dynamic-slice_fusion.3
  73.5 3.9 copy.140
  77.4 2.9 bitcast_reduce_fusion.4
  80.3 1.6 fusion.67
  81.9 3.8 fusion.66
  85.7 5.4 copy.141
  91.2 1.7 dynamic_update_slice.23
  92.9 1.7 dynamic_update_slice.22
  94.6 4.6 constant_dynamic-update-slice_fusion.3
  103.2 3.6 constant_dynamic-slice_fusion.3
  106.8 3.9 copy.140
  110.7 2.9 bitcast_reduce_fusion.4
  113.6 1.6 fusion.67
  115.2 3.8 fusion.66
  119.0 5.4 copy.141
  124.5 1.7 dynamic_update_slice.23
  126.2 1.7 dynamic_update_slice.22
  127.9 4.7 constant_dynamic-update-slice_fusion.3
  136.5 3.6 constant_dynamic-slice_fusion.3
  140.1 3.9 copy.140
  144.0 2.8 bitcast_reduce_fusion.4
  146.9 1.6 fusion.67
  148.5 3.8 fusion.66
  152.3 5.4 copy.141
  157.8 1.7 dynamic_update_slice.23
  159.5 1.7 dynamic_update_slice.22
  161.2 4.7 constant_dynamic-update-slice_fusion.3
  169.8 3.6 constant_dynamic-slice_fusion.3
  173.4 3.9 copy.140
  177.3 2.9 bitcast_reduce_fusion.4
  180.2 1.6 fusion.67
  181.8 3.8 fusion.66
  185.7 5.4 copy.141
  191.1 1.7 dynamic_update_slice.23
  192.8 1.7 dynamic_update_slice.22
  194.5 4.6 constant_dynamic-update-slice_fusion.3
  201.2 5.5 all-to-all-start.2
  206.7 1.0 reshape.146
  208.1 6.2 all-to-all-done.2
  214.3 11.2 %all_to_all.25 = f32[32,1,1024]{2,1,0:T(1,128)S(1)} all-to-all(f32[32,1,1024]{2,1,0:T(1,128)S(1)} %reshape.166), channel_id=1, replica_groups=mesh['req'=4,'blk'=32] {'blk'}, dimensions={0} | all-to-all | bytes 262144 | tf_op jit(solution)/shard_map/all_to_all | solution.py:115
  225.5 5.3 all-to-all-start.1
  232.8 1.0 convert_reduce_fusion
  238.4 1.3 copy.65
  239.8 9.6 %mul.68 = f32[32,64,16,128]{3,2,1,0:T(8,128)} broadcast(f32[32,64,16]{2,1,0:T(8,128)} %copy.65), dimensions={0,1,2} | broadcast | bytes 16908288 | tf_op jit(solution)/shard_map/mul | solution.py:122
  249.4 18.0 %mul.69 = f32[32,64,2048]{2,1,0:T(8,128)} reshape(f32[32,64,16,128]{3,2,1,0:T(8,128)} %mul.68) | data formatting | bytes 33554432 | tf_op jit(solution)/shard_map/mul | solution.py:122
  267.4 165.0 %all-to-all-done.1 = f32[32,64,2048]{2,1,0:T(8,128)} async-done(((f32[32,64,2048]{2,1,0:T(8,128)}), f32[32,64,2048]{2,1,0:T(8,128)}, u32[]{:S(2)}, u32[]{:S(2)}) %all-to-all-start.1) | async-done | bytes 16777248 | tf_op jit(solution)/shard_map/all_to_all | solution.py:114
  432.4 11.4 %multiply_reduce_fusion = f32[64,2048]{1,0:T(8,128)S(1)} fusion(f32[32,64,2048]{2,1,0:T(8,128)} %mul.69, f32[32,64,2048]{2,1,0:T(8,128)} %all-to-all-done.1), kind=kLoop, calls=%fused_computation.30 | loop fusion | flops 8257536 | bytes 34078720 | tf_op jit(solution)/shard_map/reduce_sum | solution.py:121
  444.0 5.2 multiply_reduce_fusion.1
  449.3 2.7 convolution_convert_fusion
  452.0 6.1 broadcast_in_dim.95
  458.0 6.9 broadcast_in_dim.96
  464.9 114.5 %all_to_all.26 = bf16[128,1,12,2048]{3,2,1,0:T(8,128)(2,1)S(1)} all-to-all(bf16[128,1,12,2048]{3,2,1,0:T(8,128)(2,1)} %bitcast.165), channel_id=1, replica_groups=mesh['req'=4,'blk'=32] {'req','blk'}, dimensions={0} | all-to-all | bytes 12582912 | tf_op jit(solution)/shard_map/all_to_all | solution.py:162
  579.4 12.8 %fusion.27 = f32[128,1,12,1408]{3,0,2,1:T(8,128)} fusion(bf16[1,1408,2048]{2,1,0:T(8,128)(2,1)S(1)} %bitcast.180, bf16[128,1,12,2048]{3,2,1,0:T(8,128)(2,1)S(1)} %all_to_all.26), kind=kOutput, calls=%fused_computation.40 | convolution fusion | flops 8858370048 | bytes 20709376 | tf_op jit(solution)/shard_map/shnd,hfd->shnf/dot_general | solution.py:49
  592.2 9.6 %convert_bitcast_fusion = bf16[128,1,12,2048]{3,0,2,1:T(8,128)(2,1)S(1)} fusion(bf16[1,704,2048]{2,1,0:T(8,128)(2,1)S(1)} %copy-done, f32[128,1,12,1408]{3,0,2,1:T(8,128)} %fusion.27), kind=kOutput, calls=%fused_computation.38 | convolution fusion | flops 4438818816 | bytes 18612224 | tf_op jit(solution)/shard_map/shnf,hfd->shnd/dot_general | solution.py:53
  601.8 6.9 copy.78
  608.7 103.5 %all_to_all.27 = bf16[128,1,12,2048]{3,2,1,0:T(8,128)(2,1)} all-to-all(bf16[128,1,12,2048]{3,2,1,0:T(8,128)(2,1)} %copy.78), channel_id=1, replica_groups=mesh['req'=4,'blk'=32] {'req','blk'}, dimensions={0} | all-to-all | bytes 12582912 | tf_op jit(solution)/shard_map/all_to_all | solution.py:160
  712.2 11.2 %bitcast_convert_fusion = f32[64,2,12,2048]{3,2,1,0:T(8,128)} fusion(bf16[64,2,12,2048]{3,2,1,0:T(8,128)(2,1)} %bitcast.164), kind=kLoop, calls=%fused_computation.34 | loop fusion | flops 3145728 | bytes 18874368 | tf_op jit(solution)/shard_map/convert_element_type | solution.py:171
  723.4 11.7 %fusion.22 = f32[64,1,12,2048]{3,2,0,1:T(8,128)} fusion(f32[64,2,12,2048]{3,2,1,0:T(8,128)} %bitcast_convert_fusion), kind=kLoop, calls=%fused_computation.32 | loop fusion | flops 1572864 | bytes 18874368 | tf_op jit(solution)/shard_map/add | solution.py:172
  735.1 8.2 %add.73 = f32[768,2048]{1,0:T(8,128)} reshape(f32[64,1,12,2048]{3,2,0,1:T(8,128)} %fusion.22) | data formatting | bytes 12582912 | tf_op jit(solution)/shard_map/add | solution.py:172
  743.3 7.5 fusion.37
  (101 shorter events, 18.6 us)
Async XLA Ops:
  6.5 585.7 %copy-start = (bf16[1,704,2048]{2,1,0:T(8,128)(2,1)S(1)}, bf16[1,704,2048]{2,1,0:T(8,128)(2,1)}, u32[]{:S(2)}) copy-start(bf16[1,704,2048]{2,1,0:T(8,128)(2,1)} %param.27) | copy-start | bytes 8650756
  6.5 59.3 %all-gather.2.cloned.1.call-start = ((), (), s32[]{:S(2)}) async-start(), calls=%async_computation.5 | async-start | bytes 8650752 | tf_op jit(solution)/shard_map/all_gather | solution.py:79
  9.1 56.7 %copy-start.1 = (bf16[192,512]{1,0:T(8,128)(2,1)}, bf16[192,512]{1,0:T(8,128)(2,1)S(1)}, u32[]{:S(2)}) copy-start(bf16[192,512]{1,0:T(8,128)(2,1)S(1)} %get-tuple-element.278) | copy-start | bytes 589828
  80.3 1.6 copy-start.4
  113.5 1.6 copy-start.4
  146.9 1.6 copy-start.4
  180.2 1.6 copy-start.4
  201.2 13.1 %all-to-all-start.2 = ((f32[32,1,1024]{2,1,0:T(1,128)}), f32[32,1,1024]{2,1,0:T(1,128)S(1)}, u32[]{:S(2)}, u32[]{:S(2)}) async-start(f32[32,1,1024]{2,1,0:T(1,128)} %reshape.168), calls=%async_computation.2 | async-start | bytes 262144 | tf_op jit(solution)/shard_map/all_to_all | solution.py:116
  225.5 5.3 copy-start.6
  225.5 5.7 copy-start.7
  225.5 206.9 %all-to-all-start.1 = ((f32[32,64,2048]{2,1,0:T(8,128)}), f32[32,64,2048]{2,1,0:T(8,128)}, u32[]{:S(2)}, u32[]{:S(2)}) async-start(f32[32,64,2048]{2,1,0:T(8,128)} %bitcast.166), calls=%async_computation.1 | async-start | bytes 33554432 | tf_op jit(solution)/shard_map/all_to_all | solution.py:114
  432.4 11.6 %copy-start.3 = (bf16[1,64,2048]{2,1,0:T(8,128)(2,1)S(1)}, bf16[1,64,2048]{2,1,0:T(8,128)(2,1)}, u32[]{:S(2)}) copy-start(bf16[1,64,2048]{2,1,0:T(8,128)(2,1)} %param.21) | copy-start | bytes 786436
  444.0 5.2 copy-start.2
  444.0 5.2 copy-start.5
  458.0 121.4 %slice-start = ((s8[5767168]{0:T(1024)(128)(4,1)}), s8[1572864]{0:T(1024)(128)(4,1)S(1)}, s32[]{:S(2)}) async-start(s8[5767168]{0:T(1024)(128)(4,1)} %bitcast.179), calls=%async_computation.6 | async-start | bytes 3145728
  464.9 114.5 %slice-start.1 = ((s8[5767168]{0:T(1024)(128)(4,1)}), s8[4194304]{0:T(1024)(128)(4,1)S(1)}, s32[]{:S(2)}) async-start(s8[5767168]{0:T(1024)(128)(4,1)} %bitcast.179), calls=%async_computation.7 | async-start | bytes 8388608
Sparse Core Ops, SparseCore 0:
  9.6 56.2 all-gather.1
where the time goes:
time: 760 us; the launch traced here: 758 us
  blocking collectives  229 us (30%)
  waiting for transfers between devices  227 us (30%)
  local copies, waits for them, and re-layouts  151 us (20%)
  matrix products  64.3 us (8%)
  other arithmetic  53.6 us (7%)
  between operations  13.6 us (2%)
  starting transfers between devices  10.8 us (1%)
  loops' own time  7.86 us (1%)
    all_to_all x1, waiting for transfers between devices, local(): lax.all_to_all(weighted, 'blk', split_axis=0, concat_axis=0, tiled=True)  165 us
    all_to_all x1, blocking collectives, local(): lax.all_to_all(doubled, ('req', 'blk'), split_axis=0, concat_axis=0, tile...  114 us
    all_to_all x1, blocking collectives, local(): lax.all_to_all(run_experts(lax.all_to_all(doubled, ('req', 'blk'), split_...  103 us
    all_gather x1, waiting for transfers between devices, local(): everyone = lax.all_gather(queries, 'blk', axis=1, tiled=True)[0]  55 us
    dynamic_update_slice x16, local copies, waits for them, and re-layouts, local(): weighted, row_peak, row_total = lax.map(one_block, starts)  53.8 us
    dynamic_slice x8, local copies, waits for them, and re-layouts, one_block(): lax.dynamic_slice_in_dim(everyone, first_row, block_size, 0)  30.1 us
    mul x2, local copies, waits for them, and re-layouts, local(): weight[..., None] * weighted.reshape(blk_count, tok_rows, HEADS, HEAD_DIM)  27.6 us
  transfers between devices with their start and end apart: 3, of which 3 were waited for; matrix products, arithmetic and copies ran while one was open for 5% of the time, Pallas kernels for 0%

commit v1 on v0

v1 whole, which is shorter than its diff:
```python
import math

import jax
import jax.numpy as jnp
from jax import lax
from jax.sharding import PartitionSpec as P

D = 2048
HEADS = 16
KV_HEADS = 4
HEAD_DIM = 128
EXPERTS = 64
TOP = 6


def attend(queries, kv_rows, length, blk_index, cache_len, span_len):
    tok_rows = queries.shape[0]
    group_size = HEADS // KV_HEADS
    per_dev = cache_len + span_len
    key_count = kv_rows.shape[0]
    key_rows = kv_rows[:, : KV_HEADS * HEAD_DIM].reshape(key_count, KV_HEADS, HEAD_DIM)
    value_rows = kv_rows[:, KV_HEADS * HEAD_DIM :].reshape(key_count, KV_HEADS, HEAD_DIM)
    key_index = jnp.arange(key_count, dtype=jnp.int32)
    owner = key_index // per_dev
    offset = key_index % per_dev
    in_cache = (offset < cache_len) & (owner * cache_len + offset < length)
    span_pos = owner * span_len + offset - cache_len
    row_index = blk_index * tok_rows + jnp.arange(tok_rows, dtype=jnp.int32)
    in_span = (offset >= cache_len)[None, :] & (span_pos[None, :] <= row_index[:, None])
    visible = (in_cache[None, :] | in_span)[:, None, None, :]
    query_rows = queries.reshape(tok_rows, KV_HEADS, group_size, HEAD_DIM)
    scores = jnp.einsum(
        "qgrd,kgd->qgrk", query_rows, key_rows, preferred_element_type=jnp.float32
    ) / math.sqrt(HEAD_DIM)
    masked = jnp.where(visible, scores, -1e30)
    row_peak = jnp.max(masked, axis=-1, keepdims=True)
    probs = jnp.where(visible, jnp.exp(masked - row_peak), 0.0)
    row_total = jnp.sum(probs, axis=-1)
    weighted = jnp.einsum(
        "qgrk,kgd->qgrd",
        probs.astype(jnp.bfloat16),
        value_rows,
        preferred_element_type=jnp.float32,
    )
    return (weighted / row_total[..., None]).reshape(tok_rows, HEADS * HEAD_DIM).astype(jnp.bfloat16)


def half_expert(arrived, gate_up, down_rows):
    half_width = down_rows.shape[0]
    hidden = jnp.dot(arrived, gate_up.T, preferred_element_type=jnp.float32)
    activated = (jax.nn.silu(hidden[:, :half_width]) * hidden[:, half_width:]).astype(jnp.bfloat16)
    return jnp.dot(activated, down_rows, preferred_element_type=jnp.float32).astype(jnp.bfloat16)


def local(
    queries,
    span_keys,
    span_values,
    cache_keys,
    cache_values,
    lengths,
    inputs,
    w_out,
    norm_gain,
    route_ids,
    route_weights,
    w_gate_up,
    w_down,
):
    tok_rows = queries.shape[1]
    blk_count = lax.axis_size("blk")
    blk_index = lax.axis_index("blk")
    length = lengths[0]
    cache_len = cache_keys.shape[1]
    span_len = span_keys.shape[1]

    pairs = [(b, b ^ 1) for b in range(blk_count)]
    other_gate_up = lax.ppermute(w_gate_up[0], "blk", pairs)
    other_down = lax.ppermute(w_down[0], "blk", pairs)

    local_kv = jnp.concatenate(
        [
            jnp.concatenate([cache_keys[0], span_keys[0]], 0),
            jnp.concatenate([cache_values[0], span_values[0]], 0),
        ],
        1,
    )
    kv_rows = lax.all_gather(local_kv, "blk", axis=0, tiled=True)
    attended = attend(queries[0], kv_rows, length, blk_index, cache_len, span_len)

    residual = inputs[0].astype(jnp.float32) + jnp.dot(
        attended, w_out, preferred_element_type=jnp.float32
    )
    normalized = (
        residual
        * lax.rsqrt(jnp.mean(residual * residual, axis=-1, keepdims=True) + 1e-06)
        * norm_gain
    ).astype(jnp.bfloat16)

    devices = lax.axis_size("req") * blk_count
    capacity = max(2, tok_rows * TOP * 2 // EXPERTS)
    half_cap = (capacity + 1) // 2
    flat_ids = route_ids[0].reshape(-1)
    onehot = (flat_ids[:, None] == jnp.arange(EXPERTS, dtype=jnp.int32)[None, :]).astype(jnp.int32)
    slot_index = jnp.sum((jnp.cumsum(onehot, axis=0) - onehot) * onehot, axis=1)
    slot_target = (2 * flat_ids + slot_index % 2) * half_cap + slot_index // 2
    slot_match = slot_target[:, None] == jnp.arange(devices * half_cap, dtype=jnp.int32)[None, :]
    dispatch = jnp.sum(slot_match.reshape(tok_rows, TOP, -1).astype(jnp.float32), axis=1).astype(
        jnp.bfloat16
    )
    combine_weights = jnp.sum(
        jnp.where(slot_match, route_weights[0].reshape(-1)[:, None], 0.0).reshape(
            tok_rows, TOP, -1
        ),
        axis=1,
    )
    outgoing = lax.dot_general(
        dispatch, normalized, (((0,), (0,)), ((), ())), preferred_element_type=jnp.float32
    ).astype(jnp.bfloat16)
    arrived = lax.all_to_all(
        outgoing.reshape(devices, half_cap, D), ("req", "blk"), split_axis=0, concat_axis=0, tiled=True
    ).reshape(devices * half_cap, D)
    mine = half_expert(arrived, w_gate_up[0], w_down[0])
    other = half_expert(arrived, other_gate_up, other_down)
    both = (mine.astype(jnp.float32) + other.astype(jnp.float32)).astype(jnp.bfloat16)
    returned = lax.all_to_all(
        both.reshape(devices, half_cap, D), ("req", "blk"), split_axis=0, concat_axis=0, tiled=True
    ).reshape(devices * half_cap, D)
    expert_sum = jnp.dot(
        combine_weights,
        returned.astype(jnp.float32),
        precision=lax.Precision.HIGHEST,
        preferred_element_type=jnp.float32,
    )
    return (residual + expert_sum).astype(jnp.bfloat16)[None]


def solution(mesh):
    in_specs = (
        P("req", "blk", None),
        P("req", "blk", None),
        P("req", "blk", None),
        P("req", "blk", None),
        P("req", "blk", None),
        P("req"),
        P("req", "blk", None),
        P(),
        P(),
        P("req", "blk", None),
        P("req", "blk", None),
        P(("req", "blk"), None, None),
        P(("req", "blk"), None, None),
    )
    out_specs = P("req", "blk", None)
    return jax.shard_map(local, mesh=mesh, in_specs=in_specs, out_specs=out_specs, check_vma=False)
```

time: 760 us -> 329 us (0.43)
  blocking collectives: 229 us -> 58.5 us
  waiting for transfers between devices: 227 us -> 112 us
  local copies, waits for them, and re-layouts: 151 us -> 47.5 us
  other arithmetic: 53.6 us -> 29.9 us
  matrix products: 64.3 us -> 55.6 us
  loops' own time: 7.86 us -> 0 us
    all_to_all x3 -> x1, blocking collectives: 229 us -> 58.5 us  [local(): lax.all_to_all(both.reshape(devices, half_cap, D), ('req', 'blk'), split_...]
    all_to_all x2 -> x1, waiting for transfers between devices: 171 us -> 51.4 us  [local(): lax.all_to_all(outgoing.reshape(devices, half_cap, D), ('req', 'blk'), sp...]
    dynamic_update_slice x16 -> x0, local copies, waits for them, and re-layouts: 53.8 us -> none  [local(): weighted, row_peak, row_total = lax.map(one_block, starts)]
    dynamic_slice x12 -> x0, local copies, waits for them, and re-layouts: 32.4 us -> none  [the longest x8 30.1 us: one_block(): lax.dynamic_slice_in_dim(everyone, first_row, block_size, 0)]
    mul x2 -> x0, local copies, waits for them, and re-layouts: 27.6 us -> none  [local(): weight[..., None] * weighted.reshape(blk_count, tok_rows, HEADS, HEAD_DIM)]
    sub x0 -> x2, other arithmetic: none -> 26.3 us  [the longest x1 26.3 us: attend(): probs = jnp.where(visible, jnp.exp(masked - row_peak), 0.0)]
    reduce_sum x6 -> x0, other arithmetic: 18.8 us -> none  [the longest x1 11.4 us: local(): jnp.sum(weight[..., None] * weighted.reshape(blk_count, tok_rows, HEADS,...]
    unnamed x24 -> x14, local copies, waits for them, and re-layouts: 2.06 us -> 19.7 us
  transfers between devices with their start and end apart: 3 -> 4, of which waited for: 3 -> 2; matrix products, arithmetic and copies ran while one was open for 5% -> 35% of each run, Pallas kernels for 0% -> 0%
where the time goes in v1:
time: 329 us; the launch traced here: 328 us
  waiting for transfers between devices  112 us (34%)
  blocking collectives  58.5 us (18%)
  matrix products  55.6 us (17%)
  local copies, waits for them, and re-layouts  47.5 us (14%)
  other arithmetic  29.9 us (9%)
  between operations  14.3 us (4%)
  starting transfers between devices  10.6 us (3%)
    all_gather x1, waiting for transfers between devices, local(): kv_rows = lax.all_gather(local_kv, 'blk', axis=0, tiled=True)  60.2 us
    all_to_all x1, blocking collectives, local(): lax.all_to_all(both.reshape(devices, half_cap, D), ('req', 'blk'), split_...  58.5 us
    all_to_all x1, waiting for transfers between devices, local(): lax.all_to_all(outgoing.reshape(devices, half_cap, D), ('req', 'blk'), sp...  51.4 us
    sub x1, other arithmetic, attend(): probs = jnp.where(visible, jnp.exp(masked - row_peak), 0.0)  26.3 us
    unnamed x14, local copies, waits for them, and re-layouts  19.7 us
    dot_general x2, matrix products, half_expert(): hidden = jnp.dot(arrived, gate_up.T, preferred_element_type=jnp.float32)  15.1 us
    dot_general x1, matrix products, attend(): jnp.einsum('qgrd,kgd->qgrk', query_rows, key_rows, preferred_element_type...  13 us
    slice x1, local copies, waits for them, and re-layouts, attend(): kv_rows[:, :KV_HEADS * HEAD_DIM].reshape(key_count, KV_HEADS, HEAD_DIM)  10.1 us
  transfers between devices with their start and end apart: 4, of which 2 were waited for; matrix products, arithmetic and copies ran while one was open for 35% of the time, Pallas kernels for 0%

profile of v1, /device:TPU:1, one launch (start us, length us, event | category | flops | bytes accessed | tf_op | source)
XLA Modules:
  0.0 328.0 jit_solution(2204120461121775927)
XLA Ops:
  6.5 0.0 all-gather.2.cloned.1.call-start
  6.5 1.8 maximum_maximum_fusion
  8.4 0.0 all-gather.2.cloned.1.call-update
  8.4 1.5 collective-permute-start
  9.9 0.8 copy.47
  10.6 0.1 eq.44
  10.8 0.1 eq.48
  10.9 1.1 reshape_squeeze.4
  12.7 0.9 reduce-window.6
  13.6 0.2 slice_reduce_fusion
  13.9 0.1 fusion.30
  14.0 0.1 reduce_sum.49
  14.2 0.1 copy.51
  14.3 0.7 copy.66
  15.0 0.3 convert_reduce_fusion
  15.3 0.4 and_or_fusion
  15.7 60.2 %all-gather.2.cloned.1.call-done = bf16[6144,1024]{1,0:T(8,128)(2,1)} async-done(((bf16[192,1024]{1,0:T(8,128)(2,1)}), bf16[6144,1024]{1,0:T(8,128)(2,1)}) %all-gather.2.cloned.1.call-update) | async-done | bytes 12582928 | tf_op jit(solution)/shard_map/all_gather | solution.py:88
  75.9 10.1 %fusion.55 = (bf16[6144,512]{1,0:T(8,128)(2,1)}, bf16[6144,512]{1,0:T(8,128)(2,1)}) fusion(bf16[6144,1024]{1,0:T(8,128)(2,1)} %all-gather.2.cloned.1.call-done), kind=kLoop, calls=%fused_computation.85 | loop fusion | bytes 25165824 | tf_op jit(solution)/shard_map/slice | solution.py:21
  86.0 8.8 %copy.59 = bf16[6144,512]{0,1:T(8,128)(2,1)} copy(bf16[6144,512]{1,0:T(8,128)(2,1)} %get-tuple-element.8) | data formatting | bytes 12582912
  94.8 8.7 %copy.60 = bf16[6144,512]{0,1:T(8,128)(2,1)} copy(bf16[6144,512]{1,0:T(8,128)(2,1)} %get-tuple-element.7) | data formatting | bytes 12582912
  103.5 0.0 slice-start
  103.5 13.0 %fusion.24 = f32[4,6144,64,4]{1,2,3,0:T(8,128)} fusion(bf16[6144,4,128,1]{0,2,3,1:T(8,128)(2,1)} %bitcast.81, bf16[64,4,4,128]{3,2,1,0:T(4,128)(2,1)S(1)} %reshape_squeeze.4), kind=kOutput, calls=%fused_computation.33 | convolution fusion | flops 1610612736 | bytes 31719424 | tf_op jit(solution)/shard_map/qgrd,kgd->qgrk/dot_general | solution.py:32
  116.5 0.0 slice-start.1
  116.5 26.3 %fusion.56 = (f32[64,4,4]{0,2,1:T(4,128)S(1)}, bf16[64,4,4,6144]{3,0,2,1:T(8,128)(2,1)}) fusion(f32[4,6144,64,4]{1,2,3,0:T(8,128)} %fusion.24, pred[64,6144]{1,0:T(8,128)(4,1)S(1)} %and_or_fusion), kind=kOutput, calls=%fused_computation.86 | output fusion | flops 50337792 | bytes 38146048 | tf_op jit(solution)/shard_map/sub | solution.py:37
  142.8 0.0 slice-done
  142.8 0.0 slice-done.1
  142.8 0.0 copy-start.1
  142.8 8.0 %fusion.17 = bf16[64,4,4,128]{3,0,2,1:T(8,128)(2,1)S(1)} fusion(bf16[6144,4,128,1]{0,2,3,1:T(8,128)(2,1)S(1)} %bitcast.84, bf16[64,4,4,6144]{3,0,2,1:T(8,128)(2,1)} %get-tuple-element.10, f32[64,4,4]{0,2,1:T(4,128)S(1)} %get-tuple-element.9), kind=kOutput, calls=%fused_computation.24 | convolution fusion | flops 1610874880 | bytes 19140608 | tf_op jit(solution)/shard_map/qgrk,kgd->qgrd/dot_general | solution.py:39
  150.8 0.2 copy.46
  151.0 0.2 convert_element_type.63
  151.2 0.0 copy-done.1
  151.2 0.0 copy-start.2
  151.2 5.1 %multiply_reduce_fusion = (f32[64]{0:T(128)S(1)}, f32[64,2048]{1,0:T(8,128)S(1)}) fusion(bf16[64,2048]{1,0:T(8,128)(2,1)S(1)} %convert_element_type.63, bf16[2048,2048]{1,0:T(8,128)(2,1)} %param.20, bf16[1,64,2048]{2,1,0:T(8,128)(2,1)S(1)} %copy-done.1), kind=kOutput, calls=%fused_computation.31 | convolution fusion | flops 537395136 | bytes 9437440 | tf_op jit(solution)/shard_map/dot_general | solution.py:91
  156.3 0.0 copy-start
  156.3 0.8 copy-done
  157.1 0.0 copy-done.2
  157.1 1.0 convolution_convert_fusion.2
  158.2 2.9 reshape.197
  161.0 7.9 %all-to-all-start = ((bf16[128,6,2048]{2,1,0:T(8,128)(2,1)}), bf16[128,6,2048]{2,1,0:T(8,128)(2,1)}, u32[]{:S(2)}, u32[]{:S(2)}) async-start(bf16[128,6,2048]{2,1,0:T(8,128)(2,1)} %reshape.197), calls=%async_computation | async-start | bytes 8388608 | tf_op jit(solution)/shard_map/all_to_all | solution.py:120
  169.0 1.2 collective-permute-start.1
  170.2 51.4 %all-to-all-done = bf16[128,6,2048]{2,1,0:T(8,128)(2,1)} async-done(((bf16[128,6,2048]{2,1,0:T(8,128)(2,1)}), bf16[128,6,2048]{2,1,0:T(8,128)(2,1)}, u32[]{:S(2)}, u32[]{:S(2)}) %all-to-all-start) | async-done | bytes 3145760 | tf_op jit(solution)/shard_map/all_to_all | solution.py:120
  221.5 4.9 %reshape.198 = bf16[768,2048]{1,0:T(8,128)(2,1)S(1)} reshape(bf16[128,6,2048]{2,1,0:T(8,128)(2,1)} %all-to-all-done) | data formatting | bytes 6291456 | tf_op jit(solution)/shard_map/reshape | solution.py:122
  226.4 7.6 %fusion.49 = f32[768,1408]{1,0:T(8,128)S(1)} fusion(bf16[768,2048]{1,0:T(8,128)(2,1)S(1)} %reshape.198, bf16[1,1408,2048]{2,1,0:T(8,128)(2,1)} %param.24), kind=kOutput, calls=%fused_computation.79 | convolution fusion | flops 4429185024 | bytes 13238272 | tf_op jit(solution)/shard_map/dot_general | solution.py:50
  234.0 4.9 %convolution_convert_fusion.1 = bf16[768,2048]{1,0:T(8,128)(2,1)S(1)} fusion(f32[768,1408]{1,0:T(8,128)S(1)} %fusion.49, bf16[1,704,2048]{2,1,0:T(8,128)(2,1)} %param.25), kind=kOutput, calls=%fused_computation.11 | convolution fusion | flops 2219409408 | bytes 10747904 | tf_op jit(solution)/shard_map/dot_general | solution.py:52
  238.9 0.0 collective-permute-done
  238.9 7.6 %fusion.57 = f32[768,1408]{1,0:T(8,128)S(1)} fusion(bf16[768,2048]{1,0:T(8,128)(2,1)S(1)} %reshape.198, bf16[1408,2048]{1,0:T(8,128)(2,1)} %collective-permute-done), kind=kOutput, calls=%fused_computation.87 | convolution fusion | flops 4429185024 | bytes 13238272 | tf_op jit(solution)/shard_map/dot_general | solution.py:50
  246.4 0.0 collective-permute-done.1
  246.5 4.9 %add_convert_fusion = bf16[768,2048]{1,0:T(8,128)(2,1)S(1)} fusion(bf16[768,2048]{1,0:T(8,128)(2,1)S(1)} %convolution_convert_fusion.1, bf16[704,2048]{1,0:T(8,128)(2,1)} %collective-permute-done.1, f32[768,1408]{1,0:T(8,128)S(1)} %fusion.57), kind=kOutput, calls=%fused_computation.9 | convolution fusion | flops 2225700864 | bytes 13893632 | tf_op jit(solution)/shard_map/dot_general | solution.py:52
  251.4 2.9 reshape.199
  254.3 58.5 %all_to_all.10 = bf16[128,6,2048]{2,1,0:T(8,128)(2,1)} all-to-all(bf16[128,6,2048]{2,1,0:T(8,128)(2,1)} %reshape.199), channel_id=1, replica_groups=mesh['req'=4,'blk'=32] {'req','blk'}, dimensions={0} | all-to-all | bytes 6291456 | tf_op jit(solution)/shard_map/all_to_all | solution.py:126
  312.7 4.9 %reshape.200 = bf16[768,2048]{1,0:T(8,128)(2,1)S(1)} reshape(bf16[128,6,2048]{2,1,0:T(8,128)(2,1)} %all_to_all.10) | data formatting | bytes 6291456 | tf_op jit(solution)/shard_map/reshape | solution.py:128
  317.6 3.5 %fusion.10 = bf16[1,64,2048]{2,1,0:T(8,128)(2,1)} fusion(f32[64,2048]{1,0:T(8,128)} %copy-done, f32[64,768]{1,0:T(8,128)S(1)} %get-tuple-element.6, bf16[768,2048]{1,0:T(8,128)(2,1)S(1)} %reshape.200), kind=kOutput, calls=%fused_computation.20 | convolution fusion | flops 1208221696 | bytes 4128768 | tf_op jit(solution)/shard_map/dot_general | solution.py:129
  (8 shorter events, 0.1 us)
Async XLA Ops:
  6.5 69.4 %all-gather.2.cloned.1.call-start = ((), (), s32[]{:S(2)}) async-start(), calls=%async_computation.2 | async-start | bytes 12976128 | tf_op jit(solution)/shard_map/all_gather | solution.py:88
  8.4 230.5 %collective-permute-start = (bf16[1408,2048]{1,0:T(8,128)(2,1)}, bf16[1408,2048]{1,0:T(8,128)(2,1)}, u32[]{:S(2)}, u32[]{:S(2)}) collective-permute-start(bf16[1408,2048]{1,0:T(8,128)(2,1)} %bitcast.91), channel_id=1, source_target_pairs={{0,1},{1,0},{2,3},{3,2},{4,5},{5,4},{6,7},{7,6},{8,9},{9,8},{10,11... | collective-permute-start | bytes 17301512 | tf_op jit(solution)/shard_map/ppermute | solution.py:78
  103.5 39.3 %slice-start = ((s8[6291456]{0:T(1024)(128)(4,1)}), s8[2097152]{0:T(1024)(128)(4,1)S(1)}, s32[]{:S(2)}) async-start(s8[6291456]{0:T(1024)(128)(4,1)} %bitcast.82), calls=%async_computation.3 | async-start | bytes 4194304
  116.5 26.3 %slice-start.1 = ((s8[6291456]{0:T(1024)(128)(4,1)}), s8[4194304]{0:T(1024)(128)(4,1)S(1)}, s32[]{:S(2)}) async-start(s8[6291456]{0:T(1024)(128)(4,1)} %bitcast.82), calls=%async_computation.4 | async-start | bytes 8388608
  142.8 8.4 %copy-start.1 = (bf16[1,64,2048]{2,1,0:T(8,128)(2,1)S(1)}, bf16[1,64,2048]{2,1,0:T(8,128)(2,1)}, u32[]{:S(2)}) copy-start(bf16[1,64,2048]{2,1,0:T(8,128)(2,1)} %param.19) | copy-start | bytes 786436
  151.2 5.9 %copy-start.2 = (f32[2048]{0:T(1024)S(1)}, f32[2048]{0:T(1024)}, u32[]{:S(2)}) copy-start(f32[2048]{0:T(1024)} %param.21) | copy-start | bytes 24580
  156.3 0.8 copy-start
  161.0 60.5 %all-to-all-start = ((bf16[128,6,2048]{2,1,0:T(8,128)(2,1)}), bf16[128,6,2048]{2,1,0:T(8,128)(2,1)}, u32[]{:S(2)}, u32[]{:S(2)}) async-start(bf16[128,6,2048]{2,1,0:T(8,128)(2,1)} %reshape.197), calls=%async_computation | async-start | bytes 8388608 | tf_op jit(solution)/shard_map/all_to_all | solution.py:120
  169.0 77.5 %collective-permute-start.1 = (bf16[704,2048]{1,0:T(8,128)(2,1)}, bf16[704,2048]{1,0:T(8,128)(2,1)}, u32[]{:S(2)}, u32[]{:S(2)}) collective-permute-start(bf16[704,2048]{1,0:T(8,128)(2,1)} %bitcast.15), channel_id=1, source_target_pairs={{0,1},{1,0},{2,3},{3,2},{4,5},{5,4},{6,7},{7,6},{8,9},{9,8},{10,11... | collective-permute-start | bytes 8650760 | tf_op jit(solution)/shard_map/ppermute | solution.py:79
Sparse Core Ops, SparseCore 0:
  9.6 66.2 all-gather.1

commit v2 on v1

--- a/solution.py
+++ b/solution.py
@@ -3,6 +3,8 @@
 import jax
 import jax.numpy as jnp
 from jax import lax
+from jax.experimental import pallas as pl
+from jax.experimental.pallas import tpu as pltpu
 from jax.sharding import PartitionSpec as P
 
 D = 2048
@@ -13,36 +15,85 @@
 TOP = 6
 
 
-def attend(queries, kv_rows, length, blk_index, cache_len, span_len):
+CHUNK = 512
+
+
+def attn_kernel(s_ref, q_ref, ck_ref, cv_ref, sk_ref, sv_ref, o_ref):
+    group_size = HEADS // KV_HEADS
+    tok_rows = q_ref.shape[0]
+    rows = tok_rows * group_size
+    length = s_ref[0]
+    blk = s_ref[1]
+    qb = q_ref[...]
+    qs = jnp.concatenate([qb[:, r * HEAD_DIM:(r + 1) * HEAD_DIM] for r in range(group_size)], axis=0)
+    qpos = blk * tok_rows + lax.broadcasted_iota(jnp.int32, (rows, 1), 0) % tok_rows
+    col = lax.broadcasted_iota(jnp.int32, (1, CHUNK), 1)
+    n_cache = (length + CHUNK - 1) // CHUNK
+    n_span = (blk * tok_rows + tok_rows - 1) // CHUNK + 1
+    scale = math.sqrt(HEAD_DIM)
+
+    def scores(k_ref, c):
+        k = k_ref[pl.ds(pl.multiple_of(c * CHUNK, CHUNK), CHUNK), :]
+        return lax.dot_general(qs, k, (((1,), (1,)), ((), ())), preferred_element_type=jnp.float32) / scale
+
+    def cache_mask(c):
+        return (c * CHUNK + col) < length
+
+    def span_mask(c):
+        return (c * CHUNK + col) <= qpos
+
+    def peak_step(k_ref, mask_of):
+        def body(c, m):
+            s = jnp.where(mask_of(c), scores(k_ref, c), -1e30)
+            return jnp.maximum(m, jnp.max(s, axis=-1, keepdims=True))
+        return body
+
+    m = jnp.full((rows, 1), -1e30, jnp.float32)
+    m = lax.fori_loop(0, n_cache, peak_step(ck_ref, cache_mask), m)
+    m = lax.fori_loop(0, n_span, peak_step(sk_ref, span_mask), m)
+
+    def sum_step(k_ref, v_ref, mask_of):
+        def body(c, carry):
+            l, acc = carry
+            mask = mask_of(c)
+            s = jnp.where(mask, scores(k_ref, c), -1e30)
+            p = jnp.where(mask, jnp.exp(s - m), 0.0)
+            v = v_ref[pl.ds(pl.multiple_of(c * CHUNK, CHUNK), CHUNK), :]
+            l = l + jnp.sum(p, axis=-1, keepdims=True)
+            acc = acc + jnp.dot(p.astype(jnp.bfloat16), v, preferred_element_type=jnp.float32)
+            return l, acc
+        return body
+
+    carry = (jnp.zeros((rows, 1), jnp.float32), jnp.zeros((rows, HEAD_DIM), jnp.float32))
+    carry = lax.fori_loop(0, n_cache, sum_step(ck_ref, cv_ref, cache_mask), carry)
+    l, acc = lax.fori_loop(0, n_span, sum_step(sk_ref, sv_ref, span_mask), carry)
+    out = (acc / l).astype(o_ref.dtype)
+    for r in range(group_size):
+        o_ref[:, r * HEAD_DIM:(r + 1) * HEAD_DIM] = out[r * tok_rows:(r + 1) * tok_rows]
+
+
+def attention(scalars, queries, cache_kv, span_kv):
     tok_rows = queries.shape[0]
-    group_size = HEADS // KV_HEADS
-    per_dev = cache_len + span_len
-    key_count = kv_rows.shape[0]
-    key_rows = kv_rows[:, : KV_HEADS * HEAD_DIM].reshape(key_count, KV_HEADS, HEAD_DIM)
-    value_rows = kv_rows[:, KV_HEADS * HEAD_DIM :].reshape(key_count, KV_HEADS, HEAD_DIM)
-    key_index = jnp.arange(key_count, dtype=jnp.int32)
-    owner = key_index // per_dev
-    offset = key_index % per_dev
-    in_cache = (offset < cache_len) & (owner * cache_len + offset < length)
-    span_pos = owner * span_len + offset - cache_len
-    row_index = blk_index * tok_rows + jnp.arange(tok_rows, dtype=jnp.int32)
-    in_span = (offset >= cache_len)[None, :] & (span_pos[None, :] <= row_index[:, None])
-    visible = (in_cache[None, :] | in_span)[:, None, None, :]
-    query_rows = queries.reshape(tok_rows, KV_HEADS, group_size, HEAD_DIM)
-    scores = jnp.einsum(
-        "qgrd,kgd->qgrk", query_rows, key_rows, preferred_element_type=jnp.float32
-    ) / math.sqrt(HEAD_DIM)
-    masked = jnp.where(visible, scores, -1e30)
-    row_peak = jnp.max(masked, axis=-1, keepdims=True)
-    probs = jnp.where(visible, jnp.exp(masked - row_peak), 0.0)
-    row_total = jnp.sum(probs, axis=-1)
-    weighted = jnp.einsum(
-        "qgrk,kgd->qgrd",
-        probs.astype(jnp.bfloat16),
-        value_rows,
-        preferred_element_type=jnp.float32,
-    )
-    return (weighted / row_total[..., None]).reshape(tok_rows, HEADS * HEAD_DIM).astype(jnp.bfloat16)
+    cache_len = cache_kv.shape[0]
+    span_len = span_kv.shape[0]
+    group_cols = HEAD_DIM * HEADS // KV_HEADS
+    return pl.pallas_call(
+        attn_kernel,
+        out_shape=jax.ShapeDtypeStruct(queries.shape, jnp.bfloat16),
+        grid=(KV_HEADS,),
+        in_specs=[
+            pl.BlockSpec(memory_space=pltpu.SMEM),
+            pl.BlockSpec((tok_rows, group_cols), lambda g: (0, g)),
+            pl.BlockSpec((cache_len, HEAD_DIM), lambda g: (0, g)),
+            pl.BlockSpec((cache_len, HEAD_DIM), lambda g: (0, KV_HEADS + g)),
+            pl.BlockSpec((span_len, HEAD_DIM), lambda g: (0, g)),
+            pl.BlockSpec((span_len, HEAD_DIM), lambda g: (0, KV_HEADS + g)),
+        ],
+        out_specs=pl.BlockSpec((tok_rows, group_cols), lambda g: (0, g)),
+        compiler_params=pltpu.CompilerParams(
+            dimension_semantics=("arbitrary",), vmem_limit_bytes=40 * 1024 * 1024
+        ),
+    )(scalars, queries, cache_kv, cache_kv, span_kv, span_kv)
 
 
 def half_expert(arrived, gate_up, down_rows):
@@ -78,15 +129,17 @@
     other_gate_up = lax.ppermute(w_gate_up[0], "blk", pairs)
     other_down = lax.ppermute(w_down[0], "blk", pairs)
 
-    local_kv = jnp.concatenate(
-        [
-            jnp.concatenate([cache_keys[0], span_keys[0]], 0),
-            jnp.concatenate([cache_values[0], span_values[0]], 0),
-        ],
-        1,
-    )
-    kv_rows = lax.all_gather(local_kv, "blk", axis=0, tiled=True)
-    attended = attend(queries[0], kv_rows, length, blk_index, cache_len, span_len)
+    cache_kv, span_kv = lax.all_gather(
+        (
+            jnp.concatenate([cache_keys[0], cache_values[0]], 1),
+            jnp.concatenate([span_keys[0], span_values[0]], 1),
+        ),
+        "blk",
+        axis=0,
+        tiled=True,
+    )
+    scalars = jnp.stack([length, blk_index.astype(jnp.int32)])
+    attended = attention(scalars, queries[0], cache_kv, span_kv)
 
     residual = inputs[0].astype(jnp.float32) + jnp.dot(
         attended, w_out, preferred_element_type=jnp.float32
@@ -117,15 +170,11 @@
     outgoing = lax.dot_general(
         dispatch, normalized, (((0,), (0,)), ((), ())), preferred_element_type=jnp.float32
     ).astype(jnp.bfloat16)
-    arrived = lax.all_to_all(
-        outgoing.reshape(devices, half_cap, D), ("req", "blk"), split_axis=0, concat_axis=0, tiled=True
-    ).reshape(devices * half_cap, D)
+    arrived = lax.all_to_all(outgoing, ("req", "blk"), split_axis=0, concat_axis=0, tiled=True)
     mine = half_expert(arrived, w_gate_up[0], w_down[0])
     other = half_expert(arrived, other_gate_up, other_down)
     both = (mine.astype(jnp.float32) + other.astype(jnp.float32)).astype(jnp.bfloat16)
-    returned = lax.all_to_all(
-        both.reshape(devices, half_cap, D), ("req", "blk"), split_axis=0, concat_axis=0, tiled=True
-    ).reshape(devices * half_cap, D)
+    returned = lax.all_to_all(both, ("req", "blk"), split_axis=0, concat_axis=0, tiled=True)
     expert_sum = jnp.dot(
         combine_weights,
         returned.astype(jnp.float32),

time: 329 us -> 333 us (1.012)
  waiting for transfers between devices: 112 us -> 149 us
  other arithmetic: 29.9 us -> 4.68 us
  matrix products: 55.6 us -> 31.2 us
  local copies, waits for them, and re-layouts: 47.5 us -> 24.9 us
  starting transfers between devices: 10.6 us -> 32.6 us
  Pallas kernels: 0 us -> 15.9 us
    all_gather x1 -> x2, waiting for transfers between devices: 60.2 us -> 97.8 us  [local(): lax.all_gather((jnp.concatenate([cache_keys[0], cache_values[0]], 1), jnp...]
    sub x2 -> x0, other arithmetic: 26.3 us -> none  [the longest x1 26.3 us: attend(): probs = jnp.where(visible, jnp.exp(masked - row_peak), 0.0)]
    all_to_all x1, starting transfers between devices: 7.92 us -> 29.7 us  [local(): lax.all_to_all(outgoing, ('req', 'blk'), split_axis=0, concat_axis=0, til...]
    dot_general x2 -> x0, matrix products: 21 us -> none  [the longest x1 13 us: attend(): jnp.einsum('qgrd,kgd->qgrk', query_rows, key_rows, preferred_element_type...]
    pallas_call x0 -> x1, Pallas kernels: none -> 15.9 us  [attention(): pl.pallas_call(attn_kernel, out_shape=jax.ShapeDtypeStruct(queries.shape,...]
    reshape x4 -> x0, local copies, waits for them, and re-layouts: 15.5 us -> none  [the longest x1 4.87 us: local(): arrived = lax.all_to_all(outgoing.reshape(devices, half_cap, D), ('req',...]
    all_to_all x0 -> x4, local copies, waits for them, and re-layouts: none -> 15.5 us  [the longest x2 7.74 us: local(): lax.all_to_all(both, ('req', 'blk'), split_axis=0, concat_axis=0, tiled=T...]
    unnamed x14 -> x16, local copies, waits for them, and re-layouts: 19.7 us -> 8.78 us
  transfers between devices with their start and end apart: 4 -> 5, of which waited for: 2 -> 3; matrix products, arithmetic and copies ran while one was open for 35% -> 8% of each run, Pallas kernels for 0% -> 5%
where the time goes in v2:
time: 333 us; the launch traced here: 331 us
  waiting for transfers between devices  149 us (45%)
  blocking collectives  58.5 us (18%)
  starting transfers between devices  32.6 us (10%)
  matrix products  31.2 us (9%)
  local copies, waits for them, and re-layouts  24.9 us (7%)
  Pallas kernels  15.9 us (5%)
  between operations  14.2 us (4%)
  other arithmetic  4.68 us (1%)
    all_gather x2, waiting for transfers between devices, local(): lax.all_gather((jnp.concatenate([cache_keys[0], cache_values[0]], 1), jnp...  97.8 us
    all_to_all x1, blocking collectives, local(): lax.all_to_all(both, ('req', 'blk'), split_axis=0, concat_axis=0, tiled=T...  58.5 us
    all_to_all x1, waiting for transfers between devices, local(): lax.all_to_all(outgoing, ('req', 'blk'), split_axis=0, concat_axis=0, til...  51.2 us
    all_to_all x1, starting transfers between devices, local(): lax.all_to_all(outgoing, ('req', 'blk'), split_axis=0, concat_axis=0, til...  29.7 us
    pallas_call x1, Pallas kernels, attention(): pl.pallas_call(attn_kernel, out_shape=jax.ShapeDtypeStruct(queries.shape,...  15.9 us
    dot_general x2, matrix products, half_expert(): hidden = jnp.dot(arrived, gate_up.T, preferred_element_type=jnp.float32)  15.1 us
    dot_general x2, matrix products, half_expert(): jnp.dot(activated, down_rows, preferred_element_type=jnp.float32)  9.81 us
    unnamed x16, local copies, waits for them, and re-layouts  8.78 us
  transfers between devices with their start and end apart: 5, of which 3 were waited for; matrix products, arithmetic and copies ran while one was open for 8% of the time, Pallas kernels for 5%

profile of v2, /device:TPU:1, one launch (start us, length us, event | category | flops | bytes accessed | tf_op | source)
XLA Modules:
  0.0 331.0 jit_solution(16894371530041626237)
XLA Ops:
  6.5 0.0 all-gather.5.cloned.1.call-start
  6.5 1.5 pad_maximum_fusion.1
  8.1 0.0 all-gather.5.cloned.1.call-update
  8.1 0.0 all-gather.3.cloned.1.call-start
  8.1 1.7 pad_maximum_fusion
  9.8 0.0 all-gather.3.cloned.1.call-update
  9.9 1.5 collective-permute-start
  11.3 0.8 copy.21
  12.1 0.1 eq.46
  12.2 0.1 eq.42
  12.4 0.9 reduce-window.6
  13.3 0.2 slice_reduce_fusion
  13.6 0.1 fusion.12
  13.7 0.1 reduce_sum.39
  13.9 0.1 copy.25
  13.9 0.7 copy.30
  15.3 0.1 pad_add_fusion.s_ref
  15.4 0.3 convert_reduce_fusion
  15.6 43.5 %all-gather.5.cloned.1.call-done.sk_ref.sv_ref = bf16[2048,1024]{1,0:T(8,128)(2,1)} async-done(((bf16[64,1024]{1,0:T(8,128)(2,1)}), bf16[2048,1024]{1,0:T(8,128)(2,1)}) %all-gather.5.cloned.1.call-update) | async-done | bytes 4194320 | tf_op jit(solution)/shard_map/all_gather | solution.py:132
  59.1 54.4 %all-gather.3.cloned.1.call-done.ck_ref.cv_ref = bf16[4096,1024]{1,0:T(8,128)(2,1)} async-done(((bf16[128,1024]{1,0:T(8,128)(2,1)}), bf16[4096,1024]{1,0:T(8,128)(2,1)}) %all-gather.3.cloned.1.call-update) | async-done | bytes 8388624 | tf_op jit(solution)/shard_map/all_gather | solution.py:132
  113.5 0.0 copy-start
  113.5 3.4 %copy-done = bf16[4096,1024]{1,0:T(8,128)(2,1)S(1)} copy-done((bf16[4096,1024]{1,0:T(8,128)(2,1)S(1)}, bf16[4096,1024]{1,0:T(8,128)(2,1)}, u32[]{:S(2)}) %copy-start) | copy-done | bytes 8388632
  116.9 0.0 copy-start.1
  116.9 2.2 copy-done.1
  119.1 0.0 copy-start.2
  119.1 0.9 copy-done.2
  120.0 0.0 copy-start.3
  120.0 0.0 copy-start.5
  120.0 15.9 %shard_map.127 = bf16[64,2048]{1,0:T(8,128)(2,1)S(1)} custom-call(s32[2]{0:T(128)S(1)} %pad_add_fusion.s_ref, bf16[64,2048]{1,0:T(8,128)(2,1)S(1)} %bitcast.51, bf16[4096,1024]{1,0:T(8,128)(2,1)S(1)} %copy-done, bf16[4096,1024]{1,0:T(8,128)(2,1)S(1)} %copy-done, bf16[2048,1024]{1,0:T(8,128)(2,1)S(1)} %copy-done.1, bf16[2048,1024]{1,0:T(8,128)(2,1)S(1)} %copy-done.1), custom_call_target="tpu_custom_call" | custom-call | tf_op jit(solution)/shard_map/pallas_call | solution.py:80
  135.9 0.0 copy-done.3
  135.9 0.0 copy-done.5
  135.9 0.0 copy-start.6
  135.9 1.7 multiply_reduce_fusion
  137.6 0.0 copy-start.4
  137.6 0.8 copy-done.4
  138.4 0.0 copy-done.6
  138.4 1.0 convolution_convert_fusion.2
  139.4 2.9 all_to_all.16
  142.3 29.7 %all-to-all-start = ((bf16[128,6,2048]{2,1,0:T(8,128)(2,1)}), bf16[128,6,2048]{2,1,0:T(8,128)(2,1)}, u32[]{:S(2)}, u32[]{:S(2)}) async-start(bf16[128,6,2048]{2,1,0:T(8,128)(2,1)} %all_to_all.16), calls=%async_computation | async-start | bytes 8388608 | tf_op jit(solution)/shard_map/all_to_all | solution.py:173
  172.0 1.4 collective-permute-start.1
  173.4 51.2 %all-to-all-done = bf16[128,6,2048]{2,1,0:T(8,128)(2,1)} async-done(((bf16[128,6,2048]{2,1,0:T(8,128)(2,1)}), bf16[128,6,2048]{2,1,0:T(8,128)(2,1)}, u32[]{:S(2)}, u32[]{:S(2)}) %all-to-all-start) | async-done | bytes 3145760 | tf_op jit(solution)/shard_map/all_to_all | solution.py:173
  224.6 4.9 %all_to_all.18 = bf16[768,2048]{1,0:T(8,128)(2,1)S(1)} reshape(bf16[128,6,2048]{2,1,0:T(8,128)(2,1)} %all-to-all-done) | data formatting | bytes 6291456 | tf_op jit(solution)/shard_map/all_to_all | solution.py:173
  229.5 7.6 %fusion.23 = f32[768,1408]{1,0:T(8,128)S(1)} fusion(bf16[768,2048]{1,0:T(8,128)(2,1)S(1)} %all_to_all.18, bf16[1,1408,2048]{2,1,0:T(8,128)(2,1)} %param.24), kind=kOutput, calls=%fused_computation.50 | convolution fusion | flops 4429185024 | bytes 13238272 | tf_op jit(solution)/shard_map/dot_general | solution.py:101
  237.1 4.9 %convolution_convert_fusion.1 = bf16[768,2048]{1,0:T(8,128)(2,1)S(1)} fusion(f32[768,1408]{1,0:T(8,128)S(1)} %fusion.23, bf16[1,704,2048]{2,1,0:T(8,128)(2,1)} %param.25), kind=kOutput, calls=%fused_computation.2 | convolution fusion | flops 2219409408 | bytes 10747904 | tf_op jit(solution)/shard_map/dot_general | solution.py:103
  241.9 0.0 collective-permute-done
  242.0 7.6 %fusion.27 = f32[768,1408]{1,0:T(8,128)S(1)} fusion(bf16[768,2048]{1,0:T(8,128)(2,1)S(1)} %all_to_all.18, bf16[1408,2048]{1,0:T(8,128)(2,1)} %collective-permute-done), kind=kOutput, calls=%fused_computation.54 | convolution fusion | flops 4429185024 | bytes 13238272 | tf_op jit(solution)/shard_map/dot_general | solution.py:101
  249.5 0.0 collective-permute-done.1
  249.5 4.9 %add_convert_fusion = bf16[768,2048]{1,0:T(8,128)(2,1)S(1)} fusion(bf16[768,2048]{1,0:T(8,128)(2,1)S(1)} %convolution_convert_fusion.1, bf16[704,2048]{1,0:T(8,128)(2,1)} %collective-permute-done.1, f32[768,1408]{1,0:T(8,128)S(1)} %fusion.27), kind=kOutput, calls=%fused_computation | convolution fusion | flops 2225700864 | bytes 13893632 | tf_op jit(solution)/shard_map/dot_general | solution.py:103
  254.5 2.9 all_to_all.19
  257.3 58.5 %all_to_all.24 = bf16[128,6,2048]{2,1,0:T(8,128)(2,1)} all-to-all(bf16[128,6,2048]{2,1,0:T(8,128)(2,1)} %all_to_all.19), channel_id=1, replica_groups=mesh['req'=4,'blk'=32] {'req','blk'}, dimensions={0} | all-to-all | bytes 6291456 | tf_op jit(solution)/shard_map/all_to_all | solution.py:177
  315.8 4.9 %all_to_all.21 = bf16[768,2048]{1,0:T(8,128)(2,1)S(1)} reshape(bf16[128,6,2048]{2,1,0:T(8,128)(2,1)} %all_to_all.24) | data formatting | bytes 6291456 | tf_op jit(solution)/shard_map/all_to_all | solution.py:177
  320.7 3.5 %fusion.3 = bf16[1,64,2048]{2,1,0:T(8,128)(2,1)} fusion(f32[64,2048]{1,0:T(8,128)} %copy-done.4, f32[64,768]{1,0:T(8,128)S(1)} %get-tuple-element.6, bf16[768,2048]{1,0:T(8,128)(2,1)S(1)} %all_to_all.21), kind=kOutput, calls=%fused_computation.11 | convolution fusion | flops 1208221696 | bytes 4128768 | tf_op jit(solution)/shard_map/dot_general | solution.py:178
  (4 shorter events, 0.1 us)
Async XLA Ops:
  6.5 52.6 %all-gather.5.cloned.1.call-start = ((), (), s32[]{:S(2)}) async-start(), calls=%async_computation.3 | async-start | bytes 4325376 | tf_op jit(solution)/shard_map/all_gather | solution.py:132
  8.1 105.4 %all-gather.3.cloned.1.call-start = ((), (), s32[]{:S(2)}) async-start(), calls=%async_computation.2 | async-start | bytes 8650752 | tf_op jit(solution)/shard_map/all_gather | solution.py:132
  9.9 232.1 %collective-permute-start = (bf16[1408,2048]{1,0:T(8,128)(2,1)}, bf16[1408,2048]{1,0:T(8,128)(2,1)}, u32[]{:S(2)}, u32[]{:S(2)}) collective-permute-start(bf16[1408,2048]{1,0:T(8,128)(2,1)} %bitcast.58), channel_id=1, source_target_pairs={{0,1},{1,0},{2,3},{3,2},{4,5},{5,4},{6,7},{7,6},{8,9},{9,8},{10,11... | collective-permute-start | bytes 17301512 | tf_op jit(solution)/shard_map/ppermute | solution.py:129
  113.5 3.4 %copy-start = (bf16[4096,1024]{1,0:T(8,128)(2,1)S(1)}, bf16[4096,1024]{1,0:T(8,128)(2,1)}, u32[]{:S(2)}) copy-start(bf16[4096,1024]{1,0:T(8,128)(2,1)} %all-gather.3.cloned.1.call-done.ck_ref.cv_ref) | copy-start | bytes 25165828
  116.9 2.2 copy-start.1
  119.1 0.9 copy-start.2
  120.0 15.9 %copy-start.3 = (bf16[2048,2048]{1,0:T(8,128)(2,1)S(1)}, bf16[2048,2048]{1,0:T(8,128)(2,1)}, u32[]{:S(2)}) copy-start(bf16[2048,2048]{1,0:T(8,128)(2,1)} %param.20) | copy-start | bytes 25165828
  120.0 15.9 %copy-start.5 = (bf16[1,64,2048]{2,1,0:T(8,128)(2,1)S(1)}, bf16[1,64,2048]{2,1,0:T(8,128)(2,1)}, u32[]{:S(2)}) copy-start(bf16[1,64,2048]{2,1,0:T(8,128)(2,1)} %param.19) | copy-start | bytes 786436
  135.9 2.5 copy-start.6
  137.6 0.8 copy-start.4
  142.3 82.3 %all-to-all-start = ((bf16[128,6,2048]{2,1,0:T(8,128)(2,1)}), bf16[128,6,2048]{2,1,0:T(8,128)(2,1)}, u32[]{:S(2)}, u32[]{:S(2)}) async-start(bf16[128,6,2048]{2,1,0:T(8,128)(2,1)} %all_to_all.16), calls=%async_computation | async-start | bytes 8388608 | tf_op jit(solution)/shard_map/all_to_all | solution.py:173
  172.0 77.5 %collective-permute-start.1 = (bf16[704,2048]{1,0:T(8,128)(2,1)}, bf16[704,2048]{1,0:T(8,128)(2,1)}, u32[]{:S(2)}, u32[]{:S(2)}) collective-permute-start(bf16[704,2048]{1,0:T(8,128)(2,1)} %bitcast.10), channel_id=1, source_target_pairs={{0,1},{1,0},{2,3},{3,2},{4,5},{5,4},{6,7},{7,6},{8,9},{9,8},{10,11... | collective-permute-start | bytes 8650760 | tf_op jit(solution)/shard_map/ppermute | solution.py:130
Sparse Core Ops, SparseCore 0:
  9.6 49.4 all-gather.4
  61.4 52.0 all-gather.2

commit v3 on v2

--- a/solution.py
+++ b/solution.py
@@ -18,22 +18,32 @@
 CHUNK = 512
 
 
-def attn_kernel(s_ref, q_ref, ck_ref, cv_ref, sk_ref, sv_ref, o_ref):
+def attn_kernel(s_ref, q_ref, k_ref, v_ref, o_ref):
     group_size = HEADS // KV_HEADS
     tok_rows = q_ref.shape[0]
     rows = tok_rows * group_size
+    per_dev = k_ref.shape[1]
+    span_len = per_dev - s_ref[2]
+    cache_len = s_ref[2]
     length = s_ref[0]
-    blk = s_ref[1]
+    blk = s_ref[1] + pl.program_id(1)
     qb = q_ref[...]
     qs = jnp.concatenate([qb[:, r * HEAD_DIM:(r + 1) * HEAD_DIM] for r in range(group_size)], axis=0)
     qpos = blk * tok_rows + lax.broadcasted_iota(jnp.int32, (rows, 1), 0) % tok_rows
     col = lax.broadcasted_iota(jnp.int32, (1, CHUNK), 1)
+    cache_devs = CHUNK // CACHE_ROWS
+    span_devs = CHUNK // SPAN_ROWS
     n_cache = (length + CHUNK - 1) // CHUNK
     n_span = (blk * tok_rows + tok_rows - 1) // CHUNK + 1
     scale = math.sqrt(HEAD_DIM)
 
-    def scores(k_ref, c):
-        k = k_ref[pl.ds(pl.multiple_of(c * CHUNK, CHUNK), CHUNK), :]
+    def cache_rows(ref, c):
+        return ref[pl.ds(c * cache_devs, cache_devs), pl.ds(0, CACHE_ROWS), :].reshape(CHUNK, HEAD_DIM)
+
+    def span_rows(ref, c):
+        return ref[pl.ds(c * span_devs, span_devs), pl.ds(CACHE_ROWS, SPAN_ROWS), :].reshape(CHUNK, HEAD_DIM)
+
+    def scores(k):
         return lax.dot_general(qs, k, (((1,), (1,)), ((), ())), preferred_element_type=jnp.float32) / scale
 
     def cache_mask(c):
@@ -42,58 +52,59 @@
     def span_mask(c):
         return (c * CHUNK + col) <= qpos
 
-    def peak_step(k_ref, mask_of):
+    def peak_step(rows_of, mask_of):
         def body(c, m):
-            s = jnp.where(mask_of(c), scores(k_ref, c), -1e30)
+            s = jnp.where(mask_of(c), scores(rows_of(k_ref, c)), -1e30)
             return jnp.maximum(m, jnp.max(s, axis=-1, keepdims=True))
         return body
 
     m = jnp.full((rows, 1), -1e30, jnp.float32)
-    m = lax.fori_loop(0, n_cache, peak_step(ck_ref, cache_mask), m)
-    m = lax.fori_loop(0, n_span, peak_step(sk_ref, span_mask), m)
-
-    def sum_step(k_ref, v_ref, mask_of):
+    m = lax.fori_loop(0, n_cache, peak_step(cache_rows, cache_mask), m)
+    m = lax.fori_loop(0, n_span, peak_step(span_rows, span_mask), m)
+
+    def sum_step(rows_of, mask_of):
         def body(c, carry):
             l, acc = carry
             mask = mask_of(c)
-            s = jnp.where(mask, scores(k_ref, c), -1e30)
+            s = jnp.where(mask, scores(rows_of(k_ref, c)), -1e30)
             p = jnp.where(mask, jnp.exp(s - m), 0.0)
-            v = v_ref[pl.ds(pl.multiple_of(c * CHUNK, CHUNK), CHUNK), :]
             l = l + jnp.sum(p, axis=-1, keepdims=True)
-            acc = acc + jnp.dot(p.astype(jnp.bfloat16), v, preferred_element_type=jnp.float32)
+            acc = acc + jnp.dot(p.astype(jnp.bfloat16), rows_of(v_ref, c), preferred_element_type=jnp.float32)
             return l, acc
         return body
 
     carry = (jnp.zeros((rows, 1), jnp.float32), jnp.zeros((rows, HEAD_DIM), jnp.float32))
-    carry = lax.fori_loop(0, n_cache, sum_step(ck_ref, cv_ref, cache_mask), carry)
-    l, acc = lax.fori_loop(0, n_span, sum_step(sk_ref, sv_ref, span_mask), carry)
+    carry = lax.fori_loop(0, n_cache, sum_step(cache_rows, cache_mask), carry)
+    l, acc = lax.fori_loop(0, n_span, sum_step(span_rows, span_mask), carry)
     out = (acc / l).astype(o_ref.dtype)
     for r in range(group_size):
         o_ref[:, r * HEAD_DIM:(r + 1) * HEAD_DIM] = out[r * tok_rows:(r + 1) * tok_rows]
 
 
-def attention(scalars, queries, cache_kv, span_kv):
-    tok_rows = queries.shape[0]
-    cache_len = cache_kv.shape[0]
-    span_len = span_kv.shape[0]
+CACHE_ROWS = 128
+SPAN_ROWS = 64
+
+
+def attention(scalars, queries, kv, tok_rows):
+    groups = queries.shape[1] // (HEAD_DIM * HEADS // KV_HEADS)
+    halves = queries.shape[0] // tok_rows
+    devs, per_dev, _ = kv.shape
     group_cols = HEAD_DIM * HEADS // KV_HEADS
     return pl.pallas_call(
         attn_kernel,
         out_shape=jax.ShapeDtypeStruct(queries.shape, jnp.bfloat16),
-        grid=(KV_HEADS,),
+        grid=(groups, halves),
         in_specs=[
             pl.BlockSpec(memory_space=pltpu.SMEM),
-            pl.BlockSpec((tok_rows, group_cols), lambda g: (0, g)),
-            pl.BlockSpec((cache_len, HEAD_DIM), lambda g: (0, g)),
-            pl.BlockSpec((cache_len, HEAD_DIM), lambda g: (0, KV_HEADS + g)),
-            pl.BlockSpec((span_len, HEAD_DIM), lambda g: (0, g)),
-            pl.BlockSpec((span_len, HEAD_DIM), lambda g: (0, KV_HEADS + g)),
+            pl.BlockSpec((tok_rows, group_cols), lambda g, h: (h, g)),
+            pl.BlockSpec((devs, per_dev, HEAD_DIM), lambda g, h: (0, 0, g)),
+            pl.BlockSpec((devs, per_dev, HEAD_DIM), lambda g, h: (0, 0, groups + g)),
         ],
-        out_specs=pl.BlockSpec((tok_rows, group_cols), lambda g: (0, g)),
+        out_specs=pl.BlockSpec((tok_rows, group_cols), lambda g, h: (h, g)),
         compiler_params=pltpu.CompilerParams(
-            dimension_semantics=("arbitrary",), vmem_limit_bytes=40 * 1024 * 1024
+            dimension_semantics=("arbitrary", "arbitrary"), vmem_limit_bytes=40 * 1024 * 1024
         ),
-    )(scalars, queries, cache_kv, cache_kv, span_kv, span_kv)
+    )(scalars, queries, kv, kv)
 
 
 def half_expert(arrived, gate_up, down_rows):
@@ -129,17 +140,40 @@
     other_gate_up = lax.ppermute(w_gate_up[0], "blk", pairs)
     other_down = lax.ppermute(w_down[0], "blk", pairs)
 
-    cache_kv, span_kv = lax.all_gather(
-        (
-            jnp.concatenate([cache_keys[0], cache_values[0]], 1),
-            jnp.concatenate([span_keys[0], span_values[0]], 1),
-        ),
-        "blk",
-        axis=0,
-        tiled=True,
-    )
-    scalars = jnp.stack([length, blk_index.astype(jnp.int32)])
-    attended = attention(scalars, queries[0], cache_kv, span_kv)
+    core = blk_index % 2
+    half_cols = KV_HEADS * HEAD_DIM // 2
+    key_rows = jnp.concatenate([cache_keys[0], span_keys[0]], 0)
+    value_rows = jnp.concatenate([cache_values[0], span_values[0]], 0)
+
+    def kv_cols(which):
+        return jnp.concatenate(
+            [
+                lax.dynamic_slice_in_dim(key_rows, which * half_cols, half_cols, 1),
+                lax.dynamic_slice_in_dim(value_rows, which * half_cols, half_cols, 1),
+            ],
+            1,
+        )
+
+    q_cols = queries.shape[2] // 2
+    own_q = lax.dynamic_slice_in_dim(queries[0], core * q_cols, q_cols, 1)
+    sent_q = lax.dynamic_slice_in_dim(queries[0], (1 - core) * q_cols, q_cols, 1)
+    own_kv = kv_cols(core)
+    got_kv, got_q = lax.ppermute((kv_cols(1 - core), sent_q), "blk", pairs)
+    first = core == 0
+    chip_kv = jnp.where(first, jnp.stack([own_kv, got_kv]), jnp.stack([got_kv, own_kv]))
+    chip_q = jnp.where(first, jnp.concatenate([own_q, got_q], 0), jnp.concatenate([got_q, own_q], 0))
+    same_core = [list(range(0, blk_count, 2)), list(range(1, blk_count, 2))]
+    kv = lax.all_gather(chip_kv, "blk", axis=0, tiled=True, axis_index_groups=same_core)
+    scalars = jnp.stack(
+        [length, (blk_index - core).astype(jnp.int32), jnp.int32(cache_len)]
+    )
+    chip_out = attention(scalars, chip_q, kv, tok_rows)
+    own_out = lax.dynamic_slice_in_dim(chip_out, core * tok_rows, tok_rows, 0)
+    sent_out = lax.dynamic_slice_in_dim(chip_out, (1 - core) * tok_rows, tok_rows, 0)
+    got_out = lax.ppermute(sent_out, "blk", pairs)
+    attended = jnp.where(
+        first, jnp.concatenate([own_out, got_out], 1), jnp.concatenate([got_out, own_out], 1)
+    )
 
     residual = inputs[0].astype(jnp.float32) + jnp.dot(
         attended, w_out, preferred_element_type=jnp.float32

time: 333 us -> 290 us (0.87)
  waiting for transfers between devices: 149 us -> 112 us
  starting transfers between devices: 32.6 us -> 18.8 us
  Pallas kernels: 15.9 us -> 28.8 us
  local copies, waits for them, and re-layouts: 24.9 us -> 20.8 us
    all_gather x2 -> x1, waiting for transfers between devices: 97.8 us -> 59 us  [local(): lax.all_gather(chip_kv, 'blk', axis=0, tiled=True, axis_index_groups=same...]
    all_to_all x1, starting transfers between devices: 29.7 us -> 14.4 us  [local(): lax.all_to_all(outgoing, ('req', 'blk'), split_axis=0, concat_axis=0, til...]
    pallas_call x1, Pallas kernels: 15.9 us -> 28.8 us  [attention(): pl.pallas_call(attn_kernel, out_shape=jax.ShapeDtypeStruct(queries.shape,...]
    unnamed x16, local copies, waits for them, and re-layouts: 8.78 us -> 3.67 us
  transfers between devices with their start and end apart: 5 -> 7, of which waited for: 3 -> 4; matrix products, arithmetic and copies ran while one was open for 8% -> 9% of each run, Pallas kernels for 5% -> 10%
where the time goes in v3:
time: 290 us; the launch traced here: 288 us
  waiting for transfers between devices  112 us (39%)
  blocking collectives  58.4 us (20%)
  matrix products  31.2 us (11%)
  Pallas kernels  28.8 us (10%)
  local copies, waits for them, and re-layouts  20.8 us (7%)
  starting transfers between devices  18.8 us (6%)
  between operations  14.3 us (5%)
  other arithmetic  3.4 us (1%)
    all_gather x1, waiting for transfers between devices, local(): lax.all_gather(chip_kv, 'blk', axis=0, tiled=True, axis_index_groups=same...  59 us
    all_to_all x1, blocking collectives, local(): lax.all_to_all(both, ('req', 'blk'), split_axis=0, concat_axis=0, tiled=T...  58.4 us
    all_to_all x1, waiting for transfers between devices, local(): lax.all_to_all(outgoing, ('req', 'blk'), split_axis=0, concat_axis=0, til...  51.2 us
    pallas_call x1, Pallas kernels, attention(): pl.pallas_call(attn_kernel, out_shape=jax.ShapeDtypeStruct(queries.shape,...  28.8 us
    dot_general x2, matrix products, half_expert(): hidden = jnp.dot(arrived, gate_up.T, preferred_element_type=jnp.float32)  15.1 us
    all_to_all x1, starting transfers between devices, local(): lax.all_to_all(outgoing, ('req', 'blk'), split_axis=0, concat_axis=0, til...  14.4 us
    dot_general x2, matrix products, half_expert(): jnp.dot(activated, down_rows, preferred_element_type=jnp.float32)  9.82 us
    all_to_all x2, local copies, waits for them, and re-layouts, local(): lax.all_to_all(both, ('req', 'blk'), split_axis=0, concat_axis=0, tiled=T...  7.73 us
  transfers between devices with their start and end apart: 7, of which 4 were waited for; matrix products, arithmetic and copies ran while one was open for 9% of the time, Pallas kernels for 10%

profile of v3, /device:TPU:1, one launch (start us, length us, event | category | flops | bytes accessed | tf_op | source)
XLA Modules:
  0.0 287.6 jit_solution(12106797927064662912)
XLA Ops:
  6.5 0.0 copy-start.5
  6.5 0.0 copy-start.6
  6.5 0.0 all-gather.2.cloned.1.call-start
  6.5 1.0 fusion.17
  7.6 1.5 collective-permute-start.1
  9.1 1.1 collective-permute-done.1
  10.1 0.8 maximum_select_fusion
  10.9 0.0 all-gather.2.cloned.1.call-update
  11.0 1.0 dynamic-slice_bitcast_fusion.1
  12.0 0.5 collective-permute-start
  12.4 0.1 collective-permute-start.3
  12.6 0.0 copy-done.5
  12.6 0.1 copy.26
  12.7 0.1 eq.52
  12.8 0.1 eq.48
  13.0 0.9 reduce-window.6
  13.9 0.2 slice_reduce_fusion
  14.1 0.1 fusion.22
  14.3 0.1 reduce_sum.39
  15.1 0.1 copy.30
  15.2 0.0 copy-done.6
  15.2 0.1 pad_add_fusion.s_ref
  15.3 0.0 collective-permute-done
  15.3 0.1 maximum_select_fusion.1.q_ref
  15.3 59.0 %all-gather.2.cloned.1.call-done.k_ref.v_ref = bf16[32,192,512]{2,1,0:T(8,128)(2,1)} async-done(((bf16[2,192,512]{2,1,0:T(8,128)(2,1)}), bf16[32,192,512]{2,1,0:T(8,128)(2,1)}) %all-gather.2.cloned.1.call-update) | async-done | bytes 6291472 | tf_op jit(solution)/shard_map/all_gather | solution.py:166
  74.3 0.0 copy-start
  74.3 2.8 copy-done
  77.1 0.0 copy-start.1
  77.1 0.0 copy-start.3
  77.1 28.8 %shard_map.127 = bf16[128,1024]{1,0:T(8,128)(2,1)S(1)} custom-call(s32[3]{0:T(128)S(1)} %pad_add_fusion.s_ref, bf16[128,1024]{1,0:T(8,128)(2,1)S(1)} %maximum_select_fusion.1.q_ref, bf16[32,192,512]{2,1,0:T(8,128)(2,1)S(1)} %copy-done, bf16[32,192,512]{2,1,0:T(8,128)(2,1)S(1)} %copy-done), custom_call_target="tpu_custom_call" | custom-call | tf_op jit(solution)/shard_map/pallas_call | solution.py:93
  105.9 0.9 collective-permute-start.2
  106.8 0.3 convert_reduce_fusion
  107.1 0.7 collective-permute-done.2
  107.8 0.0 copy-done.1
  107.8 0.0 copy-done.3
  107.8 0.0 copy-start.4
  107.8 1.7 multiply_reduce_fusion
  109.5 0.0 copy-start.2
  109.5 0.8 copy-done.2
  110.3 0.0 copy-done.4
  110.3 1.0 convolution_convert_fusion.2
  111.4 2.8 all_to_all.16
  114.2 14.4 %all-to-all-start = ((bf16[128,6,2048]{2,1,0:T(8,128)(2,1)}), bf16[128,6,2048]{2,1,0:T(8,128)(2,1)}, u32[]{:S(2)}, u32[]{:S(2)}) async-start(bf16[128,6,2048]{2,1,0:T(8,128)(2,1)} %all_to_all.16), calls=%async_computation | async-start | bytes 8388608 | tf_op jit(solution)/shard_map/all_to_all | solution.py:207
  128.6 1.4 collective-permute-start.4
  130.0 51.2 %all-to-all-done = bf16[128,6,2048]{2,1,0:T(8,128)(2,1)} async-done(((bf16[128,6,2048]{2,1,0:T(8,128)(2,1)}), bf16[128,6,2048]{2,1,0:T(8,128)(2,1)}, u32[]{:S(2)}, u32[]{:S(2)}) %all-to-all-start) | async-done | bytes 3145760 | tf_op jit(solution)/shard_map/all_to_all | solution.py:207
  181.2 4.9 %all_to_all.18 = bf16[768,2048]{1,0:T(8,128)(2,1)S(1)} reshape(bf16[128,6,2048]{2,1,0:T(8,128)(2,1)} %all-to-all-done) | data formatting | bytes 6291456 | tf_op jit(solution)/shard_map/all_to_all | solution.py:207
  186.0 7.6 %fusion.34 = f32[768,1408]{1,0:T(8,128)S(1)} fusion(bf16[768,2048]{1,0:T(8,128)(2,1)S(1)} %all_to_all.18, bf16[1,1408,2048]{2,1,0:T(8,128)(2,1)} %param.24), kind=kOutput, calls=%fused_computation.76 | convolution fusion | flops 4429185024 | bytes 13238272 | tf_op jit(solution)/shard_map/dot_general | solution.py:112
  193.6 4.9 %convolution_convert_fusion.1 = bf16[768,2048]{1,0:T(8,128)(2,1)S(1)} fusion(f32[768,1408]{1,0:T(8,128)S(1)} %fusion.34, bf16[1,704,2048]{2,1,0:T(8,128)(2,1)} %param.25), kind=kOutput, calls=%fused_computation.2 | convolution fusion | flops 2219409408 | bytes 10747904 | tf_op jit(solution)/shard_map/dot_general | solution.py:114
  198.5 0.0 collective-permute-done.3
  198.5 7.6 %fusion.38 = f32[768,1408]{1,0:T(8,128)S(1)} fusion(bf16[768,2048]{1,0:T(8,128)(2,1)S(1)} %all_to_all.18, bf16[1408,2048]{1,0:T(8,128)(2,1)} %collective-permute-done.3), kind=kOutput, calls=%fused_computation.80 | convolution fusion | flops 4429185024 | bytes 13238272 | tf_op jit(solution)/shard_map/dot_general | solution.py:112
  206.1 0.0 collective-permute-done.4
  206.1 4.9 %add_convert_fusion = bf16[768,2048]{1,0:T(8,128)(2,1)S(1)} fusion(bf16[768,2048]{1,0:T(8,128)(2,1)S(1)} %convolution_convert_fusion.1, bf16[704,2048]{1,0:T(8,128)(2,1)} %collective-permute-done.4, f32[768,1408]{1,0:T(8,128)S(1)} %fusion.38), kind=kOutput, calls=%fused_computation | convolution fusion | flops 2225700864 | bytes 13893632 | tf_op jit(solution)/shard_map/dot_general | solution.py:114
  211.0 2.9 all_to_all.19
  213.9 58.4 %all_to_all.24 = bf16[128,6,2048]{2,1,0:T(8,128)(2,1)} all-to-all(bf16[128,6,2048]{2,1,0:T(8,128)(2,1)} %all_to_all.19), channel_id=1, replica_groups=mesh['req'=4,'blk'=32] {'req','blk'}, dimensions={0} | all-to-all | bytes 6291456 | tf_op jit(solution)/shard_map/all_to_all | solution.py:211
  272.3 4.9 %all_to_all.21 = bf16[768,2048]{1,0:T(8,128)(2,1)S(1)} reshape(bf16[128,6,2048]{2,1,0:T(8,128)(2,1)} %all_to_all.24) | data formatting | bytes 6291456 | tf_op jit(solution)/shard_map/all_to_all | solution.py:211
  277.2 3.5 %fusion.3 = bf16[1,64,2048]{2,1,0:T(8,128)(2,1)} fusion(f32[64,2048]{1,0:T(8,128)} %copy-done.2, f32[64,768]{1,0:T(8,128)S(1)} %get-tuple-element.6, bf16[768,2048]{1,0:T(8,128)(2,1)S(1)} %all_to_all.21), kind=kOutput, calls=%fused_computation.11 | convolution fusion | flops 1208221696 | bytes 4128768 | tf_op jit(solution)/shard_map/dot_general | solution.py:212
  (8 shorter events, 0.2 us)
Async XLA Ops:
  6.5 6.0 %copy-start.5 = (s32[1,64,6]{1,0,2:T(1,128)S(1)}, s32[1,64,6]{1,0,2:T(1,128)}, u32[]{:S(2)}) copy-start(s32[1,64,6]{1,0,2:T(1,128)} %param.22) | copy-start | bytes 4612
  6.5 8.6 %copy-start.6 = (f32[1,64,6]{1,0,2:T(1,128)S(1)}, f32[1,64,6]{1,0,2:T(1,128)}, u32[]{:S(2)}) copy-start(f32[1,64,6]{1,0,2:T(1,128)} %param.23) | copy-start | bytes 4612
  6.5 67.7 %all-gather.2.cloned.1.call-start = ((), (), s32[]{:S(2)}) async-start(), calls=%async_computation.2 | async-start | bytes 6684672 | tf_op jit(solution)/shard_map/all_gather | solution.py:166
  7.6 2.5 collective-permute-start.1
  12.0 3.3 %collective-permute-start = (bf16[64,1024]{1,0:T(8,128)(2,1)S(1)}, bf16[64,1024]{1,0:T(8,128)(2,1)S(1)}, u32[]{:S(2)}, u32[]{:S(2)}) collective-permute-start(bf16[64,1024]{1,0:T(8,128)(2,1)S(1)} %get-tuple-element.10), channel_id=1, source_target_pairs={{0,1},{1,0},{2,3},{3,2},{4,5},{5,4},{6,7},{7,6},{8,9},{9,8},{10,11... | collective-permute-start | bytes 393224 | tf_op jit(solution)/shard_map/ppermute | solution.py:161
  12.4 186.1 %collective-permute-start.3 = (bf16[1408,2048]{1,0:T(8,128)(2,1)}, bf16[1408,2048]{1,0:T(8,128)(2,1)}, u32[]{:S(2)}, u32[]{:S(2)}) collective-permute-start(bf16[1408,2048]{1,0:T(8,128)(2,1)} %bitcast.63), channel_id=1, source_target_pairs={{0,1},{1,0},{2,3},{3,2},{4,5},{5,4},{6,7},{7,6},{8,9},{9,8},{10,11... | collective-permute-start | bytes 17301512 | tf_op jit(solution)/shard_map/ppermute | solution.py:140
  74.3 2.8 copy-start
  77.1 30.8 %copy-start.1 = (bf16[2048,2048]{1,0:T(8,128)(2,1)S(1)}, bf16[2048,2048]{1,0:T(8,128)(2,1)}, u32[]{:S(2)}) copy-start(bf16[2048,2048]{1,0:T(8,128)(2,1)} %param.20) | copy-start | bytes 25165828
  77.1 30.8 %copy-start.3 = (bf16[1,64,2048]{2,1,0:T(8,128)(2,1)S(1)}, bf16[1,64,2048]{2,1,0:T(8,128)(2,1)}, u32[]{:S(2)}) copy-start(bf16[1,64,2048]{2,1,0:T(8,128)(2,1)} %param.19) | copy-start | bytes 786436
  105.9 1.9 collective-permute-start.2
  107.8 2.5 copy-start.4
  109.5 0.8 copy-start.2
  114.2 67.0 %all-to-all-start = ((bf16[128,6,2048]{2,1,0:T(8,128)(2,1)}), bf16[128,6,2048]{2,1,0:T(8,128)(2,1)}, u32[]{:S(2)}, u32[]{:S(2)}) async-start(bf16[128,6,2048]{2,1,0:T(8,128)(2,1)} %all_to_all.16), calls=%async_computation | async-start | bytes 8388608 | tf_op jit(solution)/shard_map/all_to_all | solution.py:207
  128.6 77.5 %collective-permute-start.4 = (bf16[704,2048]{1,0:T(8,128)(2,1)}, bf16[704,2048]{1,0:T(8,128)(2,1)}, u32[]{:S(2)}, u32[]{:S(2)}) collective-permute-start(bf16[704,2048]{1,0:T(8,128)(2,1)} %bitcast.13), channel_id=1, source_target_pairs={{0,1},{1,0},{2,3},{3,2},{4,5},{5,4},{6,7},{7,6},{8,9},{9,8},{10,11... | collective-permute-start | bytes 8650760 | tf_op jit(solution)/shard_map/ppermute | solution.py:141
Sparse Core Ops, SparseCore 0:
  11.1 63.1 all-gather.1

commit v4 on v3

--- a/solution.py
+++ b/solution.py
@@ -22,9 +22,6 @@
     group_size = HEADS // KV_HEADS
     tok_rows = q_ref.shape[0]
     rows = tok_rows * group_size
-    per_dev = k_ref.shape[1]
-    span_len = per_dev - s_ref[2]
-    cache_len = s_ref[2]
     length = s_ref[0]
     blk = s_ref[1] + pl.program_id(1)
     qb = q_ref[...]
@@ -52,30 +49,33 @@
     def span_mask(c):
         return (c * CHUNK + col) <= qpos
 
-    def peak_step(rows_of, mask_of):
-        def body(c, m):
-            s = jnp.where(mask_of(c), scores(rows_of(k_ref, c)), -1e30)
-            return jnp.maximum(m, jnp.max(s, axis=-1, keepdims=True))
+    def step(rows_of, mask_of):
+        def body(c, carry):
+            m, l, acc = carry
+            s = scores(rows_of(k_ref, c))
+            if mask_of is not None:
+                s = jnp.where(mask_of(c), s, -1e30)
+            m_new = jnp.maximum(m, jnp.max(s, axis=-1, keepdims=True))
+            alpha = jnp.exp(m - m_new)
+            p = jnp.exp(s - m_new)
+            l = alpha * l + jnp.sum(p, axis=-1, keepdims=True)
+            acc = alpha * acc + jnp.dot(
+                p.astype(jnp.bfloat16), rows_of(v_ref, c), preferred_element_type=jnp.float32
+            )
+            return m_new, l, acc
         return body
 
-    m = jnp.full((rows, 1), -1e30, jnp.float32)
-    m = lax.fori_loop(0, n_cache, peak_step(cache_rows, cache_mask), m)
-    m = lax.fori_loop(0, n_span, peak_step(span_rows, span_mask), m)
-
-    def sum_step(rows_of, mask_of):
-        def body(c, carry):
-            l, acc = carry
-            mask = mask_of(c)
-            s = jnp.where(mask, scores(rows_of(k_ref, c)), -1e30)
-            p = jnp.where(mask, jnp.exp(s - m), 0.0)
-            l = l + jnp.sum(p, axis=-1, keepdims=True)
-            acc = acc + jnp.dot(p.astype(jnp.bfloat16), rows_of(v_ref, c), preferred_element_type=jnp.float32)
-            return l, acc
-        return body
-
-    carry = (jnp.zeros((rows, 1), jnp.float32), jnp.zeros((rows, HEAD_DIM), jnp.float32))
-    carry = lax.fori_loop(0, n_cache, sum_step(cache_rows, cache_mask), carry)
-    l, acc = lax.fori_loop(0, n_span, sum_step(span_rows, span_mask), carry)
+    carry = (
+        jnp.full((rows, 1), -1e30, jnp.float32),
+        jnp.zeros((rows, 1), jnp.float32),
+        jnp.zeros((rows, HEAD_DIM), jnp.float32),
+    )
+    cache_full = length // CHUNK
+    span_full = (blk * tok_rows + 1) // CHUNK
+    carry = lax.fori_loop(0, cache_full, step(cache_rows, None), carry)
+    carry = lax.fori_loop(cache_full, n_cache, step(cache_rows, cache_mask), carry)
+    carry = lax.fori_loop(0, span_full, step(span_rows, None), carry)
+    _, l, acc = lax.fori_loop(span_full, n_span, step(span_rows, span_mask), carry)
     out = (acc / l).astype(o_ref.dtype)
     for r in range(group_size):
         o_ref[:, r * HEAD_DIM:(r + 1) * HEAD_DIM] = out[r * tok_rows:(r + 1) * tok_rows]

time: 290 us -> 278 us (0.959)
  Pallas kernels: 28.8 us -> 16.4 us
  starting transfers between devices: 18.8 us -> 21.8 us
    pallas_call x1, Pallas kernels: 28.8 us -> 16.4 us  [attention(): pl.pallas_call(attn_kernel, out_shape=jax.ShapeDtypeStruct(queries.shape,...]
    all_to_all x1, starting transfers between devices: 14.4 us -> 17.4 us  [local(): lax.all_to_all(outgoing, ('req', 'blk'), split_axis=0, concat_axis=0, til...]
  transfers between devices with their start and end apart: 7 -> 7, of which waited for: 4 -> 4; matrix products, arithmetic and copies ran while one was open for 9% -> 9% of each run, Pallas kernels for 10% -> 6%
where the time goes in v4:
time: 278 us
  waiting for transfers between devices  112 us (40%)
  blocking collectives  58.5 us (21%)
  matrix products  31.2 us (11%)
  starting transfers between devices  21.8 us (8%)
  local copies, waits for them, and re-layouts  20.8 us (7%)
  Pallas kernels  16.4 us (6%)
  between operations  14.3 us (5%)
  other arithmetic  3.4 us (1%)
    all_gather x1, waiting for transfers between devices, local(): lax.all_gather(chip_kv, 'blk', axis=0, tiled=True, axis_index_groups=same...  59 us
    all_to_all x1, blocking collectives, local(): lax.all_to_all(both, ('req', 'blk'), split_axis=0, concat_axis=0, tiled=T...  58.5 us
    all_to_all x1, waiting for transfers between devices, local(): lax.all_to_all(outgoing, ('req', 'blk'), split_axis=0, concat_axis=0, til...  51.2 us
    all_to_all x1, starting transfers between devices, local(): lax.all_to_all(outgoing, ('req', 'blk'), split_axis=0, concat_axis=0, til...  17.4 us
    pallas_call x1, Pallas kernels, attention(): pl.pallas_call(attn_kernel, out_shape=jax.ShapeDtypeStruct(queries.shape,...  16.4 us
    dot_general x2, matrix products, half_expert(): hidden = jnp.dot(arrived, gate_up.T, preferred_element_type=jnp.float32)  15.1 us
    dot_general x2, matrix products, half_expert(): jnp.dot(activated, down_rows, preferred_element_type=jnp.float32)  9.81 us
    all_to_all x2, local copies, waits for them, and re-layouts, local(): lax.all_to_all(both, ('req', 'blk'), split_axis=0, concat_axis=0, tiled=T...  7.73 us
  transfers between devices with their start and end apart: 7, of which 4 were waited for; matrix products, arithmetic and copies ran while one was open for 9% of the time, Pallas kernels for 6%

profile of v4, /device:TPU:1, one launch (start us, length us, event | category | flops | bytes accessed | tf_op | source)
XLA Modules:
  0.0 278.2 jit_solution(6934937636606530011)
XLA Ops:
  6.5 0.0 copy-start.5
  6.5 0.0 copy-start.6
  6.5 0.0 all-gather.2.cloned.1.call-start
  6.5 1.0 fusion.17
  7.6 1.5 collective-permute-start.1
  9.1 1.1 collective-permute-done.1
  10.1 0.8 maximum_select_fusion
  10.9 0.0 all-gather.2.cloned.1.call-update
  11.0 1.0 dynamic-slice_bitcast_fusion.1
  12.0 0.5 collective-permute-start
  12.4 0.1 collective-permute-start.3
  12.6 0.0 copy-done.5
  12.6 0.1 copy.26
  12.7 0.1 eq.52
  12.8 0.1 eq.48
  13.0 0.9 reduce-window.6
  13.9 0.2 slice_reduce_fusion
  14.1 0.1 fusion.22
  14.3 0.1 reduce_sum.39
  15.1 0.1 copy.30
  15.2 0.0 copy-done.6
  15.2 0.1 pad_add_fusion.s_ref
  15.3 0.0 collective-permute-done
  15.3 0.1 maximum_select_fusion.1.q_ref
  15.3 59.0 %all-gather.2.cloned.1.call-done.k_ref.v_ref = bf16[32,192,512]{2,1,0:T(8,128)(2,1)} async-done(((bf16[2,192,512]{2,1,0:T(8,128)(2,1)}), bf16[32,192,512]{2,1,0:T(8,128)(2,1)}) %all-gather.2.cloned.1.call-update) | async-done | bytes 6291472 | tf_op jit(solution)/shard_map/all_gather | solution.py:166
  74.3 0.0 copy-start
  74.3 2.8 %copy-done = bf16[32,192,512]{2,1,0:T(8,128)(2,1)S(1)} copy-done((bf16[32,192,512]{2,1,0:T(8,128)(2,1)S(1)}, bf16[32,192,512]{2,1,0:T(8,128)(2,1)}, u32[]{:S(2)}) %copy-start) | copy-done | bytes 6291480
  77.1 0.0 copy-start.1
  77.1 0.0 copy-start.3
  77.1 16.4 %shard_map.127 = bf16[128,1024]{1,0:T(8,128)(2,1)S(1)} custom-call(s32[3]{0:T(128)S(1)} %pad_add_fusion.s_ref, bf16[128,1024]{1,0:T(8,128)(2,1)S(1)} %maximum_select_fusion.1.q_ref, bf16[32,192,512]{2,1,0:T(8,128)(2,1)S(1)} %copy-done, bf16[32,192,512]{2,1,0:T(8,128)(2,1)S(1)} %copy-done), custom_call_target="tpu_custom_call" | custom-call | tf_op jit(solution)/shard_map/pallas_call | solution.py:93
  93.6 0.9 collective-permute-start.2
  94.5 0.3 convert_reduce_fusion
  94.8 0.7 collective-permute-done.2
  95.5 0.0 copy-done.1
  95.5 0.0 copy-done.3
  95.5 0.0 copy-start.4
  95.5 1.7 multiply_reduce_fusion
  97.2 0.0 copy-start.2
  97.2 0.8 copy-done.2
  98.0 0.0 copy-done.4
  98.0 1.0 convolution_convert_fusion.2
  99.0 2.8 %all_to_all.16 = bf16[128,6,2048]{2,1,0:T(8,128)(2,1)} reshape(bf16[768,2048]{1,0:T(8,128)(2,1)S(1)} %convolution_convert_fusion.2) | data formatting | bytes 6291456 | tf_op jit(solution)/shard_map/all_to_all | solution.py:207
  101.8 17.4 %all-to-all-start = ((bf16[128,6,2048]{2,1,0:T(8,128)(2,1)}), bf16[128,6,2048]{2,1,0:T(8,128)(2,1)}, u32[]{:S(2)}, u32[]{:S(2)}) async-start(bf16[128,6,2048]{2,1,0:T(8,128)(2,1)} %all_to_all.16), calls=%async_computation | async-start | bytes 8388608 | tf_op jit(solution)/shard_map/all_to_all | solution.py:207
  119.2 1.4 collective-permute-start.4
  120.6 51.2 %all-to-all-done = bf16[128,6,2048]{2,1,0:T(8,128)(2,1)} async-done(((bf16[128,6,2048]{2,1,0:T(8,128)(2,1)}), bf16[128,6,2048]{2,1,0:T(8,128)(2,1)}, u32[]{:S(2)}, u32[]{:S(2)}) %all-to-all-start) | async-done | bytes 3145760 | tf_op jit(solution)/shard_map/all_to_all | solution.py:207
  171.8 4.9 %all_to_all.18 = bf16[768,2048]{1,0:T(8,128)(2,1)S(1)} reshape(bf16[128,6,2048]{2,1,0:T(8,128)(2,1)} %all-to-all-done) | data formatting | bytes 6291456 | tf_op jit(solution)/shard_map/all_to_all | solution.py:207
  176.7 7.6 %fusion.34 = f32[768,1408]{1,0:T(8,128)S(1)} fusion(bf16[768,2048]{1,0:T(8,128)(2,1)S(1)} %all_to_all.18, bf16[1,1408,2048]{2,1,0:T(8,128)(2,1)} %param.24), kind=kOutput, calls=%fused_computation.76 | convolution fusion | flops 4429185024 | bytes 13238272 | tf_op jit(solution)/shard_map/dot_general | solution.py:112
  184.3 4.9 %convolution_convert_fusion.1 = bf16[768,2048]{1,0:T(8,128)(2,1)S(1)} fusion(f32[768,1408]{1,0:T(8,128)S(1)} %fusion.34, bf16[1,704,2048]{2,1,0:T(8,128)(2,1)} %param.25), kind=kOutput, calls=%fused_computation.2 | convolution fusion | flops 2219409408 | bytes 10747904 | tf_op jit(solution)/shard_map/dot_general | solution.py:114
  189.1 0.0 collective-permute-done.3
  189.2 7.6 %fusion.38 = f32[768,1408]{1,0:T(8,128)S(1)} fusion(bf16[768,2048]{1,0:T(8,128)(2,1)S(1)} %all_to_all.18, bf16[1408,2048]{1,0:T(8,128)(2,1)} %collective-permute-done.3), kind=kOutput, calls=%fused_computation.80 | convolution fusion | flops 4429185024 | bytes 13238272 | tf_op jit(solution)/shard_map/dot_general | solution.py:112
  196.7 0.0 collective-permute-done.4
  196.7 4.9 %add_convert_fusion = bf16[768,2048]{1,0:T(8,128)(2,1)S(1)} fusion(bf16[768,2048]{1,0:T(8,128)(2,1)S(1)} %convolution_convert_fusion.1, bf16[704,2048]{1,0:T(8,128)(2,1)} %collective-permute-done.4, f32[768,1408]{1,0:T(8,128)S(1)} %fusion.38), kind=kOutput, calls=%fused_computation | convolution fusion | flops 2225700864 | bytes 13893632 | tf_op jit(solution)/shard_map/dot_general | solution.py:114
  201.7 2.9 %all_to_all.19 = bf16[128,6,2048]{2,1,0:T(8,128)(2,1)} reshape(bf16[768,2048]{1,0:T(8,128)(2,1)S(1)} %add_convert_fusion) | data formatting | bytes 6291456 | tf_op jit(solution)/shard_map/all_to_all | solution.py:211
  204.5 58.5 %all_to_all.24 = bf16[128,6,2048]{2,1,0:T(8,128)(2,1)} all-to-all(bf16[128,6,2048]{2,1,0:T(8,128)(2,1)} %all_to_all.19), channel_id=1, replica_groups=mesh['req'=4,'blk'=32] {'req','blk'}, dimensions={0} | all-to-all | bytes 6291456 | tf_op jit(solution)/shard_map/all_to_all | solution.py:211
  263.0 4.9 %all_to_all.21 = bf16[768,2048]{1,0:T(8,128)(2,1)S(1)} reshape(bf16[128,6,2048]{2,1,0:T(8,128)(2,1)} %all_to_all.24) | data formatting | bytes 6291456 | tf_op jit(solution)/shard_map/all_to_all | solution.py:211
  267.9 3.5 %fusion.3 = bf16[1,64,2048]{2,1,0:T(8,128)(2,1)} fusion(f32[64,2048]{1,0:T(8,128)} %copy-done.2, f32[64,768]{1,0:T(8,128)S(1)} %get-tuple-element.6, bf16[768,2048]{1,0:T(8,128)(2,1)S(1)} %all_to_all.21), kind=kOutput, calls=%fused_computation.11 | convolution fusion | flops 1208221696 | bytes 4128768 | tf_op jit(solution)/shard_map/dot_general | solution.py:212
  (8 shorter events, 0.2 us)
Async XLA Ops:
  6.5 6.0 %copy-start.5 = (s32[1,64,6]{1,0,2:T(1,128)S(1)}, s32[1,64,6]{1,0,2:T(1,128)}, u32[]{:S(2)}) copy-start(s32[1,64,6]{1,0,2:T(1,128)} %param.22) | copy-start | bytes 4612
  6.5 8.6 %copy-start.6 = (f32[1,64,6]{1,0,2:T(1,128)S(1)}, f32[1,64,6]{1,0,2:T(1,128)}, u32[]{:S(2)}) copy-start(f32[1,64,6]{1,0,2:T(1,128)} %param.23) | copy-start | bytes 4612
  6.5 67.7 %all-gather.2.cloned.1.call-start = ((), (), s32[]{:S(2)}) async-start(), calls=%async_computation.2 | async-start | bytes 6684672 | tf_op jit(solution)/shard_map/all_gather | solution.py:166
  7.6 2.5 collective-permute-start.1
  12.0 3.3 %collective-permute-start = (bf16[64,1024]{1,0:T(8,128)(2,1)S(1)}, bf16[64,1024]{1,0:T(8,128)(2,1)S(1)}, u32[]{:S(2)}, u32[]{:S(2)}) collective-permute-start(bf16[64,1024]{1,0:T(8,128)(2,1)S(1)} %get-tuple-element.10), channel_id=1, source_target_pairs={{0,1},{1,0},{2,3},{3,2},{4,5},{5,4},{6,7},{7,6},{8,9},{9,8},{10,11... | collective-permute-start | bytes 393224 | tf_op jit(solution)/shard_map/ppermute | solution.py:161
  12.4 176.7 %collective-permute-start.3 = (bf16[1408,2048]{1,0:T(8,128)(2,1)}, bf16[1408,2048]{1,0:T(8,128)(2,1)}, u32[]{:S(2)}, u32[]{:S(2)}) collective-permute-start(bf16[1408,2048]{1,0:T(8,128)(2,1)} %bitcast.63), channel_id=1, source_target_pairs={{0,1},{1,0},{2,3},{3,2},{4,5},{5,4},{6,7},{7,6},{8,9},{9,8},{10,11... | collective-permute-start | bytes 17301512 | tf_op jit(solution)/shard_map/ppermute | solution.py:140
  74.3 2.8 %copy-start = (bf16[32,192,512]{2,1,0:T(8,128)(2,1)S(1)}, bf16[32,192,512]{2,1,0:T(8,128)(2,1)}, u32[]{:S(2)}) copy-start(bf16[32,192,512]{2,1,0:T(8,128)(2,1)} %all-gather.2.cloned.1.call-done.k_ref.v_ref) | copy-start | bytes 18874372
  77.1 18.4 %copy-start.1 = (bf16[2048,2048]{1,0:T(8,128)(2,1)S(1)}, bf16[2048,2048]{1,0:T(8,128)(2,1)}, u32[]{:S(2)}) copy-start(bf16[2048,2048]{1,0:T(8,128)(2,1)} %param.20) | copy-start | bytes 25165828
  77.1 18.4 %copy-start.3 = (bf16[1,64,2048]{2,1,0:T(8,128)(2,1)S(1)}, bf16[1,64,2048]{2,1,0:T(8,128)(2,1)}, u32[]{:S(2)}) copy-start(bf16[1,64,2048]{2,1,0:T(8,128)(2,1)} %param.19) | copy-start | bytes 786436
  93.6 1.9 collective-permute-start.2
  95.5 2.5 copy-start.4
  97.2 0.8 copy-start.2
  101.8 70.0 %all-to-all-start = ((bf16[128,6,2048]{2,1,0:T(8,128)(2,1)}), bf16[128,6,2048]{2,1,0:T(8,128)(2,1)}, u32[]{:S(2)}, u32[]{:S(2)}) async-start(bf16[128,6,2048]{2,1,0:T(8,128)(2,1)} %all_to_all.16), calls=%async_computation | async-start | bytes 8388608 | tf_op jit(solution)/shard_map/all_to_all | solution.py:207
  119.2 77.5 %collective-permute-start.4 = (bf16[704,2048]{1,0:T(8,128)(2,1)}, bf16[704,2048]{1,0:T(8,128)(2,1)}, u32[]{:S(2)}, u32[]{:S(2)}) collective-permute-start(bf16[704,2048]{1,0:T(8,128)(2,1)} %bitcast.13), channel_id=1, source_target_pairs={{0,1},{1,0},{2,3},{3,2},{4,5},{5,4},{6,7},{7,6},{8,9},{9,8},{10,11... | collective-permute-start | bytes 8650760 | tf_op jit(solution)/shard_map/ppermute | solution.py:141
Sparse Core Ops, SparseCore 0:
  11.1 63.1 all-gather.1

commit v5 on v4

--- a/solution.py
+++ b/solution.py
@@ -174,6 +174,9 @@
     attended = jnp.where(
         first, jnp.concatenate([own_out, got_out], 1), jnp.concatenate([got_out, own_out], 1)
     )
+    attended, other_gate_up, other_down = lax.optimization_barrier(
+        (attended, other_gate_up, other_down)
+    )
 
     residual = inputs[0].astype(jnp.float32) + jnp.dot(
         attended, w_out, preferred_element_type=jnp.float32
@@ -186,7 +189,7 @@
 
     devices = lax.axis_size("req") * blk_count
     capacity = max(2, tok_rows * TOP * 2 // EXPERTS)
-    half_cap = (capacity + 1) // 2
+    half_cap = -(-((capacity + 1) // 2) // 8) * 8
     flat_ids = route_ids[0].reshape(-1)
     onehot = (flat_ids[:, None] == jnp.arange(EXPERTS, dtype=jnp.int32)[None, :]).astype(jnp.int32)
     slot_index = jnp.sum((jnp.cumsum(onehot, axis=0) - onehot) * onehot, axis=1)

time: 278 us -> 260 us (0.935)
  blocking collectives: 58.5 us -> 133 us
  waiting for transfers between devices: 112 us -> 58.9 us
  starting transfers between devices: 21.8 us -> 3.42 us
  local copies, waits for them, and re-layouts: 20.8 us -> 5.99 us
  Pallas kernels: 16.4 us -> 10.6 us
    all_to_all x0 -> x1, blocking collectives: none -> 75.7 us  [local(): lax.all_to_all(outgoing, ('req', 'blk'), split_axis=0, concat_axis=0, til...]
    all_to_all x1 -> x0, waiting for transfers between devices: 51.2 us -> none  [local(): lax.all_to_all(outgoing, ('req', 'blk'), split_axis=0, concat_axis=0, til...]
    all_to_all x1 -> x0, starting transfers between devices: 17.4 us -> none  [local(): lax.all_to_all(outgoing, ('req', 'blk'), split_axis=0, concat_axis=0, til...]
    all_to_all x4 -> x0, local copies, waits for them, and re-layouts: 15.4 us -> none  [the longest x2 7.73 us: local(): lax.all_to_all(both, ('req', 'blk'), split_axis=0, concat_axis=0, tiled=T...]
    all_gather x1, waiting for transfers between devices: 59 us -> 49.2 us  [local(): lax.all_gather(chip_kv, 'blk', axis=0, tiled=True, axis_index_groups=same...]
    ppermute x2, waiting for transfers between devices: 1.06 us -> 8.99 us  [local(): got_kv, got_q = lax.ppermute((kv_cols(1 - core), sent_q), 'blk', pairs)]
    pallas_call x1, Pallas kernels: 16.4 us -> 10.6 us  [attention(): pl.pallas_call(attn_kernel, out_shape=jax.ShapeDtypeStruct(queries.shape,...]
  transfers between devices with their start and end apart: 7 -> 6, of which waited for: 4 -> 4; matrix products, arithmetic and copies ran while one was open for 9% -> 2% of each run, Pallas kernels for 6% -> 4%
where the time goes in v5:
time: 260 us
  blocking collectives  133 us (51%)
  waiting for transfers between devices  58.9 us (23%)
  matrix products  30.3 us (12%)
  between operations  14.3 us (6%)
  Pallas kernels  10.6 us (4%)
  local copies, waits for them, and re-layouts  5.99 us (2%)
  other arithmetic  3.53 us (1%)
  starting transfers between devices  3.42 us (1%)
    all_to_all x1, blocking collectives, local(): lax.all_to_all(outgoing, ('req', 'blk'), split_axis=0, concat_axis=0, til...  75.7 us
    all_to_all x1, blocking collectives, local(): lax.all_to_all(both, ('req', 'blk'), split_axis=0, concat_axis=0, tiled=T...  56.8 us
    all_gather x1, waiting for transfers between devices, local(): lax.all_gather(chip_kv, 'blk', axis=0, tiled=True, axis_index_groups=same...  49.2 us
    dot_general x2, matrix products, half_expert(): hidden = jnp.dot(arrived, gate_up.T, preferred_element_type=jnp.float32)  16.3 us
    pallas_call x1, Pallas kernels, attention(): pl.pallas_call(attn_kernel, out_shape=jax.ShapeDtypeStruct(queries.shape,...  10.6 us
    ppermute x2, waiting for transfers between devices, local(): got_kv, got_q = lax.ppermute((kv_cols(1 - core), sent_q), 'blk', pairs)  8.99 us
    dot_general x2, matrix products, half_expert(): jnp.dot(activated, down_rows, preferred_element_type=jnp.float32)  7.93 us
  transfers between devices with their start and end apart: 6, of which 4 were waited for; matrix products, arithmetic and copies ran while one was open for 2% of the time, Pallas kernels for 4%

profile of v5, /device:TPU:1, one launch (start us, length us, event | category | flops | bytes accessed | tf_op | source)
XLA Modules:
  0.0 259.5 jit_solution(12259338851783035380)
XLA Ops:
  6.5 0.0 all-gather.2.cloned.1.call-start
  6.5 1.0 fusion.27
  7.6 1.5 collective-permute-start.1
  9.1 1.1 collective-permute-done.1
  10.1 0.8 maximum_select_fusion
  10.9 0.0 all-gather.2.cloned.1.call-update
  10.9 0.5 collective-permute-start.3
  11.4 0.1 collective-permute-start.4
  11.5 1.0 dynamic-slice_bitcast_fusion.1
  12.5 0.5 collective-permute-start
  13.0 0.8 copy.26
  13.7 0.1 eq.52
  13.9 0.1 eq.48
  14.0 0.9 reduce-window.6
  14.9 0.2 slice_reduce_fusion
  15.2 0.1 fusion.32
  15.3 0.1 reduce_sum.39
  16.2 0.7 copy.35
  16.9 0.1 copy.30
  16.9 0.1 pad_add_fusion.s_ref
  17.0 7.9 %collective-permute-done = bf16[64,1024]{1,0:T(8,128)(2,1)S(1)} collective-permute-done((bf16[64,1024]{1,0:T(8,128)(2,1)S(1)}, bf16[64,1024]{1,0:T(8,128)(2,1)S(1)}, u32[]{:S(2)}, u32[]{:S(2)}) %collective-permute-start) | collective-permute-done | bytes 131104 | tf_op jit(solution)/shard_map/ppermute | solution.py:161
  25.0 49.2 %all-gather.2.cloned.1.call-done.k_ref.v_ref = bf16[32,192,512]{2,1,0:T(8,128)(2,1)} async-done(((bf16[2,192,512]{2,1,0:T(8,128)(2,1)}), bf16[32,192,512]{2,1,0:T(8,128)(2,1)}) %all-gather.2.cloned.1.call-update) | async-done | bytes 6291472 | tf_op jit(solution)/shard_map/all_gather | solution.py:166
  74.2 0.0 copy-start
  74.2 2.8 %copy-done = bf16[32,192,512]{2,1,0:T(8,128)(2,1)S(1)} copy-done((bf16[32,192,512]{2,1,0:T(8,128)(2,1)S(1)}, bf16[32,192,512]{2,1,0:T(8,128)(2,1)}, u32[]{:S(2)}) %copy-start) | copy-done | bytes 6291480
  77.0 0.0 copy-start.1
  77.0 0.0 copy-start.2
  77.0 10.6 %shard_map.127 = bf16[128,1024]{1,0:T(8,128)(2,1)S(1)} custom-call(s32[3]{0:T(128)S(1)} %pad_add_fusion.s_ref, bf16[128,1024]{1,0:T(8,128)(2,1)S(1)} %maximum_select_fusion.1.q_ref, bf16[32,192,512]{2,1,0:T(8,128)(2,1)S(1)} %copy-done, bf16[32,192,512]{2,1,0:T(8,128)(2,1)S(1)} %copy-done), custom_call_target="tpu_custom_call" | custom-call | tf_op jit(solution)/shard_map/pallas_call | solution.py:93
  87.7 0.9 collective-permute-start.2
  88.6 0.4 convert_reduce_fusion
  89.0 0.6 collective-permute-done.2
  89.6 0.1 maximum_select_fusion.2
  89.7 0.0 copy-start.3
  89.7 0.0 collective-permute-done.4
  89.7 0.0 collective-permute-done.3
  89.7 0.0 copy-done.1
  89.7 0.0 copy-done.2
  89.7 1.7 multiply_reduce_fusion
  91.4 0.0 copy-done.3
  91.4 0.0 slice-start
  91.5 1.3 convert_bitcast_fusion
  92.8 0.0 slice-start.1
  92.8 75.7 %all_to_all.24 = bf16[128,8,2048]{2,1,0:T(8,128)(2,1)S(1)} all-to-all(bf16[128,8,2048]{2,1,0:T(8,128)(2,1)S(1)} %convert_bitcast_fusion), channel_id=1, replica_groups=mesh['req'=4,'blk'=32] {'req','blk'}, dimensions={0} | all-to-all | bytes 8388608 | tf_op jit(solution)/shard_map/all_to_all | solution.py:210
  168.5 0.0 slice-done
  168.5 0.0 slice-done.1
  168.5 0.0 copy-start.4
  168.5 6.7 %fusion.5 = f32[1024,1408]{1,0:T(8,128)S(1)} fusion(bf16[128,8,2048]{2,1,0:T(8,128)(2,1)S(1)} %all_to_all.24, bf16[1,1408,2048]{2,1,0:T(8,128)(2,1)S(1)} %bitcast.81), kind=kOutput, calls=%fused_computation.6 | convolution fusion | flops 5905580032 | bytes 15728640 | tf_op jit(solution)/shard_map/dot_general | solution.py:112
  175.2 0.0 copy-done.4
  175.3 3.9 %fusion.18 = bf16[1024,2048]{1,0:T(8,128)(2,1)S(1)} fusion(f32[1024,1408]{1,0:T(8,128)S(1)} %fusion.5, bf16[1,704,2048]{2,1,0:T(8,128)(2,1)S(1)} %copy-done.4), kind=kOutput, calls=%fused_computation.17 | convolution fusion | flops 2957115392 | bytes 13369344 | tf_op jit(solution)/shard_map/dot_general | solution.py:114
  179.2 9.6 %fusion.3 = f32[1024,1408]{1,0:T(8,128)S(1)} fusion(bf16[1408,2048]{1,0:T(8,128)(2,1)} %collective-permute-done.3, bf16[128,8,2048]{2,1,0:T(8,128)(2,1)S(1)} %all_to_all.24), kind=kOutput, calls=%fused_computation.4 | convolution fusion | flops 5905580032 | bytes 15728640 | tf_op jit(solution)/shard_map/dot_general | solution.py:112
  188.8 4.0 %fusion = bf16[128,8,2048]{2,1,0:T(8,128)(2,1)S(1)} fusion(bf16[1024,2048]{1,0:T(8,128)(2,1)S(1)} %fusion.18, bf16[704,2048]{1,0:T(8,128)(2,1)S(1)} %collective-permute-done.4, f32[1024,1408]{1,0:T(8,128)S(1)} %fusion.3), kind=kOutput, calls=%fused_computation.1 | convolution fusion | flops 2967601152 | bytes 17563648 | tf_op jit(solution)/shard_map/dot_general | solution.py:114
  192.8 56.8 %all_to_all.25 = bf16[128,8,2048]{2,1,0:T(8,128)(2,1)S(1)} all-to-all(bf16[128,8,2048]{2,1,0:T(8,128)(2,1)S(1)} %fusion), channel_id=1, replica_groups=mesh['req'=4,'blk'=32] {'req','blk'}, dimensions={0} | all-to-all | bytes 8388608 | tf_op jit(solution)/shard_map/all_to_all | solution.py:214
  249.6 3.0 %fusion.15 = bf16[1,64,2048]{2,1,0:T(8,128)(2,1)} fusion(f32[64,2048]{1,0:T(8,128)S(1)} %get-tuple-element.22, f32[64,1024]{1,0:T(8,128)S(1)} %get-tuple-element.12, bf16[128,8,2048]{2,1,0:T(8,128)(2,1)S(1)} %all_to_all.25), kind=kOutput, calls=%fused_computation.16 | convolution fusion | flops 1610874880 | bytes 5242880 | tf_op jit(solution)/shard_map/dot_general | solution.py:215
  (9 shorter events, 0.2 us)
Async XLA Ops:
  6.5 67.7 %all-gather.2.cloned.1.call-start = ((), (), s32[]{:S(2)}) async-start(), calls=%async_computation.2 | async-start | bytes 6684672 | tf_op jit(solution)/shard_map/all_gather | solution.py:166
  7.6 2.5 collective-permute-start.1
  10.9 78.8 %collective-permute-start.3 = (bf16[1408,2048]{1,0:T(8,128)(2,1)}, bf16[1408,2048]{1,0:T(8,128)(2,1)}, u32[]{:S(2)}, u32[]{:S(2)}) collective-permute-start(bf16[1408,2048]{1,0:T(8,128)(2,1)} %bitcast.79), channel_id=1, source_target_pairs={{0,1},{1,0},{2,3},{3,2},{4,5},{5,4},{6,7},{7,6},{8,9},{9,8},{10,11... | collective-permute-start | bytes 17301512 | tf_op jit(solution)/shard_map/ppermute | solution.py:140
  11.4 78.3 %collective-permute-start.4 = (bf16[704,2048]{1,0:T(8,128)(2,1)}, bf16[704,2048]{1,0:T(8,128)(2,1)S(1)}, u32[]{:S(2)}, u32[]{:S(2)}) collective-permute-start(bf16[704,2048]{1,0:T(8,128)(2,1)} %bitcast.82), channel_id=1, source_target_pairs={{0,1},{1,0},{2,3},{3,2},{4,5},{5,4},{6,7},{7,6},{8,9},{9,8},{10,11... | collective-permute-start | bytes 8650760 | tf_op jit(solution)/shard_map/ppermute | solution.py:141
  12.5 12.4 %collective-permute-start = (bf16[64,1024]{1,0:T(8,128)(2,1)S(1)}, bf16[64,1024]{1,0:T(8,128)(2,1)S(1)}, u32[]{:S(2)}, u32[]{:S(2)}) collective-permute-start(bf16[64,1024]{1,0:T(8,128)(2,1)S(1)} %get-tuple-element.16), channel_id=1, source_target_pairs={{0,1},{1,0},{2,3},{3,2},{4,5},{5,4},{6,7},{7,6},{8,9},{9,8},{10,11... | collective-permute-start | bytes 393224 | tf_op jit(solution)/shard_map/ppermute | solution.py:161
  74.2 2.8 %copy-start = (bf16[32,192,512]{2,1,0:T(8,128)(2,1)S(1)}, bf16[32,192,512]{2,1,0:T(8,128)(2,1)}, u32[]{:S(2)}) copy-start(bf16[32,192,512]{2,1,0:T(8,128)(2,1)} %all-gather.2.cloned.1.call-done.k_ref.v_ref) | copy-start | bytes 18874372
  77.0 12.7 %copy-start.1 = (bf16[2048,2048]{1,0:T(8,128)(2,1)S(1)}, bf16[2048,2048]{1,0:T(8,128)(2,1)}, u32[]{:S(2)}) copy-start(bf16[2048,2048]{1,0:T(8,128)(2,1)} %param.20) | copy-start | bytes 25165828
  77.0 12.7 %copy-start.2 = (bf16[1,64,2048]{2,1,0:T(8,128)(2,1)S(1)}, bf16[1,64,2048]{2,1,0:T(8,128)(2,1)}, u32[]{:S(2)}) copy-start(bf16[1,64,2048]{2,1,0:T(8,128)(2,1)} %param.19) | copy-start | bytes 786436
  87.7 1.9 collective-permute-start.2
  89.7 1.8 copy-start.3
  91.4 77.1 %slice-start = ((s8[5767168]{0:T(1024)(128)(4,1)}), s8[4194304]{0:T(1024)(128)(4,1)S(1)}, s32[]{:S(2)}) async-start(s8[5767168]{0:T(1024)(128)(4,1)} %bitcast.80), calls=%async_computation.3 | async-start | bytes 8388608
  92.8 75.7 %slice-start.1 = ((s8[5767168]{0:T(1024)(128)(4,1)}), s8[1572864]{0:T(1024)(128)(4,1)S(1)}, s32[]{:S(2)}) async-start(s8[5767168]{0:T(1024)(128)(4,1)} %bitcast.80), calls=%async_computation.4 | async-start | bytes 3145728
  168.5 6.7 %copy-start.4 = (bf16[1,704,2048]{2,1,0:T(8,128)(2,1)S(1)}, bf16[1,704,2048]{2,1,0:T(8,128)(2,1)}, u32[]{:S(2)}) copy-start(bf16[1,704,2048]{2,1,0:T(8,128)(2,1)} %param.25) | copy-start | bytes 8650756
Sparse Core Ops, SparseCore 0:
  11.0 63.1 all-gather.1

commit v6 on v5

--- a/solution.py
+++ b/solution.py
@@ -32,7 +32,8 @@
     span_devs = CHUNK // SPAN_ROWS
     n_cache = (length + CHUNK - 1) // CHUNK
     n_span = (blk * tok_rows + tok_rows - 1) // CHUNK + 1
-    scale = math.sqrt(HEAD_DIM)
+    factor = math.log2(math.e) / math.sqrt(HEAD_DIM)
+    ones = jnp.ones((CHUNK, HEAD_DIM), jnp.bfloat16)
 
     def cache_rows(ref, c):
         return ref[pl.ds(c * cache_devs, cache_devs), pl.ds(0, CACHE_ROWS), :].reshape(CHUNK, HEAD_DIM)
@@ -41,7 +42,7 @@
         return ref[pl.ds(c * span_devs, span_devs), pl.ds(CACHE_ROWS, SPAN_ROWS), :].reshape(CHUNK, HEAD_DIM)
 
     def scores(k):
-        return lax.dot_general(qs, k, (((1,), (1,)), ((), ())), preferred_element_type=jnp.float32) / scale
+        return lax.dot_general(qs, k, (((1,), (1,)), ((), ())), preferred_element_type=jnp.float32)
 
     def cache_mask(c):
         return (c * CHUNK + col) < length
@@ -56,12 +57,10 @@
             if mask_of is not None:
                 s = jnp.where(mask_of(c), s, -1e30)
             m_new = jnp.maximum(m, jnp.max(s, axis=-1, keepdims=True))
-            alpha = jnp.exp(m - m_new)
-            p = jnp.exp(s - m_new)
-            l = alpha * l + jnp.sum(p, axis=-1, keepdims=True)
-            acc = alpha * acc + jnp.dot(
-                p.astype(jnp.bfloat16), rows_of(v_ref, c), preferred_element_type=jnp.float32
-            )
+            alpha = jnp.exp2((m - m_new) * factor)
+            p = jnp.exp2((s - m_new) * factor).astype(jnp.bfloat16)
+            l = alpha * l + jnp.dot(p, ones, preferred_element_type=jnp.float32)[:, :1]
+            acc = alpha * acc + jnp.dot(p, rows_of(v_ref, c), preferred_element_type=jnp.float32)
             return m_new, l, acc
         return body
 

time: 260 us -> 263 us (1.012)
  transfers between devices with their start and end apart: 6 -> 6, of which waited for: 4 -> 4; matrix products, arithmetic and copies ran while one was open for 2% -> 2% of each run, Pallas kernels for 4% -> 5%
where the time goes in v6:
time: 263 us
  blocking collectives  134 us (51%)
  waiting for transfers between devices  58.9 us (22%)
  matrix products  30.3 us (12%)
  between operations  14.3 us (5%)
  Pallas kernels  12 us (5%)
  local copies, waits for them, and re-layouts  5.99 us (2%)
  other arithmetic  3.53 us (1%)
  starting transfers between devices  3.41 us (1%)
    all_to_all x1, blocking collectives, local(): lax.all_to_all(outgoing, ('req', 'blk'), split_axis=0, concat_axis=0, til...  77.5 us
    all_to_all x1, blocking collectives, local(): lax.all_to_all(both, ('req', 'blk'), split_axis=0, concat_axis=0, tiled=T...  56.9 us
    all_gather x1, waiting for transfers between devices, local(): lax.all_gather(chip_kv, 'blk', axis=0, tiled=True, axis_index_groups=same...  49.2 us
    dot_general x2, matrix products, half_expert(): hidden = jnp.dot(arrived, gate_up.T, preferred_element_type=jnp.float32)  16.3 us
    pallas_call x1, Pallas kernels, attention(): pl.pallas_call(attn_kernel, out_shape=jax.ShapeDtypeStruct(queries.shape,...  12 us
    ppermute x2, waiting for transfers between devices, local(): got_kv, got_q = lax.ppermute((kv_cols(1 - core), sent_q), 'blk', pairs)  8.99 us
    dot_general x2, matrix products, half_expert(): jnp.dot(activated, down_rows, preferred_element_type=jnp.float32)  7.93 us
  transfers between devices with their start and end apart: 6, of which 4 were waited for; matrix products, arithmetic and copies ran while one was open for 2% of the time, Pallas kernels for 5%

profile of v6, /device:TPU:1, one launch (start us, length us, event | category | flops | bytes accessed | tf_op | source)
XLA Modules:
  0.0 262.7 jit_solution(18035420464096166027)
XLA Ops:
  6.5 0.0 all-gather.2.cloned.1.call-start
  6.5 1.0 fusion.27
  7.6 1.5 collective-permute-start.1
  9.1 1.1 collective-permute-done.1
  10.1 0.8 maximum_select_fusion
  10.9 0.0 all-gather.2.cloned.1.call-update
  10.9 0.5 collective-permute-start.3
  11.4 0.1 collective-permute-start.4
  11.5 1.0 dynamic-slice_bitcast_fusion.1
  12.5 0.5 collective-permute-start
  13.0 0.8 copy.26
  13.7 0.1 eq.52
  13.9 0.1 eq.48
  14.0 0.9 reduce-window.6
  14.9 0.2 slice_reduce_fusion
  15.2 0.1 fusion.32
  15.3 0.1 reduce_sum.39
  16.2 0.7 copy.35
  16.9 0.1 copy.30
  16.9 0.1 pad_add_fusion.s_ref
  17.0 7.9 %collective-permute-done = bf16[64,1024]{1,0:T(8,128)(2,1)S(1)} collective-permute-done((bf16[64,1024]{1,0:T(8,128)(2,1)S(1)}, bf16[64,1024]{1,0:T(8,128)(2,1)S(1)}, u32[]{:S(2)}, u32[]{:S(2)}) %collective-permute-start) | collective-permute-done | bytes 131104 | tf_op jit(solution)/shard_map/ppermute | solution.py:160
  25.0 49.2 %all-gather.2.cloned.1.call-done.k_ref.v_ref = bf16[32,192,512]{2,1,0:T(8,128)(2,1)} async-done(((bf16[2,192,512]{2,1,0:T(8,128)(2,1)}), bf16[32,192,512]{2,1,0:T(8,128)(2,1)}) %all-gather.2.cloned.1.call-update) | async-done | bytes 6291472 | tf_op jit(solution)/shard_map/all_gather | solution.py:165
  74.2 0.0 copy-start
  74.2 2.8 %copy-done = bf16[32,192,512]{2,1,0:T(8,128)(2,1)S(1)} copy-done((bf16[32,192,512]{2,1,0:T(8,128)(2,1)S(1)}, bf16[32,192,512]{2,1,0:T(8,128)(2,1)}, u32[]{:S(2)}) %copy-start) | copy-done | bytes 6291480
  77.0 0.0 copy-start.1
  77.0 0.0 copy-start.2
  77.0 12.0 %shard_map.127 = bf16[128,1024]{1,0:T(8,128)(2,1)S(1)} custom-call(s32[3]{0:T(128)S(1)} %pad_add_fusion.s_ref, bf16[128,1024]{1,0:T(8,128)(2,1)S(1)} %maximum_select_fusion.1.q_ref, bf16[32,192,512]{2,1,0:T(8,128)(2,1)S(1)} %copy-done, bf16[32,192,512]{2,1,0:T(8,128)(2,1)S(1)} %copy-done), custom_call_target="tpu_custom_call" | custom-call | tf_op jit(solution)/shard_map/pallas_call | solution.py:92
  89.1 0.9 collective-permute-start.2
  90.0 0.4 convert_reduce_fusion
  90.4 0.6 collective-permute-done.2
  91.0 0.1 maximum_select_fusion.2
  91.1 0.0 copy-start.3
  91.1 0.0 collective-permute-done.4
  91.1 0.0 collective-permute-done.3
  91.1 0.0 copy-done.1
  91.1 0.0 copy-done.2
  91.1 1.7 multiply_reduce_fusion
  92.9 0.0 copy-done.3
  92.9 0.0 slice-start
  92.9 1.3 convert_bitcast_fusion
  94.2 0.0 slice-start.1
  94.2 77.5 %all_to_all.24 = bf16[128,8,2048]{2,1,0:T(8,128)(2,1)S(1)} all-to-all(bf16[128,8,2048]{2,1,0:T(8,128)(2,1)S(1)} %convert_bitcast_fusion), channel_id=1, replica_groups=mesh['req'=4,'blk'=32] {'req','blk'}, dimensions={0} | all-to-all | bytes 8388608 | tf_op jit(solution)/shard_map/all_to_all | solution.py:209
  171.7 0.0 slice-done
  171.7 0.0 slice-done.1
  171.7 0.0 copy-start.4
  171.7 6.7 %fusion.5 = f32[1024,1408]{1,0:T(8,128)S(1)} fusion(bf16[128,8,2048]{2,1,0:T(8,128)(2,1)S(1)} %all_to_all.24, bf16[1,1408,2048]{2,1,0:T(8,128)(2,1)S(1)} %bitcast.81), kind=kOutput, calls=%fused_computation.6 | convolution fusion | flops 5905580032 | bytes 15728640 | tf_op jit(solution)/shard_map/dot_general | solution.py:111
  178.4 0.0 copy-done.4
  178.4 3.9 %fusion.18 = bf16[1024,2048]{1,0:T(8,128)(2,1)S(1)} fusion(f32[1024,1408]{1,0:T(8,128)S(1)} %fusion.5, bf16[1,704,2048]{2,1,0:T(8,128)(2,1)S(1)} %copy-done.4), kind=kOutput, calls=%fused_computation.17 | convolution fusion | flops 2957115392 | bytes 13369344 | tf_op jit(solution)/shard_map/dot_general | solution.py:113
  182.4 9.6 %fusion.3 = f32[1024,1408]{1,0:T(8,128)S(1)} fusion(bf16[1408,2048]{1,0:T(8,128)(2,1)} %collective-permute-done.3, bf16[128,8,2048]{2,1,0:T(8,128)(2,1)S(1)} %all_to_all.24), kind=kOutput, calls=%fused_computation.4 | convolution fusion | flops 5905580032 | bytes 15728640 | tf_op jit(solution)/shard_map/dot_general | solution.py:111
  192.0 4.0 %fusion = bf16[128,8,2048]{2,1,0:T(8,128)(2,1)S(1)} fusion(bf16[1024,2048]{1,0:T(8,128)(2,1)S(1)} %fusion.18, bf16[704,2048]{1,0:T(8,128)(2,1)S(1)} %collective-permute-done.4, f32[1024,1408]{1,0:T(8,128)S(1)} %fusion.3), kind=kOutput, calls=%fused_computation.1 | convolution fusion | flops 2967601152 | bytes 17563648 | tf_op jit(solution)/shard_map/dot_general | solution.py:113
  196.0 56.9 %all_to_all.25 = bf16[128,8,2048]{2,1,0:T(8,128)(2,1)S(1)} all-to-all(bf16[128,8,2048]{2,1,0:T(8,128)(2,1)S(1)} %fusion), channel_id=1, replica_groups=mesh['req'=4,'blk'=32] {'req','blk'}, dimensions={0} | all-to-all | bytes 8388608 | tf_op jit(solution)/shard_map/all_to_all | solution.py:213
  252.8 3.0 %fusion.15 = bf16[1,64,2048]{2,1,0:T(8,128)(2,1)} fusion(f32[64,2048]{1,0:T(8,128)S(1)} %get-tuple-element.22, f32[64,1024]{1,0:T(8,128)S(1)} %get-tuple-element.12, bf16[128,8,2048]{2,1,0:T(8,128)(2,1)S(1)} %all_to_all.25), kind=kOutput, calls=%fused_computation.16 | convolution fusion | flops 1610874880 | bytes 5242880 | tf_op jit(solution)/shard_map/dot_general | solution.py:214
  (9 shorter events, 0.2 us)
Async XLA Ops:
  6.5 67.7 %all-gather.2.cloned.1.call-start = ((), (), s32[]{:S(2)}) async-start(), calls=%async_computation.2 | async-start | bytes 6684672 | tf_op jit(solution)/shard_map/all_gather | solution.py:165
  7.6 2.5 collective-permute-start.1
  10.9 80.2 %collective-permute-start.3 = (bf16[1408,2048]{1,0:T(8,128)(2,1)}, bf16[1408,2048]{1,0:T(8,128)(2,1)}, u32[]{:S(2)}, u32[]{:S(2)}) collective-permute-start(bf16[1408,2048]{1,0:T(8,128)(2,1)} %bitcast.79), channel_id=1, source_target_pairs={{0,1},{1,0},{2,3},{3,2},{4,5},{5,4},{6,7},{7,6},{8,9},{9,8},{10,11... | collective-permute-start | bytes 17301512 | tf_op jit(solution)/shard_map/ppermute | solution.py:139
  11.4 79.7 %collective-permute-start.4 = (bf16[704,2048]{1,0:T(8,128)(2,1)}, bf16[704,2048]{1,0:T(8,128)(2,1)S(1)}, u32[]{:S(2)}, u32[]{:S(2)}) collective-permute-start(bf16[704,2048]{1,0:T(8,128)(2,1)} %bitcast.82), channel_id=1, source_target_pairs={{0,1},{1,0},{2,3},{3,2},{4,5},{5,4},{6,7},{7,6},{8,9},{9,8},{10,11... | collective-permute-start | bytes 8650760 | tf_op jit(solution)/shard_map/ppermute | solution.py:140
  12.5 12.4 %collective-permute-start = (bf16[64,1024]{1,0:T(8,128)(2,1)S(1)}, bf16[64,1024]{1,0:T(8,128)(2,1)S(1)}, u32[]{:S(2)}, u32[]{:S(2)}) collective-permute-start(bf16[64,1024]{1,0:T(8,128)(2,1)S(1)} %get-tuple-element.16), channel_id=1, source_target_pairs={{0,1},{1,0},{2,3},{3,2},{4,5},{5,4},{6,7},{7,6},{8,9},{9,8},{10,11... | collective-permute-start | bytes 393224 | tf_op jit(solution)/shard_map/ppermute | solution.py:160
  74.2 2.8 %copy-start = (bf16[32,192,512]{2,1,0:T(8,128)(2,1)S(1)}, bf16[32,192,512]{2,1,0:T(8,128)(2,1)}, u32[]{:S(2)}) copy-start(bf16[32,192,512]{2,1,0:T(8,128)(2,1)} %all-gather.2.cloned.1.call-done.k_ref.v_ref) | copy-start | bytes 18874372
  77.0 14.1 %copy-start.1 = (bf16[2048,2048]{1,0:T(8,128)(2,1)S(1)}, bf16[2048,2048]{1,0:T(8,128)(2,1)}, u32[]{:S(2)}) copy-start(bf16[2048,2048]{1,0:T(8,128)(2,1)} %param.20) | copy-start | bytes 25165828
  77.0 14.1 %copy-start.2 = (bf16[1,64,2048]{2,1,0:T(8,128)(2,1)S(1)}, bf16[1,64,2048]{2,1,0:T(8,128)(2,1)}, u32[]{:S(2)}) copy-start(bf16[1,64,2048]{2,1,0:T(8,128)(2,1)} %param.19) | copy-start | bytes 786436
  89.1 1.9 collective-permute-start.2
  91.1 1.8 copy-start.3
  92.9 78.8 %slice-start = ((s8[5767168]{0:T(1024)(128)(4,1)}), s8[4194304]{0:T(1024)(128)(4,1)S(1)}, s32[]{:S(2)}) async-start(s8[5767168]{0:T(1024)(128)(4,1)} %bitcast.80), calls=%async_computation.3 | async-start | bytes 8388608
  94.2 77.5 %slice-start.1 = ((s8[5767168]{0:T(1024)(128)(4,1)}), s8[1572864]{0:T(1024)(128)(4,1)S(1)}, s32[]{:S(2)}) async-start(s8[5767168]{0:T(1024)(128)(4,1)} %bitcast.80), calls=%async_computation.4 | async-start | bytes 3145728
  171.7 6.7 %copy-start.4 = (bf16[1,704,2048]{2,1,0:T(8,128)(2,1)S(1)}, bf16[1,704,2048]{2,1,0:T(8,128)(2,1)}, u32[]{:S(2)}) copy-start(bf16[1,704,2048]{2,1,0:T(8,128)(2,1)} %param.25) | copy-start | bytes 8650756
Sparse Core Ops, SparseCore 0:
  11.0 63.1 all-gather.1

commit v7 on v5

--- a/solution.py
+++ b/solution.py
@@ -15,7 +15,7 @@
 TOP = 6
 
 
-CHUNK = 512
+CHUNK = 256
 
 
 def attn_kernel(s_ref, q_ref, k_ref, v_ref, o_ref):
@@ -32,7 +32,7 @@
     span_devs = CHUNK // SPAN_ROWS
     n_cache = (length + CHUNK - 1) // CHUNK
     n_span = (blk * tok_rows + tok_rows - 1) // CHUNK + 1
-    scale = math.sqrt(HEAD_DIM)
+    factor = math.log2(math.e) / math.sqrt(HEAD_DIM)
 
     def cache_rows(ref, c):
         return ref[pl.ds(c * cache_devs, cache_devs), pl.ds(0, CACHE_ROWS), :].reshape(CHUNK, HEAD_DIM)
@@ -41,7 +41,7 @@
         return ref[pl.ds(c * span_devs, span_devs), pl.ds(CACHE_ROWS, SPAN_ROWS), :].reshape(CHUNK, HEAD_DIM)
 
     def scores(k):
-        return lax.dot_general(qs, k, (((1,), (1,)), ((), ())), preferred_element_type=jnp.float32) / scale
+        return lax.dot_general(qs, k, (((1,), (1,)), ((), ())), preferred_element_type=jnp.float32)
 
     def cache_mask(c):
         return (c * CHUNK + col) < length
@@ -56,8 +56,8 @@
             if mask_of is not None:
                 s = jnp.where(mask_of(c), s, -1e30)
             m_new = jnp.maximum(m, jnp.max(s, axis=-1, keepdims=True))
-            alpha = jnp.exp(m - m_new)
-            p = jnp.exp(s - m_new)
+            alpha = jnp.exp2((m - m_new) * factor)
+            p = jnp.exp2((s - m_new) * factor)
             l = alpha * l + jnp.sum(p, axis=-1, keepdims=True)
             acc = alpha * acc + jnp.dot(
                 p.astype(jnp.bfloat16), rows_of(v_ref, c), preferred_element_type=jnp.float32

time: 260 us -> 277 us (1.065)
  Pallas kernels: 10.6 us -> 29.2 us
    pallas_call x1, Pallas kernels: 10.6 us -> 29.2 us  [attention(): pl.pallas_call(attn_kernel, out_shape=jax.ShapeDtypeStruct(queries.shape,...]
  transfers between devices with their start and end apart: 6 -> 6, of which waited for: 4 -> 4; matrix products, arithmetic and copies ran while one was open for 2% -> 2% of each run, Pallas kernels for 4% -> 10%
where the time goes in v7:
time: 277 us; the launch traced here: 278 us
  blocking collectives  133 us (48%)
  waiting for transfers between devices  58.9 us (21%)
  matrix products  30.3 us (11%)
  Pallas kernels  29.2 us (11%)
  between operations  14.3 us (5%)
  local copies, waits for them, and re-layouts  5.99 us (2%)
  other arithmetic  3.53 us (1%)
  starting transfers between devices  3.42 us (1%)
    all_to_all x1, blocking collectives, local(): lax.all_to_all(outgoing, ('req', 'blk'), split_axis=0, concat_axis=0, til...  75.8 us
    all_to_all x1, blocking collectives, local(): lax.all_to_all(both, ('req', 'blk'), split_axis=0, concat_axis=0, tiled=T...  56.9 us
    all_gather x1, waiting for transfers between devices, local(): lax.all_gather(chip_kv, 'blk', axis=0, tiled=True, axis_index_groups=same...  49.2 us
    pallas_call x1, Pallas kernels, attention(): pl.pallas_call(attn_kernel, out_shape=jax.ShapeDtypeStruct(queries.shape,...  29.2 us
    dot_general x2, matrix products, half_expert(): hidden = jnp.dot(arrived, gate_up.T, preferred_element_type=jnp.float32)  16.3 us
    ppermute x2, waiting for transfers between devices, local(): got_kv, got_q = lax.ppermute((kv_cols(1 - core), sent_q), 'blk', pairs)  8.99 us
    dot_general x2, matrix products, half_expert(): jnp.dot(activated, down_rows, preferred_element_type=jnp.float32)  7.93 us
  transfers between devices with their start and end apart: 6, of which 4 were waited for; matrix products, arithmetic and copies ran while one was open for 2% of the time, Pallas kernels for 10%

profile of v7, /device:TPU:1, one launch (start us, length us, event | category | flops | bytes accessed | tf_op | source)
XLA Modules:
  0.0 278.2 jit_solution(5288327093953200913)
XLA Ops:
  6.5 0.0 all-gather.2.cloned.1.call-start
  6.5 1.0 fusion.27
  7.6 1.5 collective-permute-start.1
  9.1 1.1 collective-permute-done.1
  10.1 0.8 maximum_select_fusion
  10.9 0.0 all-gather.2.cloned.1.call-update
  10.9 0.5 collective-permute-start.3
  11.4 0.1 collective-permute-start.4
  11.5 1.0 dynamic-slice_bitcast_fusion.1
  12.5 0.5 collective-permute-start
  13.0 0.8 copy.26
  13.7 0.1 eq.52
  13.9 0.1 eq.48
  14.0 0.9 reduce-window.6
  14.9 0.2 slice_reduce_fusion
  15.2 0.1 fusion.32
  15.3 0.1 reduce_sum.39
  16.2 0.7 copy.35
  16.9 0.1 copy.30
  16.9 0.1 pad_add_fusion.s_ref
  17.0 7.9 %collective-permute-done = bf16[64,1024]{1,0:T(8,128)(2,1)S(1)} collective-permute-done((bf16[64,1024]{1,0:T(8,128)(2,1)S(1)}, bf16[64,1024]{1,0:T(8,128)(2,1)S(1)}, u32[]{:S(2)}, u32[]{:S(2)}) %collective-permute-start) | collective-permute-done | bytes 131104 | tf_op jit(solution)/shard_map/ppermute | solution.py:161
  25.0 49.2 %all-gather.2.cloned.1.call-done.k_ref.v_ref = bf16[32,192,512]{2,1,0:T(8,128)(2,1)} async-done(((bf16[2,192,512]{2,1,0:T(8,128)(2,1)}), bf16[32,192,512]{2,1,0:T(8,128)(2,1)}) %all-gather.2.cloned.1.call-update) | async-done | bytes 6291472 | tf_op jit(solution)/shard_map/all_gather | solution.py:166
  74.2 0.0 copy-start
  74.2 2.8 %copy-done = bf16[32,192,512]{2,1,0:T(8,128)(2,1)S(1)} copy-done((bf16[32,192,512]{2,1,0:T(8,128)(2,1)S(1)}, bf16[32,192,512]{2,1,0:T(8,128)(2,1)}, u32[]{:S(2)}) %copy-start) | copy-done | bytes 6291480
  77.0 0.0 copy-start.1
  77.0 0.0 copy-start.2
  77.0 29.2 %shard_map.127 = bf16[128,1024]{1,0:T(8,128)(2,1)S(1)} custom-call(s32[3]{0:T(128)S(1)} %pad_add_fusion.s_ref, bf16[128,1024]{1,0:T(8,128)(2,1)S(1)} %maximum_select_fusion.1.q_ref, bf16[32,192,512]{2,1,0:T(8,128)(2,1)S(1)} %copy-done, bf16[32,192,512]{2,1,0:T(8,128)(2,1)S(1)} %copy-done), custom_call_target="tpu_custom_call" | custom-call | tf_op jit(solution)/shard_map/pallas_call | solution.py:93
  106.3 0.9 collective-permute-start.2
  107.2 0.4 convert_reduce_fusion
  107.5 0.6 collective-permute-done.2
  108.2 0.1 maximum_select_fusion.2
  108.2 0.0 copy-start.3
  108.2 0.0 collective-permute-done.4
  108.3 0.0 collective-permute-done.3
  108.3 0.0 copy-done.1
  108.3 0.0 copy-done.2
  108.3 1.7 multiply_reduce_fusion
  110.0 0.0 copy-done.3
  110.0 0.0 slice-start
  110.0 1.3 convert_bitcast_fusion
  111.3 0.0 slice-start.1
  111.4 75.8 %all_to_all.24 = bf16[128,8,2048]{2,1,0:T(8,128)(2,1)S(1)} all-to-all(bf16[128,8,2048]{2,1,0:T(8,128)(2,1)S(1)} %convert_bitcast_fusion), channel_id=1, replica_groups=mesh['req'=4,'blk'=32] {'req','blk'}, dimensions={0} | all-to-all | bytes 8388608 | tf_op jit(solution)/shard_map/all_to_all | solution.py:210
  187.1 0.0 slice-done
  187.1 0.0 slice-done.1
  187.2 0.0 copy-start.4
  187.2 6.7 %fusion.5 = f32[1024,1408]{1,0:T(8,128)S(1)} fusion(bf16[128,8,2048]{2,1,0:T(8,128)(2,1)S(1)} %all_to_all.24, bf16[1,1408,2048]{2,1,0:T(8,128)(2,1)S(1)} %bitcast.81), kind=kOutput, calls=%fused_computation.6 | convolution fusion | flops 5905580032 | bytes 15728640 | tf_op jit(solution)/shard_map/dot_general | solution.py:112
  193.9 0.0 copy-done.4
  193.9 3.9 %fusion.18 = bf16[1024,2048]{1,0:T(8,128)(2,1)S(1)} fusion(f32[1024,1408]{1,0:T(8,128)S(1)} %fusion.5, bf16[1,704,2048]{2,1,0:T(8,128)(2,1)S(1)} %copy-done.4), kind=kOutput, calls=%fused_computation.17 | convolution fusion | flops 2957115392 | bytes 13369344 | tf_op jit(solution)/shard_map/dot_general | solution.py:114
  197.8 9.6 %fusion.3 = f32[1024,1408]{1,0:T(8,128)S(1)} fusion(bf16[1408,2048]{1,0:T(8,128)(2,1)} %collective-permute-done.3, bf16[128,8,2048]{2,1,0:T(8,128)(2,1)S(1)} %all_to_all.24), kind=kOutput, calls=%fused_computation.4 | convolution fusion | flops 5905580032 | bytes 15728640 | tf_op jit(solution)/shard_map/dot_general | solution.py:112
  207.4 4.0 %fusion = bf16[128,8,2048]{2,1,0:T(8,128)(2,1)S(1)} fusion(bf16[1024,2048]{1,0:T(8,128)(2,1)S(1)} %fusion.18, bf16[704,2048]{1,0:T(8,128)(2,1)S(1)} %collective-permute-done.4, f32[1024,1408]{1,0:T(8,128)S(1)} %fusion.3), kind=kOutput, calls=%fused_computation.1 | convolution fusion | flops 2967601152 | bytes 17563648 | tf_op jit(solution)/shard_map/dot_general | solution.py:114
  211.4 56.9 %all_to_all.25 = bf16[128,8,2048]{2,1,0:T(8,128)(2,1)S(1)} all-to-all(bf16[128,8,2048]{2,1,0:T(8,128)(2,1)S(1)} %fusion), channel_id=1, replica_groups=mesh['req'=4,'blk'=32] {'req','blk'}, dimensions={0} | all-to-all | bytes 8388608 | tf_op jit(solution)/shard_map/all_to_all | solution.py:214
  268.3 3.0 %fusion.15 = bf16[1,64,2048]{2,1,0:T(8,128)(2,1)} fusion(f32[64,2048]{1,0:T(8,128)S(1)} %get-tuple-element.22, f32[64,1024]{1,0:T(8,128)S(1)} %get-tuple-element.12, bf16[128,8,2048]{2,1,0:T(8,128)(2,1)S(1)} %all_to_all.25), kind=kOutput, calls=%fused_computation.16 | convolution fusion | flops 1610874880 | bytes 5242880 | tf_op jit(solution)/shard_map/dot_general | solution.py:215
  (9 shorter events, 0.2 us)
Async XLA Ops:
  6.5 67.7 %all-gather.2.cloned.1.call-start = ((), (), s32[]{:S(2)}) async-start(), calls=%async_computation.2 | async-start | bytes 6684672 | tf_op jit(solution)/shard_map/all_gather | solution.py:166
  7.6 2.5 collective-permute-start.1
  10.9 97.3 %collective-permute-start.3 = (bf16[1408,2048]{1,0:T(8,128)(2,1)}, bf16[1408,2048]{1,0:T(8,128)(2,1)}, u32[]{:S(2)}, u32[]{:S(2)}) collective-permute-start(bf16[1408,2048]{1,0:T(8,128)(2,1)} %bitcast.79), channel_id=1, source_target_pairs={{0,1},{1,0},{2,3},{3,2},{4,5},{5,4},{6,7},{7,6},{8,9},{9,8},{10,11... | collective-permute-start | bytes 17301512 | tf_op jit(solution)/shard_map/ppermute | solution.py:140
  11.4 96.9 %collective-permute-start.4 = (bf16[704,2048]{1,0:T(8,128)(2,1)}, bf16[704,2048]{1,0:T(8,128)(2,1)S(1)}, u32[]{:S(2)}, u32[]{:S(2)}) collective-permute-start(bf16[704,2048]{1,0:T(8,128)(2,1)} %bitcast.82), channel_id=1, source_target_pairs={{0,1},{1,0},{2,3},{3,2},{4,5},{5,4},{6,7},{7,6},{8,9},{9,8},{10,11... | collective-permute-start | bytes 8650760 | tf_op jit(solution)/shard_map/ppermute | solution.py:141
  12.5 12.4 %collective-permute-start = (bf16[64,1024]{1,0:T(8,128)(2,1)S(1)}, bf16[64,1024]{1,0:T(8,128)(2,1)S(1)}, u32[]{:S(2)}, u32[]{:S(2)}) collective-permute-start(bf16[64,1024]{1,0:T(8,128)(2,1)S(1)} %get-tuple-element.16), channel_id=1, source_target_pairs={{0,1},{1,0},{2,3},{3,2},{4,5},{5,4},{6,7},{7,6},{8,9},{9,8},{10,11... | collective-permute-start | bytes 393224 | tf_op jit(solution)/shard_map/ppermute | solution.py:161
  74.2 2.8 %copy-start = (bf16[32,192,512]{2,1,0:T(8,128)(2,1)S(1)}, bf16[32,192,512]{2,1,0:T(8,128)(2,1)}, u32[]{:S(2)}) copy-start(bf16[32,192,512]{2,1,0:T(8,128)(2,1)} %all-gather.2.cloned.1.call-done.k_ref.v_ref) | copy-start | bytes 18874372
  77.0 31.2 %copy-start.1 = (bf16[2048,2048]{1,0:T(8,128)(2,1)S(1)}, bf16[2048,2048]{1,0:T(8,128)(2,1)}, u32[]{:S(2)}) copy-start(bf16[2048,2048]{1,0:T(8,128)(2,1)} %param.20) | copy-start | bytes 25165828
  77.0 31.3 %copy-start.2 = (bf16[1,64,2048]{2,1,0:T(8,128)(2,1)S(1)}, bf16[1,64,2048]{2,1,0:T(8,128)(2,1)}, u32[]{:S(2)}) copy-start(bf16[1,64,2048]{2,1,0:T(8,128)(2,1)} %param.19) | copy-start | bytes 786436
  106.3 1.9 collective-permute-start.2
  108.2 1.8 copy-start.3
  110.0 77.1 %slice-start = ((s8[5767168]{0:T(1024)(128)(4,1)}), s8[4194304]{0:T(1024)(128)(4,1)S(1)}, s32[]{:S(2)}) async-start(s8[5767168]{0:T(1024)(128)(4,1)} %bitcast.80), calls=%async_computation.3 | async-start | bytes 8388608
  111.3 75.8 %slice-start.1 = ((s8[5767168]{0:T(1024)(128)(4,1)}), s8[1572864]{0:T(1024)(128)(4,1)S(1)}, s32[]{:S(2)}) async-start(s8[5767168]{0:T(1024)(128)(4,1)} %bitcast.80), calls=%async_computation.4 | async-start | bytes 3145728
  187.2 6.7 %copy-start.4 = (bf16[1,704,2048]{2,1,0:T(8,128)(2,1)S(1)}, bf16[1,704,2048]{2,1,0:T(8,128)(2,1)}, u32[]{:S(2)}) copy-start(bf16[1,704,2048]{2,1,0:T(8,128)(2,1)} %param.25) | copy-start | bytes 8650756
Sparse Core Ops, SparseCore 0:
  11.0 63.1 all-gather.1

commit v8 on v7

--- a/solution.py
+++ b/solution.py
@@ -15,7 +15,7 @@
 TOP = 6
 
 
-CHUNK = 256
+CHUNK = 1024
 
 
 def attn_kernel(s_ref, q_ref, k_ref, v_ref, o_ref):

time: 277 us -> 253 us (0.913)
  blocking collectives: 133 us -> 120 us
  Pallas kernels: 29.2 us -> 16.5 us
    pallas_call x1, Pallas kernels: 29.2 us -> 16.5 us  [attention(): pl.pallas_call(attn_kernel, out_shape=jax.ShapeDtypeStruct(queries.shape,...]
    all_to_all x1, blocking collectives: 75.8 us -> 63.5 us  [local(): lax.all_to_all(outgoing, ('req', 'blk'), split_axis=0, concat_axis=0, til...]
  transfers between devices with their start and end apart: 6 -> 6, of which waited for: 4 -> 4; matrix products, arithmetic and copies ran while one was open for 2% -> 2% of each run, Pallas kernels for 10% -> 7%
where the time goes in v8:
time: 253 us
  blocking collectives  120 us (47%)
  waiting for transfers between devices  58.9 us (23%)
  matrix products  30.3 us (12%)
  Pallas kernels  16.5 us (7%)
  between operations  14.3 us (6%)
  local copies, waits for them, and re-layouts  5.99 us (2%)
  other arithmetic  3.53 us (1%)
  starting transfers between devices  3.42 us (1%)
    all_to_all x1, blocking collectives, local(): lax.all_to_all(outgoing, ('req', 'blk'), split_axis=0, concat_axis=0, til...  63.5 us
    all_to_all x1, blocking collectives, local(): lax.all_to_all(both, ('req', 'blk'), split_axis=0, concat_axis=0, tiled=T...  56.9 us
    all_gather x1, waiting for transfers between devices, local(): lax.all_gather(chip_kv, 'blk', axis=0, tiled=True, axis_index_groups=same...  49.2 us
    pallas_call x1, Pallas kernels, attention(): pl.pallas_call(attn_kernel, out_shape=jax.ShapeDtypeStruct(queries.shape,...  16.5 us
    dot_general x2, matrix products, half_expert(): hidden = jnp.dot(arrived, gate_up.T, preferred_element_type=jnp.float32)  16.3 us
    ppermute x2, waiting for transfers between devices, local(): got_kv, got_q = lax.ppermute((kv_cols(1 - core), sent_q), 'blk', pairs)  8.99 us
    dot_general x2, matrix products, half_expert(): jnp.dot(activated, down_rows, preferred_element_type=jnp.float32)  7.94 us
  transfers between devices with their start and end apart: 6, of which 4 were waited for; matrix products, arithmetic and copies ran while one was open for 2% of the time, Pallas kernels for 7%

profile of v8, /device:TPU:1, one launch (start us, length us, event | category | flops | bytes accessed | tf_op | source)
XLA Modules:
  0.0 253.2 jit_solution(4026941621155603225)
XLA Ops:
  6.5 0.0 all-gather.2.cloned.1.call-start
  6.5 1.0 fusion.27
  7.6 1.5 collective-permute-start.1
  9.1 1.1 collective-permute-done.1
  10.1 0.8 maximum_select_fusion
  10.9 0.0 all-gather.2.cloned.1.call-update
  10.9 0.5 collective-permute-start.3
  11.4 0.1 collective-permute-start.4
  11.5 1.0 dynamic-slice_bitcast_fusion.1
  12.5 0.5 collective-permute-start
  13.0 0.8 copy.26
  13.7 0.1 eq.52
  13.9 0.1 eq.48
  14.0 0.9 reduce-window.6
  14.9 0.2 slice_reduce_fusion
  15.2 0.1 fusion.32
  15.3 0.1 reduce_sum.39
  16.2 0.7 copy.35
  16.9 0.1 copy.30
  16.9 0.1 pad_add_fusion.s_ref
  17.0 7.9 %collective-permute-done = bf16[64,1024]{1,0:T(8,128)(2,1)S(1)} collective-permute-done((bf16[64,1024]{1,0:T(8,128)(2,1)S(1)}, bf16[64,1024]{1,0:T(8,128)(2,1)S(1)}, u32[]{:S(2)}, u32[]{:S(2)}) %collective-permute-start) | collective-permute-done | bytes 131104 | tf_op jit(solution)/shard_map/ppermute | solution.py:161
  25.0 49.2 %all-gather.2.cloned.1.call-done.k_ref.v_ref = bf16[32,192,512]{2,1,0:T(8,128)(2,1)} async-done(((bf16[2,192,512]{2,1,0:T(8,128)(2,1)}), bf16[32,192,512]{2,1,0:T(8,128)(2,1)}) %all-gather.2.cloned.1.call-update) | async-done | bytes 6291472 | tf_op jit(solution)/shard_map/all_gather | solution.py:166
  74.2 0.0 copy-start
  74.2 2.8 %copy-done = bf16[32,192,512]{2,1,0:T(8,128)(2,1)S(1)} copy-done((bf16[32,192,512]{2,1,0:T(8,128)(2,1)S(1)}, bf16[32,192,512]{2,1,0:T(8,128)(2,1)}, u32[]{:S(2)}) %copy-start) | copy-done | bytes 6291480
  77.0 0.0 copy-start.1
  77.0 0.0 copy-start.2
  77.0 16.5 %shard_map.127 = bf16[128,1024]{1,0:T(8,128)(2,1)S(1)} custom-call(s32[3]{0:T(128)S(1)} %pad_add_fusion.s_ref, bf16[128,1024]{1,0:T(8,128)(2,1)S(1)} %maximum_select_fusion.1.q_ref, bf16[32,192,512]{2,1,0:T(8,128)(2,1)S(1)} %copy-done, bf16[32,192,512]{2,1,0:T(8,128)(2,1)S(1)} %copy-done), custom_call_target="tpu_custom_call" | custom-call | tf_op jit(solution)/shard_map/pallas_call | solution.py:93
  93.6 0.9 collective-permute-start.2
  94.5 0.4 convert_reduce_fusion
  94.9 0.6 collective-permute-done.2
  95.5 0.1 maximum_select_fusion.2
  95.6 0.0 copy-start.3
  95.6 0.0 collective-permute-done.4
  95.6 0.0 collective-permute-done.3
  95.6 0.0 copy-done.1
  95.6 0.0 copy-done.2
  95.7 1.7 multiply_reduce_fusion
  97.4 0.0 copy-done.3
  97.4 0.0 slice-start
  97.4 1.3 convert_bitcast_fusion
  98.7 0.0 slice-start.1
  98.7 63.5 %all_to_all.24 = bf16[128,8,2048]{2,1,0:T(8,128)(2,1)S(1)} all-to-all(bf16[128,8,2048]{2,1,0:T(8,128)(2,1)S(1)} %convert_bitcast_fusion), channel_id=1, replica_groups=mesh['req'=4,'blk'=32] {'req','blk'}, dimensions={0} | all-to-all | bytes 8388608 | tf_op jit(solution)/shard_map/all_to_all | solution.py:210
  162.2 0.0 slice-done
  162.2 0.0 slice-done.1
  162.2 0.0 copy-start.4
  162.2 6.7 %fusion.5 = f32[1024,1408]{1,0:T(8,128)S(1)} fusion(bf16[128,8,2048]{2,1,0:T(8,128)(2,1)S(1)} %all_to_all.24, bf16[1,1408,2048]{2,1,0:T(8,128)(2,1)S(1)} %bitcast.81), kind=kOutput, calls=%fused_computation.6 | convolution fusion | flops 5905580032 | bytes 15728640 | tf_op jit(solution)/shard_map/dot_general | solution.py:112
  168.9 0.0 copy-done.4
  168.9 3.9 %fusion.18 = bf16[1024,2048]{1,0:T(8,128)(2,1)S(1)} fusion(f32[1024,1408]{1,0:T(8,128)S(1)} %fusion.5, bf16[1,704,2048]{2,1,0:T(8,128)(2,1)S(1)} %copy-done.4), kind=kOutput, calls=%fused_computation.17 | convolution fusion | flops 2957115392 | bytes 13369344 | tf_op jit(solution)/shard_map/dot_general | solution.py:114
  172.9 9.6 %fusion.3 = f32[1024,1408]{1,0:T(8,128)S(1)} fusion(bf16[1408,2048]{1,0:T(8,128)(2,1)} %collective-permute-done.3, bf16[128,8,2048]{2,1,0:T(8,128)(2,1)S(1)} %all_to_all.24), kind=kOutput, calls=%fused_computation.4 | convolution fusion | flops 5905580032 | bytes 15728640 | tf_op jit(solution)/shard_map/dot_general | solution.py:112
  182.5 4.0 %fusion = bf16[128,8,2048]{2,1,0:T(8,128)(2,1)S(1)} fusion(bf16[1024,2048]{1,0:T(8,128)(2,1)S(1)} %fusion.18, bf16[704,2048]{1,0:T(8,128)(2,1)S(1)} %collective-permute-done.4, f32[1024,1408]{1,0:T(8,128)S(1)} %fusion.3), kind=kOutput, calls=%fused_computation.1 | convolution fusion | flops 2967601152 | bytes 17563648 | tf_op jit(solution)/shard_map/dot_general | solution.py:114
  186.5 56.9 %all_to_all.25 = bf16[128,8,2048]{2,1,0:T(8,128)(2,1)S(1)} all-to-all(bf16[128,8,2048]{2,1,0:T(8,128)(2,1)S(1)} %fusion), channel_id=1, replica_groups=mesh['req'=4,'blk'=32] {'req','blk'}, dimensions={0} | all-to-all | bytes 8388608 | tf_op jit(solution)/shard_map/all_to_all | solution.py:214
  243.4 3.0 %fusion.15 = bf16[1,64,2048]{2,1,0:T(8,128)(2,1)} fusion(f32[64,2048]{1,0:T(8,128)S(1)} %get-tuple-element.22, f32[64,1024]{1,0:T(8,128)S(1)} %get-tuple-element.12, bf16[128,8,2048]{2,1,0:T(8,128)(2,1)S(1)} %all_to_all.25), kind=kOutput, calls=%fused_computation.16 | convolution fusion | flops 1610874880 | bytes 5242880 | tf_op jit(solution)/shard_map/dot_general | solution.py:215
  (9 shorter events, 0.2 us)
Async XLA Ops:
  6.5 67.7 %all-gather.2.cloned.1.call-start = ((), (), s32[]{:S(2)}) async-start(), calls=%async_computation.2 | async-start | bytes 6684672 | tf_op jit(solution)/shard_map/all_gather | solution.py:166
  7.6 2.5 collective-permute-start.1
  10.9 84.7 %collective-permute-start.3 = (bf16[1408,2048]{1,0:T(8,128)(2,1)}, bf16[1408,2048]{1,0:T(8,128)(2,1)}, u32[]{:S(2)}, u32[]{:S(2)}) collective-permute-start(bf16[1408,2048]{1,0:T(8,128)(2,1)} %bitcast.79), channel_id=1, source_target_pairs={{0,1},{1,0},{2,3},{3,2},{4,5},{5,4},{6,7},{7,6},{8,9},{9,8},{10,11... | collective-permute-start | bytes 17301512 | tf_op jit(solution)/shard_map/ppermute | solution.py:140
  11.4 84.2 %collective-permute-start.4 = (bf16[704,2048]{1,0:T(8,128)(2,1)}, bf16[704,2048]{1,0:T(8,128)(2,1)S(1)}, u32[]{:S(2)}, u32[]{:S(2)}) collective-permute-start(bf16[704,2048]{1,0:T(8,128)(2,1)} %bitcast.82), channel_id=1, source_target_pairs={{0,1},{1,0},{2,3},{3,2},{4,5},{5,4},{6,7},{7,6},{8,9},{9,8},{10,11... | collective-permute-start | bytes 8650760 | tf_op jit(solution)/shard_map/ppermute | solution.py:141
  12.5 12.4 %collective-permute-start = (bf16[64,1024]{1,0:T(8,128)(2,1)S(1)}, bf16[64,1024]{1,0:T(8,128)(2,1)S(1)}, u32[]{:S(2)}, u32[]{:S(2)}) collective-permute-start(bf16[64,1024]{1,0:T(8,128)(2,1)S(1)} %get-tuple-element.16), channel_id=1, source_target_pairs={{0,1},{1,0},{2,3},{3,2},{4,5},{5,4},{6,7},{7,6},{8,9},{9,8},{10,11... | collective-permute-start | bytes 393224 | tf_op jit(solution)/shard_map/ppermute | solution.py:161
  74.2 2.8 %copy-start = (bf16[32,192,512]{2,1,0:T(8,128)(2,1)S(1)}, bf16[32,192,512]{2,1,0:T(8,128)(2,1)}, u32[]{:S(2)}) copy-start(bf16[32,192,512]{2,1,0:T(8,128)(2,1)} %all-gather.2.cloned.1.call-done.k_ref.v_ref) | copy-start | bytes 18874372
  77.0 18.6 %copy-start.1 = (bf16[2048,2048]{1,0:T(8,128)(2,1)S(1)}, bf16[2048,2048]{1,0:T(8,128)(2,1)}, u32[]{:S(2)}) copy-start(bf16[2048,2048]{1,0:T(8,128)(2,1)} %param.20) | copy-start | bytes 25165828
  77.0 18.6 %copy-start.2 = (bf16[1,64,2048]{2,1,0:T(8,128)(2,1)S(1)}, bf16[1,64,2048]{2,1,0:T(8,128)(2,1)}, u32[]{:S(2)}) copy-start(bf16[1,64,2048]{2,1,0:T(8,128)(2,1)} %param.19) | copy-start | bytes 786436
  93.6 1.9 collective-permute-start.2
  95.6 1.8 copy-start.3
  97.4 64.8 %slice-start = ((s8[5767168]{0:T(1024)(128)(4,1)}), s8[4194304]{0:T(1024)(128)(4,1)S(1)}, s32[]{:S(2)}) async-start(s8[5767168]{0:T(1024)(128)(4,1)} %bitcast.80), calls=%async_computation.3 | async-start | bytes 8388608
  98.7 63.5 %slice-start.1 = ((s8[5767168]{0:T(1024)(128)(4,1)}), s8[1572864]{0:T(1024)(128)(4,1)S(1)}, s32[]{:S(2)}) async-start(s8[5767168]{0:T(1024)(128)(4,1)} %bitcast.80), calls=%async_computation.4 | async-start | bytes 3145728
  162.2 6.7 %copy-start.4 = (bf16[1,704,2048]{2,1,0:T(8,128)(2,1)S(1)}, bf16[1,704,2048]{2,1,0:T(8,128)(2,1)}, u32[]{:S(2)}) copy-start(bf16[1,704,2048]{2,1,0:T(8,128)(2,1)} %param.25) | copy-start | bytes 8650756
Sparse Core Ops, SparseCore 0:
  11.0 63.1 all-gather.1

commit v9 on v8

--- a/solution.py
+++ b/solution.py
@@ -15,7 +15,7 @@
 TOP = 6
 
 
-CHUNK = 1024
+CHUNK = 2048
 
 
 def attn_kernel(s_ref, q_ref, k_ref, v_ref, o_ref):

time: 253 us -> 250 us (0.988)
  blocking collectives: 120 us -> 117 us
    all_to_all x1, blocking collectives: 63.5 us -> 60.1 us  [local(): lax.all_to_all(outgoing, ('req', 'blk'), split_axis=0, concat_axis=0, til...]
where the time goes in v9:
time: 250 us
  blocking collectives  117 us (47%)
  waiting for transfers between devices  58.9 us (24%)
  matrix products  30.3 us (12%)
  Pallas kernels  16.7 us (7%)
  between operations  14.3 us (6%)
  local copies, waits for them, and re-layouts  5.99 us (2%)
  other arithmetic  3.53 us (1%)
  starting transfers between devices  3.42 us (1%)
    all_to_all x1, blocking collectives, local(): lax.all_to_all(outgoing, ('req', 'blk'), split_axis=0, concat_axis=0, til...  60.1 us
    all_to_all x1, blocking collectives, local(): lax.all_to_all(both, ('req', 'blk'), split_axis=0, concat_axis=0, tiled=T...  56.9 us
    all_gather x1, waiting for transfers between devices, local(): lax.all_gather(chip_kv, 'blk', axis=0, tiled=True, axis_index_groups=same...  49.2 us
    pallas_call x1, Pallas kernels, attention(): pl.pallas_call(attn_kernel, out_shape=jax.ShapeDtypeStruct(queries.shape,...  16.7 us
    dot_general x2, matrix products, half_expert(): hidden = jnp.dot(arrived, gate_up.T, preferred_element_type=jnp.float32)  16.3 us
    ppermute x2, waiting for transfers between devices, local(): got_kv, got_q = lax.ppermute((kv_cols(1 - core), sent_q), 'blk', pairs)  8.99 us
    dot_general x2, matrix products, half_expert(): jnp.dot(activated, down_rows, preferred_element_type=jnp.float32)  7.94 us
  transfers between devices with their start and end apart: 6, of which 4 were waited for; matrix products, arithmetic and copies ran while one was open for 2% of the time, Pallas kernels for 7%

profile of v9, /device:TPU:1, one launch (start us, length us, event | category | flops | bytes accessed | tf_op | source)
XLA Modules:
  0.0 249.9 jit_solution(11224056603588635048)
XLA Ops:
  6.5 0.0 all-gather.2.cloned.1.call-start
  6.5 1.0 fusion.27
  7.6 1.5 collective-permute-start.1
  9.1 1.1 collective-permute-done.1
  10.1 0.8 maximum_select_fusion
  10.9 0.0 all-gather.2.cloned.1.call-update
  10.9 0.5 collective-permute-start.3
  11.4 0.1 collective-permute-start.4
  11.5 1.0 dynamic-slice_bitcast_fusion.1
  12.5 0.5 collective-permute-start
  13.0 0.8 copy.26
  13.7 0.1 eq.52
  13.9 0.1 eq.48
  14.0 0.9 reduce-window.6
  14.9 0.2 slice_reduce_fusion
  15.2 0.1 fusion.32
  15.3 0.1 reduce_sum.39
  16.2 0.7 copy.35
  16.9 0.1 copy.30
  16.9 0.1 pad_add_fusion.s_ref
  17.0 7.9 %collective-permute-done = bf16[64,1024]{1,0:T(8,128)(2,1)S(1)} collective-permute-done((bf16[64,1024]{1,0:T(8,128)(2,1)S(1)}, bf16[64,1024]{1,0:T(8,128)(2,1)S(1)}, u32[]{:S(2)}, u32[]{:S(2)}) %collective-permute-start) | collective-permute-done | bytes 131104 | tf_op jit(solution)/shard_map/ppermute | solution.py:161
  25.0 49.2 %all-gather.2.cloned.1.call-done.k_ref.v_ref = bf16[32,192,512]{2,1,0:T(8,128)(2,1)} async-done(((bf16[2,192,512]{2,1,0:T(8,128)(2,1)}), bf16[32,192,512]{2,1,0:T(8,128)(2,1)}) %all-gather.2.cloned.1.call-update) | async-done | bytes 6291472 | tf_op jit(solution)/shard_map/all_gather | solution.py:166
  74.2 0.0 copy-start
  74.2 2.8 %copy-done = bf16[32,192,512]{2,1,0:T(8,128)(2,1)S(1)} copy-done((bf16[32,192,512]{2,1,0:T(8,128)(2,1)S(1)}, bf16[32,192,512]{2,1,0:T(8,128)(2,1)}, u32[]{:S(2)}) %copy-start) | copy-done | bytes 6291480
  77.0 0.0 copy-start.1
  77.0 0.0 copy-start.2
  77.0 16.7 %shard_map.127 = bf16[128,1024]{1,0:T(8,128)(2,1)S(1)} custom-call(s32[3]{0:T(128)S(1)} %pad_add_fusion.s_ref, bf16[128,1024]{1,0:T(8,128)(2,1)S(1)} %maximum_select_fusion.1.q_ref, bf16[32,192,512]{2,1,0:T(8,128)(2,1)S(1)} %copy-done, bf16[32,192,512]{2,1,0:T(8,128)(2,1)S(1)} %copy-done), custom_call_target="tpu_custom_call" | custom-call | tf_op jit(solution)/shard_map/pallas_call | solution.py:93
  93.7 0.9 collective-permute-start.2
  94.7 0.4 convert_reduce_fusion
  95.0 0.6 collective-permute-done.2
  95.6 0.1 maximum_select_fusion.2
  95.7 0.0 copy-start.3
  95.7 0.0 collective-permute-done.4
  95.7 0.0 collective-permute-done.3
  95.8 0.0 copy-done.1
  95.8 0.0 copy-done.2
  95.8 1.7 multiply_reduce_fusion
  97.5 0.0 copy-done.3
  97.5 0.0 slice-start
  97.5 1.3 convert_bitcast_fusion
  98.8 0.0 slice-start.1
  98.8 60.1 %all_to_all.24 = bf16[128,8,2048]{2,1,0:T(8,128)(2,1)S(1)} all-to-all(bf16[128,8,2048]{2,1,0:T(8,128)(2,1)S(1)} %convert_bitcast_fusion), channel_id=1, replica_groups=mesh['req'=4,'blk'=32] {'req','blk'}, dimensions={0} | all-to-all | bytes 8388608 | tf_op jit(solution)/shard_map/all_to_all | solution.py:210
  158.9 0.0 slice-done
  158.9 0.0 slice-done.1
  158.9 0.0 copy-start.4
  158.9 6.7 %fusion.5 = f32[1024,1408]{1,0:T(8,128)S(1)} fusion(bf16[128,8,2048]{2,1,0:T(8,128)(2,1)S(1)} %all_to_all.24, bf16[1,1408,2048]{2,1,0:T(8,128)(2,1)S(1)} %bitcast.81), kind=kOutput, calls=%fused_computation.6 | convolution fusion | flops 5905580032 | bytes 15728640 | tf_op jit(solution)/shard_map/dot_general | solution.py:112
  165.6 0.0 copy-done.4
  165.6 3.9 %fusion.18 = bf16[1024,2048]{1,0:T(8,128)(2,1)S(1)} fusion(f32[1024,1408]{1,0:T(8,128)S(1)} %fusion.5, bf16[1,704,2048]{2,1,0:T(8,128)(2,1)S(1)} %copy-done.4), kind=kOutput, calls=%fused_computation.17 | convolution fusion | flops 2957115392 | bytes 13369344 | tf_op jit(solution)/shard_map/dot_general | solution.py:114
  169.6 9.6 %fusion.3 = f32[1024,1408]{1,0:T(8,128)S(1)} fusion(bf16[1408,2048]{1,0:T(8,128)(2,1)} %collective-permute-done.3, bf16[128,8,2048]{2,1,0:T(8,128)(2,1)S(1)} %all_to_all.24), kind=kOutput, calls=%fused_computation.4 | convolution fusion | flops 5905580032 | bytes 15728640 | tf_op jit(solution)/shard_map/dot_general | solution.py:112
  179.2 4.0 %fusion = bf16[128,8,2048]{2,1,0:T(8,128)(2,1)S(1)} fusion(bf16[1024,2048]{1,0:T(8,128)(2,1)S(1)} %fusion.18, bf16[704,2048]{1,0:T(8,128)(2,1)S(1)} %collective-permute-done.4, f32[1024,1408]{1,0:T(8,128)S(1)} %fusion.3), kind=kOutput, calls=%fused_computation.1 | convolution fusion | flops 2967601152 | bytes 17563648 | tf_op jit(solution)/shard_map/dot_general | solution.py:114
  183.2 56.9 %all_to_all.25 = bf16[128,8,2048]{2,1,0:T(8,128)(2,1)S(1)} all-to-all(bf16[128,8,2048]{2,1,0:T(8,128)(2,1)S(1)} %fusion), channel_id=1, replica_groups=mesh['req'=4,'blk'=32] {'req','blk'}, dimensions={0} | all-to-all | bytes 8388608 | tf_op jit(solution)/shard_map/all_to_all | solution.py:214
  240.0 3.0 %fusion.15 = bf16[1,64,2048]{2,1,0:T(8,128)(2,1)} fusion(f32[64,2048]{1,0:T(8,128)S(1)} %get-tuple-element.22, f32[64,1024]{1,0:T(8,128)S(1)} %get-tuple-element.12, bf16[128,8,2048]{2,1,0:T(8,128)(2,1)S(1)} %all_to_all.25), kind=kOutput, calls=%fused_computation.16 | convolution fusion | flops 1610874880 | bytes 5242880 | tf_op jit(solution)/shard_map/dot_general | solution.py:215
  (9 shorter events, 0.2 us)
Async XLA Ops:
  6.5 67.7 %all-gather.2.cloned.1.call-start = ((), (), s32[]{:S(2)}) async-start(), calls=%async_computation.2 | async-start | bytes 6684672 | tf_op jit(solution)/shard_map/all_gather | solution.py:166
  7.6 2.5 %collective-permute-start.1 = (bf16[192,512]{1,0:T(8,128)(2,1)S(1)}, bf16[192,512]{1,0:T(8,128)(2,1)S(1)}, u32[]{:S(2)}, u32[]{:S(2)}) collective-permute-start(bf16[192,512]{1,0:T(8,128)(2,1)S(1)} %pad_maximum_fusion), channel_id=1, source_target_pairs={{0,1},{1,0},{2,3},{3,2},{4,5},{5,4},{6,7},{7,6},{8,9},{9,8},{10,11... | collective-permute-start | bytes 589832 | tf_op jit(solution)/shard_map/ppermute | solution.py:161
  10.9 84.8 %collective-permute-start.3 = (bf16[1408,2048]{1,0:T(8,128)(2,1)}, bf16[1408,2048]{1,0:T(8,128)(2,1)}, u32[]{:S(2)}, u32[]{:S(2)}) collective-permute-start(bf16[1408,2048]{1,0:T(8,128)(2,1)} %bitcast.79), channel_id=1, source_target_pairs={{0,1},{1,0},{2,3},{3,2},{4,5},{5,4},{6,7},{7,6},{8,9},{9,8},{10,11... | collective-permute-start | bytes 17301512 | tf_op jit(solution)/shard_map/ppermute | solution.py:140
  11.4 84.4 %collective-permute-start.4 = (bf16[704,2048]{1,0:T(8,128)(2,1)}, bf16[704,2048]{1,0:T(8,128)(2,1)S(1)}, u32[]{:S(2)}, u32[]{:S(2)}) collective-permute-start(bf16[704,2048]{1,0:T(8,128)(2,1)} %bitcast.82), channel_id=1, source_target_pairs={{0,1},{1,0},{2,3},{3,2},{4,5},{5,4},{6,7},{7,6},{8,9},{9,8},{10,11... | collective-permute-start | bytes 8650760 | tf_op jit(solution)/shard_map/ppermute | solution.py:141
  12.5 12.4 %collective-permute-start = (bf16[64,1024]{1,0:T(8,128)(2,1)S(1)}, bf16[64,1024]{1,0:T(8,128)(2,1)S(1)}, u32[]{:S(2)}, u32[]{:S(2)}) collective-permute-start(bf16[64,1024]{1,0:T(8,128)(2,1)S(1)} %get-tuple-element.16), channel_id=1, source_target_pairs={{0,1},{1,0},{2,3},{3,2},{4,5},{5,4},{6,7},{7,6},{8,9},{9,8},{10,11... | collective-permute-start | bytes 393224 | tf_op jit(solution)/shard_map/ppermute | solution.py:161
  74.2 2.8 %copy-start = (bf16[32,192,512]{2,1,0:T(8,128)(2,1)S(1)}, bf16[32,192,512]{2,1,0:T(8,128)(2,1)}, u32[]{:S(2)}) copy-start(bf16[32,192,512]{2,1,0:T(8,128)(2,1)} %all-gather.2.cloned.1.call-done.k_ref.v_ref) | copy-start | bytes 18874372
  77.0 18.7 %copy-start.1 = (bf16[2048,2048]{1,0:T(8,128)(2,1)S(1)}, bf16[2048,2048]{1,0:T(8,128)(2,1)}, u32[]{:S(2)}) copy-start(bf16[2048,2048]{1,0:T(8,128)(2,1)} %param.20) | copy-start | bytes 25165828
  77.0 18.7 %copy-start.2 = (bf16[1,64,2048]{2,1,0:T(8,128)(2,1)S(1)}, bf16[1,64,2048]{2,1,0:T(8,128)(2,1)}, u32[]{:S(2)}) copy-start(bf16[1,64,2048]{2,1,0:T(8,128)(2,1)} %param.19) | copy-start | bytes 786436
  93.7 1.9 collective-permute-start.2
  95.7 1.8 copy-start.3
  97.5 61.4 %slice-start = ((s8[5767168]{0:T(1024)(128)(4,1)}), s8[4194304]{0:T(1024)(128)(4,1)S(1)}, s32[]{:S(2)}) async-start(s8[5767168]{0:T(1024)(128)(4,1)} %bitcast.80), calls=%async_computation.3 | async-start | bytes 8388608
  98.8 60.1 %slice-start.1 = ((s8[5767168]{0:T(1024)(128)(4,1)}), s8[1572864]{0:T(1024)(128)(4,1)S(1)}, s32[]{:S(2)}) async-start(s8[5767168]{0:T(1024)(128)(4,1)} %bitcast.80), calls=%async_computation.4 | async-start | bytes 3145728
  158.9 6.7 %copy-start.4 = (bf16[1,704,2048]{2,1,0:T(8,128)(2,1)S(1)}, bf16[1,704,2048]{2,1,0:T(8,128)(2,1)}, u32[]{:S(2)}) copy-start(bf16[1,704,2048]{2,1,0:T(8,128)(2,1)} %param.25) | copy-start | bytes 8650756
Sparse Core Ops, SparseCore 0:
  11.0 63.1 all-gather.1

commit v10 on v9

--- a/solution.py
+++ b/solution.py
@@ -23,7 +23,7 @@
     tok_rows = q_ref.shape[0]
     rows = tok_rows * group_size
     length = s_ref[0]
-    blk = s_ref[1] + pl.program_id(1)
+    blk = s_ref[1] // 2
     qb = q_ref[...]
     qs = jnp.concatenate([qb[:, r * HEAD_DIM:(r + 1) * HEAD_DIM] for r in range(group_size)], axis=0)
     qpos = blk * tok_rows + lax.broadcasted_iota(jnp.int32, (rows, 1), 0) % tok_rows
@@ -85,24 +85,24 @@
 SPAN_ROWS = 64
 
 
-def attention(scalars, queries, kv, tok_rows):
+def attention(scalars, queries, kv):
     groups = queries.shape[1] // (HEAD_DIM * HEADS // KV_HEADS)
-    halves = queries.shape[0] // tok_rows
     devs, per_dev, _ = kv.shape
     group_cols = HEAD_DIM * HEADS // KV_HEADS
+    chip_rows = queries.shape[0]
     return pl.pallas_call(
         attn_kernel,
         out_shape=jax.ShapeDtypeStruct(queries.shape, jnp.bfloat16),
-        grid=(groups, halves),
+        grid=(groups,),
         in_specs=[
             pl.BlockSpec(memory_space=pltpu.SMEM),
-            pl.BlockSpec((tok_rows, group_cols), lambda g, h: (h, g)),
-            pl.BlockSpec((devs, per_dev, HEAD_DIM), lambda g, h: (0, 0, g)),
-            pl.BlockSpec((devs, per_dev, HEAD_DIM), lambda g, h: (0, 0, groups + g)),
+            pl.BlockSpec((chip_rows, group_cols), lambda g: (0, g)),
+            pl.BlockSpec((devs, per_dev, HEAD_DIM), lambda g: (0, 0, g)),
+            pl.BlockSpec((devs, per_dev, HEAD_DIM), lambda g: (0, 0, groups + g)),
         ],
-        out_specs=pl.BlockSpec((tok_rows, group_cols), lambda g, h: (h, g)),
+        out_specs=pl.BlockSpec((chip_rows, group_cols), lambda g: (0, g)),
         compiler_params=pltpu.CompilerParams(
-            dimension_semantics=("arbitrary", "arbitrary"), vmem_limit_bytes=40 * 1024 * 1024
+            dimension_semantics=("arbitrary",), vmem_limit_bytes=48 * 1024 * 1024
         ),
     )(scalars, queries, kv, kv)
 
@@ -167,7 +167,7 @@
     scalars = jnp.stack(
         [length, (blk_index - core).astype(jnp.int32), jnp.int32(cache_len)]
     )
-    chip_out = attention(scalars, chip_q, kv, tok_rows)
+    chip_out = attention(scalars, chip_q, kv)
     own_out = lax.dynamic_slice_in_dim(chip_out, core * tok_rows, tok_rows, 0)
     sent_out = lax.dynamic_slice_in_dim(chip_out, (1 - core) * tok_rows, tok_rows, 0)
     got_out = lax.ppermute(sent_out, "blk", pairs)

time: 250 us -> 250 us (level)
  matrix products: 30.3 us -> 33.7 us
  local copies, waits for them, and re-layouts: 5.99 us -> 3.21 us
    dot_general x1, matrix products: 1.69 us -> 5.09 us  [local(): jnp.dot(attended, w_out, preferred_element_type=jnp.float32)]
    unnamed x16 -> x12, local copies, waits for them, and re-layouts: 4.28 us -> 1.49 us
  transfers between devices with their start and end apart: 6 -> 6, of which waited for: 4 -> 4; matrix products, arithmetic and copies ran while one was open for 2% -> 2% of each run, Pallas kernels for 7% -> 6%
where the time goes in v10:
time: 250 us; the launch traced here: 249 us
  blocking collectives  117 us (47%)
  waiting for transfers between devices  58.9 us (24%)
  matrix products  33.7 us (13%)
  Pallas kernels  15.7 us (6%)
  between operations  14.3 us (6%)
  starting transfers between devices  3.61 us (1%)
  other arithmetic  3.52 us (1%)
  local copies, waits for them, and re-layouts  3.21 us (1%)
    all_to_all x1, blocking collectives, local(): lax.all_to_all(outgoing, ('req', 'blk'), split_axis=0, concat_axis=0, til...  59.8 us
    all_to_all x1, blocking collectives, local(): lax.all_to_all(both, ('req', 'blk'), split_axis=0, concat_axis=0, tiled=T...  56.9 us
    all_gather x1, waiting for transfers between devices, local(): lax.all_gather(chip_kv, 'blk', axis=0, tiled=True, axis_index_groups=same...  49.2 us
    dot_general x2, matrix products, half_expert(): hidden = jnp.dot(arrived, gate_up.T, preferred_element_type=jnp.float32)  16.3 us
    pallas_call x1, Pallas kernels, attention(): pl.pallas_call(attn_kernel, out_shape=jax.ShapeDtypeStruct(queries.shape,...  15.7 us
    ppermute x2, waiting for transfers between devices, local(): got_kv, got_q = lax.ppermute((kv_cols(1 - core), sent_q), 'blk', pairs)  8.99 us
    dot_general x2, matrix products, half_expert(): jnp.dot(activated, down_rows, preferred_element_type=jnp.float32)  7.93 us
    dot_general x1, matrix products, local(): jnp.dot(attended, w_out, preferred_element_type=jnp.float32)  5.09 us
  transfers between devices with their start and end apart: 6, of which 4 were waited for; matrix products, arithmetic and copies ran while one was open for 2% of the time, Pallas kernels for 6%

profile of v10, /device:TPU:1, one launch (start us, length us, event | category | flops | bytes accessed | tf_op | source)
XLA Modules:
  0.0 249.4 jit_solution(14731263667434199880)
XLA Ops:
  6.5 0.0 all-gather.2.cloned.1.call-start
  6.5 1.0 fusion.27
  7.6 1.5 collective-permute-start.1
  9.1 1.1 collective-permute-done.1
  10.1 0.8 maximum_select_fusion
  10.9 0.0 all-gather.2.cloned.1.call-update
  10.9 0.5 collective-permute-start.3
  11.4 0.1 collective-permute-start.4
  11.5 1.0 dynamic-slice_bitcast_fusion.1
  12.5 0.5 collective-permute-start
  13.0 0.8 copy.26
  13.7 0.1 eq.52
  13.9 0.1 eq.48
  14.0 0.9 reduce-window.6
  14.9 0.2 slice_reduce_fusion
  15.2 0.1 fusion.32
  15.3 0.1 reduce_sum.39
  16.2 0.7 copy.35
  16.9 0.1 copy.30
  16.9 0.1 pad_add_fusion.s_ref
  17.0 7.9 %collective-permute-done = bf16[64,1024]{1,0:T(8,128)(2,1)S(1)} collective-permute-done((bf16[64,1024]{1,0:T(8,128)(2,1)S(1)}, bf16[64,1024]{1,0:T(8,128)(2,1)S(1)}, u32[]{:S(2)}, u32[]{:S(2)}) %collective-permute-start) | collective-permute-done | bytes 131104 | tf_op jit(solution)/shard_map/ppermute | solution.py:161
  25.0 0.0 copy-start
  25.0 49.2 %all-gather.2.cloned.1.call-done.k_ref.v_ref = bf16[32,192,512]{2,1,0:T(8,128)(2,1)} async-done(((bf16[2,192,512]{2,1,0:T(8,128)(2,1)}), bf16[32,192,512]{2,1,0:T(8,128)(2,1)}) %all-gather.2.cloned.1.call-update) | async-done | bytes 6291472 | tf_op jit(solution)/shard_map/all_gather | solution.py:166
  74.2 15.7 %shard_map.127 = bf16[128,1024]{1,0:T(8,128)(2,1)S(1)} custom-call(s32[3]{0:T(128)S(1)} %pad_add_fusion.s_ref, bf16[128,1024]{1,0:T(8,128)(2,1)S(1)} %maximum_select_fusion.1.q_ref, bf16[32,192,512]{2,1,0:T(8,128)(2,1)} %all-gather.2.cloned.1.call-done.k_ref.v_ref, bf16[32,192,512]{2,1,0:T(8,128)(2,1)} %all-gather.2.cloned.1.call-done.k_ref.v_ref), custom_call_target="tpu_custom_call" | custom-call | tf_op jit(solution)/shard_map/pallas_call | solution.py:93
  90.0 1.1 collective-permute-start.2
  91.1 0.4 convert_reduce_fusion
  91.5 0.6 collective-permute-done.2
  92.1 0.1 maximum_select_fusion.2
  92.1 0.0 copy-start.1
  92.2 0.0 collective-permute-done.4
  92.2 0.0 collective-permute-done.3
  92.2 0.0 copy-done
  92.2 5.1 %multiply_reduce_fusion = (f32[64]{0:T(128)S(1)}, f32[64,2048]{1,0:T(8,128)S(1)}) fusion(bf16[64,2048]{1,0:T(8,128)(2,1)S(1)} %maximum_select_fusion.2, bf16[2048,2048]{1,0:T(8,128)(2,1)} %param.20, bf16[1,64,2048]{2,1,0:T(8,128)(2,1)S(1)} %copy-done), kind=kOutput, calls=%fused_computation.24 | convolution fusion | flops 537395136 | bytes 9437440 | tf_op jit(solution)/shard_map/dot_general | solution.py:181
  97.3 0.0 copy-done.1
  97.3 0.0 slice-start
  97.3 1.3 convert_bitcast_fusion
  98.6 0.0 slice-start.1
  98.6 59.8 %all_to_all.24 = bf16[128,8,2048]{2,1,0:T(8,128)(2,1)S(1)} all-to-all(bf16[128,8,2048]{2,1,0:T(8,128)(2,1)S(1)} %convert_bitcast_fusion), channel_id=1, replica_groups=mesh['req'=4,'blk'=32] {'req','blk'}, dimensions={0} | all-to-all | bytes 8388608 | tf_op jit(solution)/shard_map/all_to_all | solution.py:210
  158.4 0.0 slice-done
  158.4 0.0 slice-done.1
  158.4 0.0 copy-start.2
  158.4 6.7 %fusion.5 = f32[1024,1408]{1,0:T(8,128)S(1)} fusion(bf16[128,8,2048]{2,1,0:T(8,128)(2,1)S(1)} %all_to_all.24, bf16[1,1408,2048]{2,1,0:T(8,128)(2,1)S(1)} %bitcast.81), kind=kOutput, calls=%fused_computation.6 | convolution fusion | flops 5905580032 | bytes 15728640 | tf_op jit(solution)/shard_map/dot_general | solution.py:112
  165.2 0.0 copy-done.2
  165.2 3.9 %fusion.18 = bf16[1024,2048]{1,0:T(8,128)(2,1)S(1)} fusion(f32[1024,1408]{1,0:T(8,128)S(1)} %fusion.5, bf16[1,704,2048]{2,1,0:T(8,128)(2,1)S(1)} %copy-done.2), kind=kOutput, calls=%fused_computation.17 | convolution fusion | flops 2957115392 | bytes 13369344 | tf_op jit(solution)/shard_map/dot_general | solution.py:114
  169.1 9.6 %fusion.3 = f32[1024,1408]{1,0:T(8,128)S(1)} fusion(bf16[1408,2048]{1,0:T(8,128)(2,1)} %collective-permute-done.3, bf16[128,8,2048]{2,1,0:T(8,128)(2,1)S(1)} %all_to_all.24), kind=kOutput, calls=%fused_computation.4 | convolution fusion | flops 5905580032 | bytes 15728640 | tf_op jit(solution)/shard_map/dot_general | solution.py:112
  178.7 4.0 %fusion = bf16[128,8,2048]{2,1,0:T(8,128)(2,1)S(1)} fusion(bf16[1024,2048]{1,0:T(8,128)(2,1)S(1)} %fusion.18, bf16[704,2048]{1,0:T(8,128)(2,1)S(1)} %collective-permute-done.4, f32[1024,1408]{1,0:T(8,128)S(1)} %fusion.3), kind=kOutput, calls=%fused_computation.1 | convolution fusion | flops 2967601152 | bytes 17563648 | tf_op jit(solution)/shard_map/dot_general | solution.py:114
  182.7 56.9 %all_to_all.25 = bf16[128,8,2048]{2,1,0:T(8,128)(2,1)S(1)} all-to-all(bf16[128,8,2048]{2,1,0:T(8,128)(2,1)S(1)} %fusion), channel_id=1, replica_groups=mesh['req'=4,'blk'=32] {'req','blk'}, dimensions={0} | all-to-all | bytes 8388608 | tf_op jit(solution)/shard_map/all_to_all | solution.py:214
  239.6 3.0 %fusion.15 = bf16[1,64,2048]{2,1,0:T(8,128)(2,1)} fusion(f32[64,2048]{1,0:T(8,128)S(1)} %get-tuple-element.22, f32[64,1024]{1,0:T(8,128)S(1)} %get-tuple-element.12, bf16[128,8,2048]{2,1,0:T(8,128)(2,1)S(1)} %all_to_all.25), kind=kOutput, calls=%fused_computation.16 | convolution fusion | flops 1610874880 | bytes 5242880 | tf_op jit(solution)/shard_map/dot_general | solution.py:215
  (9 shorter events, 0.2 us)
Async XLA Ops:
  6.5 67.7 %all-gather.2.cloned.1.call-start = ((), (), s32[]{:S(2)}) async-start(), calls=%async_computation.2 | async-start | bytes 6684672 | tf_op jit(solution)/shard_map/all_gather | solution.py:166
  7.6 2.5 %collective-permute-start.1 = (bf16[192,512]{1,0:T(8,128)(2,1)S(1)}, bf16[192,512]{1,0:T(8,128)(2,1)S(1)}, u32[]{:S(2)}, u32[]{:S(2)}) collective-permute-start(bf16[192,512]{1,0:T(8,128)(2,1)S(1)} %pad_maximum_fusion), channel_id=1, source_target_pairs={{0,1},{1,0},{2,3},{3,2},{4,5},{5,4},{6,7},{7,6},{8,9},{9,8},{10,11... | collective-permute-start | bytes 589832 | tf_op jit(solution)/shard_map/ppermute | solution.py:161
  10.9 81.2 %collective-permute-start.3 = (bf16[1408,2048]{1,0:T(8,128)(2,1)}, bf16[1408,2048]{1,0:T(8,128)(2,1)}, u32[]{:S(2)}, u32[]{:S(2)}) collective-permute-start(bf16[1408,2048]{1,0:T(8,128)(2,1)} %bitcast.79), channel_id=1, source_target_pairs={{0,1},{1,0},{2,3},{3,2},{4,5},{5,4},{6,7},{7,6},{8,9},{9,8},{10,11... | collective-permute-start | bytes 17301512 | tf_op jit(solution)/shard_map/ppermute | solution.py:140
  11.4 80.8 %collective-permute-start.4 = (bf16[704,2048]{1,0:T(8,128)(2,1)}, bf16[704,2048]{1,0:T(8,128)(2,1)S(1)}, u32[]{:S(2)}, u32[]{:S(2)}) collective-permute-start(bf16[704,2048]{1,0:T(8,128)(2,1)} %bitcast.82), channel_id=1, source_target_pairs={{0,1},{1,0},{2,3},{3,2},{4,5},{5,4},{6,7},{7,6},{8,9},{9,8},{10,11... | collective-permute-start | bytes 8650760 | tf_op jit(solution)/shard_map/ppermute | solution.py:141
  12.5 12.4 %collective-permute-start = (bf16[64,1024]{1,0:T(8,128)(2,1)S(1)}, bf16[64,1024]{1,0:T(8,128)(2,1)S(1)}, u32[]{:S(2)}, u32[]{:S(2)}) collective-permute-start(bf16[64,1024]{1,0:T(8,128)(2,1)S(1)} %get-tuple-element.16), channel_id=1, source_target_pairs={{0,1},{1,0},{2,3},{3,2},{4,5},{5,4},{6,7},{7,6},{8,9},{9,8},{10,11... | collective-permute-start | bytes 393224 | tf_op jit(solution)/shard_map/ppermute | solution.py:161
  25.0 67.2 %copy-start = (bf16[1,64,2048]{2,1,0:T(8,128)(2,1)S(1)}, bf16[1,64,2048]{2,1,0:T(8,128)(2,1)}, u32[]{:S(2)}) copy-start(bf16[1,64,2048]{2,1,0:T(8,128)(2,1)} %param.19) | copy-start | bytes 786436
  90.0 2.1 collective-permute-start.2
  92.1 5.1 %copy-start.1 = (f32[2048]{0:T(1024)S(1)}, f32[2048]{0:T(1024)}, u32[]{:S(2)}) copy-start(f32[2048]{0:T(1024)} %param.21) | copy-start | bytes 24580
  97.3 61.1 %slice-start = ((s8[5767168]{0:T(1024)(128)(4,1)}), s8[4194304]{0:T(1024)(128)(4,1)S(1)}, s32[]{:S(2)}) async-start(s8[5767168]{0:T(1024)(128)(4,1)} %bitcast.80), calls=%async_computation.3 | async-start | bytes 8388608
  98.6 59.8 %slice-start.1 = ((s8[5767168]{0:T(1024)(128)(4,1)}), s8[1572864]{0:T(1024)(128)(4,1)S(1)}, s32[]{:S(2)}) async-start(s8[5767168]{0:T(1024)(128)(4,1)} %bitcast.80), calls=%async_computation.4 | async-start | bytes 3145728
  158.4 6.7 %copy-start.2 = (bf16[1,704,2048]{2,1,0:T(8,128)(2,1)S(1)}, bf16[1,704,2048]{2,1,0:T(8,128)(2,1)}, u32[]{:S(2)}) copy-start(bf16[1,704,2048]{2,1,0:T(8,128)(2,1)} %param.25) | copy-start | bytes 8650756
Sparse Core Ops, SparseCore 0:
  11.0 63.1 all-gather.1

commit v11 on v9

--- a/solution.py
+++ b/solution.py
@@ -137,8 +137,6 @@
     span_len = span_keys.shape[1]
 
     pairs = [(b, b ^ 1) for b in range(blk_count)]
-    other_gate_up = lax.ppermute(w_gate_up[0], "blk", pairs)
-    other_down = lax.ppermute(w_down[0], "blk", pairs)
 
     core = blk_index % 2
     half_cols = KV_HEADS * HEAD_DIM // 2
@@ -164,6 +162,11 @@
     chip_q = jnp.where(first, jnp.concatenate([own_q, got_q], 0), jnp.concatenate([got_q, own_q], 0))
     same_core = [list(range(0, blk_count, 2)), list(range(1, blk_count, 2))]
     kv = lax.all_gather(chip_kv, "blk", axis=0, tiled=True, axis_index_groups=same_core)
+    kv, chip_q, own_gate_up, own_down = lax.optimization_barrier(
+        (kv, chip_q, w_gate_up[0], w_down[0])
+    )
+    other_gate_up = lax.ppermute(own_gate_up, "blk", pairs)
+    other_down = lax.ppermute(own_down, "blk", pairs)
     scalars = jnp.stack(
         [length, (blk_index - core).astype(jnp.int32), jnp.int32(cache_len)]
     )

time: 250 us -> 254 us (1.016)
  waiting for transfers between devices: 58.9 us -> 63.5 us
    all_gather x1, waiting for transfers between devices: 49.2 us -> 60.8 us  [local(): lax.all_gather(chip_kv, 'blk', axis=0, tiled=True, axis_index_groups=same...]
    ppermute x2, waiting for transfers between devices: 8.99 us -> 2.04 us  [local(): got_kv, got_q = lax.ppermute((kv_cols(1 - core), sent_q), 'blk', pairs)]
where the time goes in v11:
time: 254 us; the launch traced here: 253 us
  blocking collectives  115 us (45%)
  waiting for transfers between devices  63.5 us (25%)
  matrix products  30.2 us (12%)
  Pallas kernels  16.6 us (7%)
  between operations  14.3 us (6%)
  local copies, waits for them, and re-layouts  6.01 us (2%)
  other arithmetic  3.56 us (1%)
  starting transfers between devices  3.35 us (1%)
    all_gather x1, waiting for transfers between devices, local(): lax.all_gather(chip_kv, 'blk', axis=0, tiled=True, axis_index_groups=same...  60.8 us
    all_to_all x1, blocking collectives, local(): lax.all_to_all(outgoing, ('req', 'blk'), split_axis=0, concat_axis=0, til...  58.5 us
    all_to_all x1, blocking collectives, local(): lax.all_to_all(both, ('req', 'blk'), split_axis=0, concat_axis=0, tiled=T...  56.9 us
    pallas_call x1, Pallas kernels, attention(): pl.pallas_call(attn_kernel, out_shape=jax.ShapeDtypeStruct(queries.shape,...  16.6 us
    dot_general x2, matrix products, half_expert(): hidden = jnp.dot(arrived, gate_up.T, preferred_element_type=jnp.float32)  16.3 us
    dot_general x2, matrix products, half_expert(): jnp.dot(activated, down_rows, preferred_element_type=jnp.float32)  7.88 us
  transfers between devices with their start and end apart: 6, of which 4 were waited for; matrix products, arithmetic and copies ran while one was open for 2% of the time, Pallas kernels for 7%

profile of v11, /device:TPU:1, one launch (start us, length us, event | category | flops | bytes accessed | tf_op | source)
XLA Modules:
  0.0 252.8 jit_solution(1491989472938598687)
XLA Ops:
  6.5 0.0 all-gather.2.cloned.1.call-start
  6.5 1.0 fusion.27
  7.6 1.5 collective-permute-start
  9.1 1.1 collective-permute-done
  10.1 0.8 maximum_select_fusion
  10.9 0.0 all-gather.2.cloned.1.call-update
  11.0 1.0 dynamic-slice_bitcast_fusion.1
  12.0 0.5 collective-permute-start.1
  12.4 1.0 collective-permute-done.1
  13.5 60.8 %all-gather.2.cloned.1.call-done.k_ref.v_ref = bf16[32,192,512]{2,1,0:T(8,128)(2,1)} async-done(((bf16[2,192,512]{2,1,0:T(8,128)(2,1)}), bf16[32,192,512]{2,1,0:T(8,128)(2,1)}) %all-gather.2.cloned.1.call-update) | async-done | bytes 6291472 | tf_op jit(solution)/shard_map/all_gather | solution.py:164
  74.3 0.8 collective-permute-start.3
  75.1 0.0 collective-permute-start.4
  75.1 0.8 copy.26
  75.9 0.1 eq.52
  76.0 0.1 eq.48
  76.8 0.7 copy.35
  77.5 0.9 reduce-window.6
  78.4 0.2 slice_reduce_fusion
  78.7 0.1 fusion.32
  78.8 0.1 reduce_sum.39
  79.0 0.1 copy.30
  79.1 0.1 pad_add_fusion.s_ref
  79.2 0.0 copy-start
  79.2 2.8 %copy-done = bf16[32,192,512]{2,1,0:T(8,128)(2,1)S(1)} copy-done((bf16[32,192,512]{2,1,0:T(8,128)(2,1)S(1)}, bf16[32,192,512]{2,1,0:T(8,128)(2,1)}, u32[]{:S(2)}) %copy-start) | copy-done | bytes 6291480
  82.0 0.0 copy-start.1
  82.0 0.0 copy-start.2
  82.0 16.6 %shard_map.127 = bf16[128,1024]{1,0:T(8,128)(2,1)S(1)} custom-call(s32[3]{0:T(128)S(1)} %pad_add_fusion.s_ref, bf16[128,1024]{1,0:T(8,128)(2,1)S(1)} %maximum_select_fusion.1.q_ref, bf16[32,192,512]{2,1,0:T(8,128)(2,1)S(1)} %copy-done, bf16[32,192,512]{2,1,0:T(8,128)(2,1)S(1)} %copy-done), custom_call_target="tpu_custom_call" | custom-call | tf_op jit(solution)/shard_map/pallas_call | solution.py:93
  98.6 0.6 collective-permute-start.2
  99.2 0.4 convert_reduce_fusion
  99.6 0.6 collective-permute-done.2
  100.2 0.1 maximum_select_fusion.2
  100.3 0.0 copy-start.3
  100.3 0.0 collective-permute-done.4
  100.3 0.0 collective-permute-done.3
  100.3 0.0 copy-done.1
  100.4 0.0 copy-done.2
  100.4 1.7 multiply_reduce_fusion
  102.1 0.0 copy-done.3
  102.1 0.0 slice-start
  102.1 1.3 convert_bitcast_fusion
  103.4 0.0 slice-start.1
  103.4 58.5 %all_to_all.24 = bf16[128,8,2048]{2,1,0:T(8,128)(2,1)S(1)} all-to-all(bf16[128,8,2048]{2,1,0:T(8,128)(2,1)S(1)} %convert_bitcast_fusion), channel_id=1, replica_groups=mesh['req'=4,'blk'=32] {'req','blk'}, dimensions={0} | all-to-all | bytes 8388608 | tf_op jit(solution)/shard_map/all_to_all | solution.py:213
  161.9 0.0 slice-done
  161.9 0.0 slice-done.1
  161.9 0.0 copy-start.4
  161.9 6.7 %fusion.5 = f32[1024,1408]{1,0:T(8,128)S(1)} fusion(bf16[128,8,2048]{2,1,0:T(8,128)(2,1)S(1)} %all_to_all.24, bf16[1,1408,2048]{2,1,0:T(8,128)(2,1)S(1)} %bitcast.81), kind=kOutput, calls=%fused_computation.6 | convolution fusion | flops 5905580032 | bytes 15728640 | tf_op jit(solution)/shard_map/dot_general | solution.py:112
  168.6 0.0 copy-done.4
  168.6 3.9 %fusion.18 = bf16[1024,2048]{1,0:T(8,128)(2,1)S(1)} fusion(f32[1024,1408]{1,0:T(8,128)S(1)} %fusion.5, bf16[1,704,2048]{2,1,0:T(8,128)(2,1)S(1)} %copy-done.4), kind=kOutput, calls=%fused_computation.17 | convolution fusion | flops 2957115392 | bytes 13369344 | tf_op jit(solution)/shard_map/dot_general | solution.py:114
  172.5 9.6 %fusion.3 = f32[1024,1408]{1,0:T(8,128)S(1)} fusion(bf16[1408,2048]{1,0:T(8,128)(2,1)} %collective-permute-done.3, bf16[128,8,2048]{2,1,0:T(8,128)(2,1)S(1)} %all_to_all.24), kind=kOutput, calls=%fused_computation.4 | convolution fusion | flops 5905580032 | bytes 15728640 | tf_op jit(solution)/shard_map/dot_general | solution.py:112
  182.1 4.0 %fusion = bf16[128,8,2048]{2,1,0:T(8,128)(2,1)S(1)} fusion(bf16[1024,2048]{1,0:T(8,128)(2,1)S(1)} %fusion.18, bf16[704,2048]{1,0:T(8,128)(2,1)S(1)} %collective-permute-done.4, f32[1024,1408]{1,0:T(8,128)S(1)} %fusion.3), kind=kOutput, calls=%fused_computation.1 | convolution fusion | flops 2967601152 | bytes 17563648 | tf_op jit(solution)/shard_map/dot_general | solution.py:114
  186.1 56.9 %all_to_all.25 = bf16[128,8,2048]{2,1,0:T(8,128)(2,1)S(1)} all-to-all(bf16[128,8,2048]{2,1,0:T(8,128)(2,1)S(1)} %fusion), channel_id=1, replica_groups=mesh['req'=4,'blk'=32] {'req','blk'}, dimensions={0} | all-to-all | bytes 8388608 | tf_op jit(solution)/shard_map/all_to_all | solution.py:217
  243.0 3.0 %fusion.15 = bf16[1,64,2048]{2,1,0:T(8,128)(2,1)} fusion(f32[64,2048]{1,0:T(8,128)S(1)} %get-tuple-element.30, f32[64,1024]{1,0:T(8,128)S(1)} %get-tuple-element.20, bf16[128,8,2048]{2,1,0:T(8,128)(2,1)S(1)} %all_to_all.25), kind=kOutput, calls=%fused_computation.16 | convolution fusion | flops 1610874880 | bytes 5242880 | tf_op jit(solution)/shard_map/dot_general | solution.py:218
  (9 shorter events, 0.2 us)
Async XLA Ops:
  6.5 67.7 %all-gather.2.cloned.1.call-start = ((), (), s32[]{:S(2)}) async-start(), calls=%async_computation.2 | async-start | bytes 6684672 | tf_op jit(solution)/shard_map/all_gather | solution.py:164
  7.6 2.5 %collective-permute-start = (bf16[192,512]{1,0:T(8,128)(2,1)S(1)}, bf16[192,512]{1,0:T(8,128)(2,1)S(1)}, u32[]{:S(2)}, u32[]{:S(2)}) collective-permute-start(bf16[192,512]{1,0:T(8,128)(2,1)S(1)} %pad_maximum_fusion), channel_id=1, source_target_pairs={{0,1},{1,0},{2,3},{3,2},{4,5},{5,4},{6,7},{7,6},{8,9},{9,8},{10,11... | collective-permute-start | bytes 589832 | tf_op jit(solution)/shard_map/ppermute | solution.py:159
  12.0 1.4 collective-permute-start.1
  74.3 26.1 %collective-permute-start.3 = (bf16[1408,2048]{1,0:T(8,128)(2,1)}, bf16[1408,2048]{1,0:T(8,128)(2,1)}, u32[]{:S(2)}, u32[]{:S(2)}) collective-permute-start(bf16[1408,2048]{1,0:T(8,128)(2,1)} %bitcast.79), channel_id=1, source_target_pairs={{0,1},{1,0},{2,3},{3,2},{4,5},{5,4},{6,7},{7,6},{8,9},{9,8},{10,11... | collective-permute-start | bytes 17301512 | tf_op jit(solution)/shard_map/ppermute | solution.py:168
  75.1 25.2 %collective-permute-start.4 = (bf16[704,2048]{1,0:T(8,128)(2,1)}, bf16[704,2048]{1,0:T(8,128)(2,1)S(1)}, u32[]{:S(2)}, u32[]{:S(2)}) collective-permute-start(bf16[704,2048]{1,0:T(8,128)(2,1)} %bitcast.82), channel_id=1, source_target_pairs={{0,1},{1,0},{2,3},{3,2},{4,5},{5,4},{6,7},{7,6},{8,9},{9,8},{10,11... | collective-permute-start | bytes 8650760 | tf_op jit(solution)/shard_map/ppermute | solution.py:169
  79.2 2.8 %copy-start = (bf16[32,192,512]{2,1,0:T(8,128)(2,1)S(1)}, bf16[32,192,512]{2,1,0:T(8,128)(2,1)}, u32[]{:S(2)}) copy-start(bf16[32,192,512]{2,1,0:T(8,128)(2,1)} %all-gather.2.cloned.1.call-done.k_ref.v_ref) | copy-start | bytes 18874372
  82.0 18.4 %copy-start.1 = (bf16[2048,2048]{1,0:T(8,128)(2,1)S(1)}, bf16[2048,2048]{1,0:T(8,128)(2,1)}, u32[]{:S(2)}) copy-start(bf16[2048,2048]{1,0:T(8,128)(2,1)} %param.20) | copy-start | bytes 25165828
  82.0 18.4 %copy-start.2 = (bf16[1,64,2048]{2,1,0:T(8,128)(2,1)S(1)}, bf16[1,64,2048]{2,1,0:T(8,128)(2,1)}, u32[]{:S(2)}) copy-start(bf16[1,64,2048]{2,1,0:T(8,128)(2,1)} %param.19) | copy-start | bytes 786436
  98.6 1.6 collective-permute-start.2
  100.3 1.8 copy-start.3
  102.1 59.8 %slice-start = ((s8[5767168]{0:T(1024)(128)(4,1)}), s8[4194304]{0:T(1024)(128)(4,1)S(1)}, s32[]{:S(2)}) async-start(s8[5767168]{0:T(1024)(128)(4,1)} %bitcast.80), calls=%async_computation.3 | async-start | bytes 8388608
  103.4 58.5 %slice-start.1 = ((s8[5767168]{0:T(1024)(128)(4,1)}), s8[1572864]{0:T(1024)(128)(4,1)S(1)}, s32[]{:S(2)}) async-start(s8[5767168]{0:T(1024)(128)(4,1)} %bitcast.80), calls=%async_computation.4 | async-start | bytes 3145728
  161.9 6.7 %copy-start.4 = (bf16[1,704,2048]{2,1,0:T(8,128)(2,1)S(1)}, bf16[1,704,2048]{2,1,0:T(8,128)(2,1)}, u32[]{:S(2)}) copy-start(bf16[1,704,2048]{2,1,0:T(8,128)(2,1)} %param.25) | copy-start | bytes 8650756
Sparse Core Ops, SparseCore 0:
  11.1 63.1 all-gather.1

commit v12 on v9

--- a/solution.py
+++ b/solution.py
@@ -212,11 +212,10 @@
     other = half_expert(arrived, other_gate_up, other_down)
     both = (mine.astype(jnp.float32) + other.astype(jnp.float32)).astype(jnp.bfloat16)
     returned = lax.all_to_all(both, ("req", "blk"), split_axis=0, concat_axis=0, tiled=True)
-    expert_sum = jnp.dot(
-        combine_weights,
-        returned.astype(jnp.float32),
-        precision=lax.Precision.HIGHEST,
-        preferred_element_type=jnp.float32,
+    weights_hi = combine_weights.astype(jnp.bfloat16)
+    weights_lo = (combine_weights - weights_hi.astype(jnp.float32)).astype(jnp.bfloat16)
+    expert_sum = jnp.dot(weights_hi, returned, preferred_element_type=jnp.float32) + jnp.dot(
+        weights_lo, returned, preferred_element_type=jnp.float32
     )
     return (residual + expert_sum).astype(jnp.bfloat16)[None]
 

time: 250 us -> 250 us (level)
  blocking collectives: 117 us -> 122 us
  Pallas kernels: 16.7 us -> 12.1 us
    all_to_all x1, blocking collectives: 60.1 us -> 64.7 us  [local(): lax.all_to_all(outgoing, ('req', 'blk'), split_axis=0, concat_axis=0, til...]
    pallas_call x1, Pallas kernels: 16.7 us -> 12.1 us  [attention(): pl.pallas_call(attn_kernel, out_shape=jax.ShapeDtypeStruct(queries.shape,...]
  transfers between devices with their start and end apart: 6 -> 6, of which waited for: 4 -> 4; matrix products, arithmetic and copies ran while one was open for 2% -> 2% of each run, Pallas kernels for 7% -> 5%
where the time goes in v12:
time: 250 us; the launch traced here: 249 us
  blocking collectives  122 us (49%)
  waiting for transfers between devices  58.9 us (24%)
  matrix products  29.7 us (12%)
  between operations  14.3 us (6%)
  Pallas kernels  12.1 us (5%)
  local copies, waits for them, and re-layouts  5.99 us (2%)
  other arithmetic  3.53 us (1%)
  starting transfers between devices  3.42 us (1%)
    all_to_all x1, blocking collectives, local(): lax.all_to_all(outgoing, ('req', 'blk'), split_axis=0, concat_axis=0, til...  64.7 us
    all_to_all x1, blocking collectives, local(): lax.all_to_all(both, ('req', 'blk'), split_axis=0, concat_axis=0, tiled=T...  56.8 us
    all_gather x1, waiting for transfers between devices, local(): lax.all_gather(chip_kv, 'blk', axis=0, tiled=True, axis_index_groups=same...  49.2 us
    dot_general x2, matrix products, half_expert(): hidden = jnp.dot(arrived, gate_up.T, preferred_element_type=jnp.float32)  16.3 us
    pallas_call x1, Pallas kernels, attention(): pl.pallas_call(attn_kernel, out_shape=jax.ShapeDtypeStruct(queries.shape,...  12.1 us
    ppermute x2, waiting for transfers between devices, local(): got_kv, got_q = lax.ppermute((kv_cols(1 - core), sent_q), 'blk', pairs)  8.99 us
    dot_general x2, matrix products, half_expert(): jnp.dot(activated, down_rows, preferred_element_type=jnp.float32)  7.93 us
  transfers between devices with their start and end apart: 6, of which 4 were waited for; matrix products, arithmetic and copies ran while one was open for 2% of the time, Pallas kernels for 5%

profile of v12, /device:TPU:1, one launch (start us, length us, event | category | flops | bytes accessed | tf_op | source)
XLA Modules:
  0.0 249.5 jit_solution(9615858111813551253)
XLA Ops:
  6.5 0.0 all-gather.2.cloned.1.call-start
  6.5 1.0 fusion.32
  7.6 1.5 collective-permute-start.1
  9.1 1.1 collective-permute-done.1
  10.1 0.8 maximum_select_fusion
  10.9 0.0 all-gather.2.cloned.1.call-update
  10.9 0.5 collective-permute-start.3
  11.4 0.1 collective-permute-start.4
  11.5 1.0 dynamic-slice_bitcast_fusion.1
  12.5 0.5 collective-permute-start
  13.0 0.8 copy.26
  13.7 0.1 eq.52
  13.9 0.1 eq.48
  14.0 0.9 reduce-window.6
  14.9 0.2 slice_reduce_fusion
  15.2 0.1 fusion.37
  15.3 0.1 reduce_sum.39
  16.2 0.7 copy.35
  16.9 0.1 copy.30
  16.9 0.1 pad_add_fusion.s_ref
  17.0 7.9 %collective-permute-done = bf16[64,1024]{1,0:T(8,128)(2,1)S(1)} collective-permute-done((bf16[64,1024]{1,0:T(8,128)(2,1)S(1)}, bf16[64,1024]{1,0:T(8,128)(2,1)S(1)}, u32[]{:S(2)}, u32[]{:S(2)}) %collective-permute-start) | collective-permute-done | bytes 131104 | tf_op jit(solution)/shard_map/ppermute | solution.py:161
  25.0 49.2 %all-gather.2.cloned.1.call-done.k_ref.v_ref = bf16[32,192,512]{2,1,0:T(8,128)(2,1)} async-done(((bf16[2,192,512]{2,1,0:T(8,128)(2,1)}), bf16[32,192,512]{2,1,0:T(8,128)(2,1)}) %all-gather.2.cloned.1.call-update) | async-done | bytes 6291472 | tf_op jit(solution)/shard_map/all_gather | solution.py:166
  74.2 0.0 copy-start
  74.2 2.8 %copy-done = bf16[32,192,512]{2,1,0:T(8,128)(2,1)S(1)} copy-done((bf16[32,192,512]{2,1,0:T(8,128)(2,1)S(1)}, bf16[32,192,512]{2,1,0:T(8,128)(2,1)}, u32[]{:S(2)}) %copy-start) | copy-done | bytes 6291480
  77.0 0.0 copy-start.1
  77.0 0.0 copy-start.2
  77.0 12.1 %shard_map.127 = bf16[128,1024]{1,0:T(8,128)(2,1)S(1)} custom-call(s32[3]{0:T(128)S(1)} %pad_add_fusion.s_ref, bf16[128,1024]{1,0:T(8,128)(2,1)S(1)} %maximum_select_fusion.1.q_ref, bf16[32,192,512]{2,1,0:T(8,128)(2,1)S(1)} %copy-done, bf16[32,192,512]{2,1,0:T(8,128)(2,1)S(1)} %copy-done), custom_call_target="tpu_custom_call" | custom-call | tf_op jit(solution)/shard_map/pallas_call | solution.py:93
  89.2 0.9 collective-permute-start.2
  90.1 0.4 select_reduce_fusion
  90.5 0.6 collective-permute-done.2
  91.1 0.1 maximum_select_fusion.2
  91.2 0.0 copy-start.3
  91.2 0.0 collective-permute-done.4
  91.2 0.0 collective-permute-done.3
  91.2 0.0 copy-done.1
  91.2 0.0 copy-done.2
  91.2 1.7 multiply_reduce_fusion
  92.9 0.0 copy-done.3
  93.0 0.0 slice-start
  93.0 1.3 convert_bitcast_fusion
  94.3 0.0 slice-start.1
  94.3 64.7 %all_to_all.24 = bf16[128,8,2048]{2,1,0:T(8,128)(2,1)S(1)} all-to-all(bf16[128,8,2048]{2,1,0:T(8,128)(2,1)S(1)} %convert_bitcast_fusion), channel_id=1, replica_groups=mesh['req'=4,'blk'=32] {'req','blk'}, dimensions={0} | all-to-all | bytes 8388608 | tf_op jit(solution)/shard_map/all_to_all | solution.py:210
  159.0 0.0 slice-done
  159.0 0.0 slice-done.1
  159.1 0.0 copy-start.4
  159.1 6.7 %fusion.7 = f32[1024,1408]{1,0:T(8,128)S(1)} fusion(bf16[128,8,2048]{2,1,0:T(8,128)(2,1)S(1)} %all_to_all.24, bf16[1,1408,2048]{2,1,0:T(8,128)(2,1)S(1)} %bitcast.84), kind=kOutput, calls=%fused_computation.8 | convolution fusion | flops 5905580032 | bytes 15728640 | tf_op jit(solution)/shard_map/dot_general | solution.py:112
  165.8 0.0 copy-done.4
  165.8 3.9 %fusion.23 = bf16[1024,2048]{1,0:T(8,128)(2,1)S(1)} fusion(f32[1024,1408]{1,0:T(8,128)S(1)} %fusion.7, bf16[1,704,2048]{2,1,0:T(8,128)(2,1)S(1)} %copy-done.4), kind=kOutput, calls=%fused_computation.20 | convolution fusion | flops 2957115392 | bytes 13369344 | tf_op jit(solution)/shard_map/dot_general | solution.py:114
  169.7 9.6 %fusion.5 = f32[1024,1408]{1,0:T(8,128)S(1)} fusion(bf16[1408,2048]{1,0:T(8,128)(2,1)} %collective-permute-done.3, bf16[128,8,2048]{2,1,0:T(8,128)(2,1)S(1)} %all_to_all.24), kind=kOutput, calls=%fused_computation.6 | convolution fusion | flops 5905580032 | bytes 15728640 | tf_op jit(solution)/shard_map/dot_general | solution.py:112
  179.3 4.0 %fusion = bf16[128,8,2048]{2,1,0:T(8,128)(2,1)S(1)} fusion(bf16[1024,2048]{1,0:T(8,128)(2,1)S(1)} %fusion.23, bf16[704,2048]{1,0:T(8,128)(2,1)S(1)} %collective-permute-done.4, f32[1024,1408]{1,0:T(8,128)S(1)} %fusion.5), kind=kOutput, calls=%fused_computation.1 | convolution fusion | flops 2967601152 | bytes 17563648 | tf_op jit(solution)/shard_map/dot_general | solution.py:114
  183.3 56.8 %all_to_all.25 = bf16[128,8,2048]{2,1,0:T(8,128)(2,1)S(1)} all-to-all(bf16[128,8,2048]{2,1,0:T(8,128)(2,1)S(1)} %fusion), channel_id=1, replica_groups=mesh['req'=4,'blk'=32] {'req','blk'}, dimensions={0} | all-to-all | bytes 8388608 | tf_op jit(solution)/shard_map/all_to_all | solution.py:214
  240.2 0.8 fusion.1
  241.0 1.6 fusion.20
  (9 shorter events, 0.2 us)
Async XLA Ops:
  6.5 67.7 %all-gather.2.cloned.1.call-start = ((), (), s32[]{:S(2)}) async-start(), calls=%async_computation.2 | async-start | bytes 6684672 | tf_op jit(solution)/shard_map/all_gather | solution.py:166
  7.6 2.5 %collective-permute-start.1 = (bf16[192,512]{1,0:T(8,128)(2,1)S(1)}, bf16[192,512]{1,0:T(8,128)(2,1)S(1)}, u32[]{:S(2)}, u32[]{:S(2)}) collective-permute-start(bf16[192,512]{1,0:T(8,128)(2,1)S(1)} %pad_maximum_fusion), channel_id=1, source_target_pairs={{0,1},{1,0},{2,3},{3,2},{4,5},{5,4},{6,7},{7,6},{8,9},{9,8},{10,11... | collective-permute-start | bytes 589832 | tf_op jit(solution)/shard_map/ppermute | solution.py:161
  10.9 80.3 %collective-permute-start.3 = (bf16[1408,2048]{1,0:T(8,128)(2,1)}, bf16[1408,2048]{1,0:T(8,128)(2,1)}, u32[]{:S(2)}, u32[]{:S(2)}) collective-permute-start(bf16[1408,2048]{1,0:T(8,128)(2,1)} %bitcast.82), channel_id=1, source_target_pairs={{0,1},{1,0},{2,3},{3,2},{4,5},{5,4},{6,7},{7,6},{8,9},{9,8},{10,11... | collective-permute-start | bytes 17301512 | tf_op jit(solution)/shard_map/ppermute | solution.py:140
  11.4 79.8 %collective-permute-start.4 = (bf16[704,2048]{1,0:T(8,128)(2,1)}, bf16[704,2048]{1,0:T(8,128)(2,1)S(1)}, u32[]{:S(2)}, u32[]{:S(2)}) collective-permute-start(bf16[704,2048]{1,0:T(8,128)(2,1)} %bitcast.85), channel_id=1, source_target_pairs={{0,1},{1,0},{2,3},{3,2},{4,5},{5,4},{6,7},{7,6},{8,9},{9,8},{10,11... | collective-permute-start | bytes 8650760 | tf_op jit(solution)/shard_map/ppermute | solution.py:141
  12.5 12.4 %collective-permute-start = (bf16[64,1024]{1,0:T(8,128)(2,1)S(1)}, bf16[64,1024]{1,0:T(8,128)(2,1)S(1)}, u32[]{:S(2)}, u32[]{:S(2)}) collective-permute-start(bf16[64,1024]{1,0:T(8,128)(2,1)S(1)} %get-tuple-element.16), channel_id=1, source_target_pairs={{0,1},{1,0},{2,3},{3,2},{4,5},{5,4},{6,7},{7,6},{8,9},{9,8},{10,11... | collective-permute-start | bytes 393224 | tf_op jit(solution)/shard_map/ppermute | solution.py:161
  74.2 2.8 %copy-start = (bf16[32,192,512]{2,1,0:T(8,128)(2,1)S(1)}, bf16[32,192,512]{2,1,0:T(8,128)(2,1)}, u32[]{:S(2)}) copy-start(bf16[32,192,512]{2,1,0:T(8,128)(2,1)} %all-gather.2.cloned.1.call-done.k_ref.v_ref) | copy-start | bytes 18874372
  77.0 14.2 %copy-start.1 = (bf16[2048,2048]{1,0:T(8,128)(2,1)S(1)}, bf16[2048,2048]{1,0:T(8,128)(2,1)}, u32[]{:S(2)}) copy-start(bf16[2048,2048]{1,0:T(8,128)(2,1)} %param.20) | copy-start | bytes 25165828
  77.0 14.2 %copy-start.2 = (bf16[1,64,2048]{2,1,0:T(8,128)(2,1)S(1)}, bf16[1,64,2048]{2,1,0:T(8,128)(2,1)}, u32[]{:S(2)}) copy-start(bf16[1,64,2048]{2,1,0:T(8,128)(2,1)} %param.19) | copy-start | bytes 786436
  89.2 1.9 collective-permute-start.2
  91.2 1.8 copy-start.3
  93.0 66.1 %slice-start = ((s8[5767168]{0:T(1024)(128)(4,1)}), s8[4194304]{0:T(1024)(128)(4,1)S(1)}, s32[]{:S(2)}) async-start(s8[5767168]{0:T(1024)(128)(4,1)} %bitcast.83), calls=%async_computation.3 | async-start | bytes 8388608
  94.3 64.8 %slice-start.1 = ((s8[5767168]{0:T(1024)(128)(4,1)}), s8[1572864]{0:T(1024)(128)(4,1)S(1)}, s32[]{:S(2)}) async-start(s8[5767168]{0:T(1024)(128)(4,1)} %bitcast.83), calls=%async_computation.4 | async-start | bytes 3145728
  159.1 6.7 %copy-start.4 = (bf16[1,704,2048]{2,1,0:T(8,128)(2,1)S(1)}, bf16[1,704,2048]{2,1,0:T(8,128)(2,1)}, u32[]{:S(2)}) copy-start(bf16[1,704,2048]{2,1,0:T(8,128)(2,1)} %param.25) | copy-start | bytes 8650756
Sparse Core Ops, SparseCore 0:
  11.0 63.1 all-gather.1

commit v13 on v9

--- a/solution.py
+++ b/solution.py
@@ -215,7 +215,7 @@
     expert_sum = jnp.dot(
         combine_weights,
         returned.astype(jnp.float32),
-        precision=lax.Precision.HIGHEST,
+        precision=lax.Precision.HIGH,
         preferred_element_type=jnp.float32,
     )
     return (residual + expert_sum).astype(jnp.bfloat16)[None]

time: 250 us -> 249 us (level)
  blocking collectives: 117 us -> 122 us
  Pallas kernels: 16.7 us -> 12.1 us
    all_to_all x1, blocking collectives: 60.1 us -> 65 us  [local(): lax.all_to_all(outgoing, ('req', 'blk'), split_axis=0, concat_axis=0, til...]
    pallas_call x1, Pallas kernels: 16.7 us -> 12.1 us  [attention(): pl.pallas_call(attn_kernel, out_shape=jax.ShapeDtypeStruct(queries.shape,...]
  transfers between devices with their start and end apart: 6 -> 6, of which waited for: 4 -> 4; matrix products, arithmetic and copies ran while one was open for 2% -> 2% of each run, Pallas kernels for 7% -> 5%
where the time goes in v13:
time: 249 us; the launch traced here: 250 us
  blocking collectives  122 us (49%)
  waiting for transfers between devices  58.9 us (24%)
  matrix products  29.5 us (12%)
  between operations  14.3 us (6%)
  Pallas kernels  12.1 us (5%)
  local copies, waits for them, and re-layouts  5.99 us (2%)
  other arithmetic  3.53 us (1%)
  starting transfers between devices  3.42 us (1%)
    all_to_all x1, blocking collectives, local(): lax.all_to_all(outgoing, ('req', 'blk'), split_axis=0, concat_axis=0, til...  65 us
    all_to_all x1, blocking collectives, local(): lax.all_to_all(both, ('req', 'blk'), split_axis=0, concat_axis=0, tiled=T...  56.8 us
    all_gather x1, waiting for transfers between devices, local(): lax.all_gather(chip_kv, 'blk', axis=0, tiled=True, axis_index_groups=same...  49.2 us
    dot_general x2, matrix products, half_expert(): hidden = jnp.dot(arrived, gate_up.T, preferred_element_type=jnp.float32)  16.3 us
    pallas_call x1, Pallas kernels, attention(): pl.pallas_call(attn_kernel, out_shape=jax.ShapeDtypeStruct(queries.shape,...  12.1 us
    ppermute x2, waiting for transfers between devices, local(): got_kv, got_q = lax.ppermute((kv_cols(1 - core), sent_q), 'blk', pairs)  8.99 us
    dot_general x2, matrix products, half_expert(): jnp.dot(activated, down_rows, preferred_element_type=jnp.float32)  7.94 us
  transfers between devices with their start and end apart: 6, of which 4 were waited for; matrix products, arithmetic and copies ran while one was open for 2% of the time, Pallas kernels for 5%

profile of v13, /device:TPU:1, one launch (start us, length us, event | category | flops | bytes accessed | tf_op | source)
XLA Modules:
  0.0 249.5 jit_solution(2824175397744195163)
XLA Ops:
  6.5 0.0 all-gather.2.cloned.1.call-start
  6.5 1.0 fusion.27
  7.6 1.5 collective-permute-start.1
  9.1 1.1 collective-permute-done.1
  10.1 0.8 maximum_select_fusion
  10.9 0.0 all-gather.2.cloned.1.call-update
  10.9 0.5 collective-permute-start.3
  11.4 0.1 collective-permute-start.4
  11.5 1.0 dynamic-slice_bitcast_fusion.1
  12.5 0.5 collective-permute-start
  13.0 0.8 copy.26
  13.7 0.1 eq.52
  13.9 0.1 eq.48
  14.0 0.9 reduce-window.6
  14.9 0.2 slice_reduce_fusion
  15.2 0.1 fusion.32
  15.3 0.1 reduce_sum.39
  16.2 0.7 copy.35
  16.9 0.1 copy.30
  16.9 0.1 pad_add_fusion.s_ref
  17.0 7.9 %collective-permute-done = bf16[64,1024]{1,0:T(8,128)(2,1)S(1)} collective-permute-done((bf16[64,1024]{1,0:T(8,128)(2,1)S(1)}, bf16[64,1024]{1,0:T(8,128)(2,1)S(1)}, u32[]{:S(2)}, u32[]{:S(2)}) %collective-permute-start) | collective-permute-done | bytes 131104 | tf_op jit(solution)/shard_map/ppermute | solution.py:161
  25.0 49.2 %all-gather.2.cloned.1.call-done.k_ref.v_ref = bf16[32,192,512]{2,1,0:T(8,128)(2,1)} async-done(((bf16[2,192,512]{2,1,0:T(8,128)(2,1)}), bf16[32,192,512]{2,1,0:T(8,128)(2,1)}) %all-gather.2.cloned.1.call-update) | async-done | bytes 6291472 | tf_op jit(solution)/shard_map/all_gather | solution.py:166
  74.2 0.0 copy-start
  74.2 2.8 %copy-done = bf16[32,192,512]{2,1,0:T(8,128)(2,1)S(1)} copy-done((bf16[32,192,512]{2,1,0:T(8,128)(2,1)S(1)}, bf16[32,192,512]{2,1,0:T(8,128)(2,1)}, u32[]{:S(2)}) %copy-start) | copy-done | bytes 6291480
  77.0 0.0 copy-start.1
  77.0 0.0 copy-start.2
  77.0 12.1 %shard_map.127 = bf16[128,1024]{1,0:T(8,128)(2,1)S(1)} custom-call(s32[3]{0:T(128)S(1)} %pad_add_fusion.s_ref, bf16[128,1024]{1,0:T(8,128)(2,1)S(1)} %maximum_select_fusion.1.q_ref, bf16[32,192,512]{2,1,0:T(8,128)(2,1)S(1)} %copy-done, bf16[32,192,512]{2,1,0:T(8,128)(2,1)S(1)} %copy-done), custom_call_target="tpu_custom_call" | custom-call | tf_op jit(solution)/shard_map/pallas_call | solution.py:93
  89.2 0.9 collective-permute-start.2
  90.1 0.4 convert_reduce_fusion
  90.5 0.6 collective-permute-done.2
  91.1 0.1 maximum_select_fusion.2
  91.2 0.0 copy-start.3
  91.2 0.0 collective-permute-done.4
  91.2 0.0 collective-permute-done.3
  91.2 0.0 copy-done.1
  91.2 0.0 copy-done.2
  91.2 1.7 multiply_reduce_fusion
  92.9 0.0 copy-done.3
  93.0 0.0 slice-start
  93.0 1.3 convert_bitcast_fusion
  94.3 0.0 slice-start.1
  94.3 65.0 %all_to_all.24 = bf16[128,8,2048]{2,1,0:T(8,128)(2,1)S(1)} all-to-all(bf16[128,8,2048]{2,1,0:T(8,128)(2,1)S(1)} %convert_bitcast_fusion), channel_id=1, replica_groups=mesh['req'=4,'blk'=32] {'req','blk'}, dimensions={0} | all-to-all | bytes 8388608 | tf_op jit(solution)/shard_map/all_to_all | solution.py:210
  159.3 0.0 slice-done
  159.3 0.0 slice-done.1
  159.3 0.0 copy-start.4
  159.3 6.7 %fusion.5 = f32[1024,1408]{1,0:T(8,128)S(1)} fusion(bf16[128,8,2048]{2,1,0:T(8,128)(2,1)S(1)} %all_to_all.24, bf16[1,1408,2048]{2,1,0:T(8,128)(2,1)S(1)} %bitcast.81), kind=kOutput, calls=%fused_computation.6 | convolution fusion | flops 5905580032 | bytes 15728640 | tf_op jit(solution)/shard_map/dot_general | solution.py:112
  166.0 0.0 copy-done.4
  166.0 3.9 %fusion.18 = bf16[1024,2048]{1,0:T(8,128)(2,1)S(1)} fusion(f32[1024,1408]{1,0:T(8,128)S(1)} %fusion.5, bf16[1,704,2048]{2,1,0:T(8,128)(2,1)S(1)} %copy-done.4), kind=kOutput, calls=%fused_computation.17 | convolution fusion | flops 2957115392 | bytes 13369344 | tf_op jit(solution)/shard_map/dot_general | solution.py:114
  169.9 9.6 %fusion.3 = f32[1024,1408]{1,0:T(8,128)S(1)} fusion(bf16[1408,2048]{1,0:T(8,128)(2,1)} %collective-permute-done.3, bf16[128,8,2048]{2,1,0:T(8,128)(2,1)S(1)} %all_to_all.24), kind=kOutput, calls=%fused_computation.4 | convolution fusion | flops 5905580032 | bytes 15728640 | tf_op jit(solution)/shard_map/dot_general | solution.py:112
  179.5 4.0 %fusion = bf16[128,8,2048]{2,1,0:T(8,128)(2,1)S(1)} fusion(bf16[1024,2048]{1,0:T(8,128)(2,1)S(1)} %fusion.18, bf16[704,2048]{1,0:T(8,128)(2,1)S(1)} %collective-permute-done.4, f32[1024,1408]{1,0:T(8,128)S(1)} %fusion.3), kind=kOutput, calls=%fused_computation.1 | convolution fusion | flops 2967601152 | bytes 17563648 | tf_op jit(solution)/shard_map/dot_general | solution.py:114
  183.5 56.8 %all_to_all.25 = bf16[128,8,2048]{2,1,0:T(8,128)(2,1)S(1)} all-to-all(bf16[128,8,2048]{2,1,0:T(8,128)(2,1)S(1)} %fusion), channel_id=1, replica_groups=mesh['req'=4,'blk'=32] {'req','blk'}, dimensions={0} | all-to-all | bytes 8388608 | tf_op jit(solution)/shard_map/all_to_all | solution.py:214
  240.4 2.3 fusion.15
  (9 shorter events, 0.2 us)
Async XLA Ops:
  6.5 67.7 %all-gather.2.cloned.1.call-start = ((), (), s32[]{:S(2)}) async-start(), calls=%async_computation.2 | async-start | bytes 6684672 | tf_op jit(solution)/shard_map/all_gather | solution.py:166
  7.6 2.5 %collective-permute-start.1 = (bf16[192,512]{1,0:T(8,128)(2,1)S(1)}, bf16[192,512]{1,0:T(8,128)(2,1)S(1)}, u32[]{:S(2)}, u32[]{:S(2)}) collective-permute-start(bf16[192,512]{1,0:T(8,128)(2,1)S(1)} %pad_maximum_fusion), channel_id=1, source_target_pairs={{0,1},{1,0},{2,3},{3,2},{4,5},{5,4},{6,7},{7,6},{8,9},{9,8},{10,11... | collective-permute-start | bytes 589832 | tf_op jit(solution)/shard_map/ppermute | solution.py:161
  10.9 80.3 %collective-permute-start.3 = (bf16[1408,2048]{1,0:T(8,128)(2,1)}, bf16[1408,2048]{1,0:T(8,128)(2,1)}, u32[]{:S(2)}, u32[]{:S(2)}) collective-permute-start(bf16[1408,2048]{1,0:T(8,128)(2,1)} %bitcast.79), channel_id=1, source_target_pairs={{0,1},{1,0},{2,3},{3,2},{4,5},{5,4},{6,7},{7,6},{8,9},{9,8},{10,11... | collective-permute-start | bytes 17301512 | tf_op jit(solution)/shard_map/ppermute | solution.py:140
  11.4 79.8 %collective-permute-start.4 = (bf16[704,2048]{1,0:T(8,128)(2,1)}, bf16[704,2048]{1,0:T(8,128)(2,1)S(1)}, u32[]{:S(2)}, u32[]{:S(2)}) collective-permute-start(bf16[704,2048]{1,0:T(8,128)(2,1)} %bitcast.82), channel_id=1, source_target_pairs={{0,1},{1,0},{2,3},{3,2},{4,5},{5,4},{6,7},{7,6},{8,9},{9,8},{10,11... | collective-permute-start | bytes 8650760 | tf_op jit(solution)/shard_map/ppermute | solution.py:141
  12.5 12.4 %collective-permute-start = (bf16[64,1024]{1,0:T(8,128)(2,1)S(1)}, bf16[64,1024]{1,0:T(8,128)(2,1)S(1)}, u32[]{:S(2)}, u32[]{:S(2)}) collective-permute-start(bf16[64,1024]{1,0:T(8,128)(2,1)S(1)} %get-tuple-element.16), channel_id=1, source_target_pairs={{0,1},{1,0},{2,3},{3,2},{4,5},{5,4},{6,7},{7,6},{8,9},{9,8},{10,11... | collective-permute-start | bytes 393224 | tf_op jit(solution)/shard_map/ppermute | solution.py:161
  74.2 2.8 %copy-start = (bf16[32,192,512]{2,1,0:T(8,128)(2,1)S(1)}, bf16[32,192,512]{2,1,0:T(8,128)(2,1)}, u32[]{:S(2)}) copy-start(bf16[32,192,512]{2,1,0:T(8,128)(2,1)} %all-gather.2.cloned.1.call-done.k_ref.v_ref) | copy-start | bytes 18874372
  77.0 14.2 %copy-start.1 = (bf16[2048,2048]{1,0:T(8,128)(2,1)S(1)}, bf16[2048,2048]{1,0:T(8,128)(2,1)}, u32[]{:S(2)}) copy-start(bf16[2048,2048]{1,0:T(8,128)(2,1)} %param.20) | copy-start | bytes 25165828
  77.0 14.2 %copy-start.2 = (bf16[1,64,2048]{2,1,0:T(8,128)(2,1)S(1)}, bf16[1,64,2048]{2,1,0:T(8,128)(2,1)}, u32[]{:S(2)}) copy-start(bf16[1,64,2048]{2,1,0:T(8,128)(2,1)} %param.19) | copy-start | bytes 786436
  89.2 1.9 collective-permute-start.2
  91.2 1.8 copy-start.3
  93.0 66.3 %slice-start = ((s8[5767168]{0:T(1024)(128)(4,1)}), s8[4194304]{0:T(1024)(128)(4,1)S(1)}, s32[]{:S(2)}) async-start(s8[5767168]{0:T(1024)(128)(4,1)} %bitcast.80), calls=%async_computation.3 | async-start | bytes 8388608
  94.3 65.0 %slice-start.1 = ((s8[5767168]{0:T(1024)(128)(4,1)}), s8[1572864]{0:T(1024)(128)(4,1)S(1)}, s32[]{:S(2)}) async-start(s8[5767168]{0:T(1024)(128)(4,1)} %bitcast.80), calls=%async_computation.4 | async-start | bytes 3145728
  159.3 6.7 %copy-start.4 = (bf16[1,704,2048]{2,1,0:T(8,128)(2,1)S(1)}, bf16[1,704,2048]{2,1,0:T(8,128)(2,1)}, u32[]{:S(2)}) copy-start(bf16[1,704,2048]{2,1,0:T(8,128)(2,1)} %param.25) | copy-start | bytes 8650756
Sparse Core Ops, SparseCore 0:
  11.0 63.1 all-gather.1
